TPU v7x, 1024 devices: a whole 4x4x32 slice. The times are simulated.
1024 devices in a mesh: lat: 16 (over z_hi, x), lon: 64 (over y, z_lo, core).
Axes of the slice: x: 4, y: 4, z: 32 (z_hi: 4, z_lo: 8; z = z_hi * 8 + z_lo), core: 2. Of those that a mesh axis runs over, the one named last changes fastest.
Arguments:
- queries: bfloat16 [256, 512, 512], P('lat', 'lon'), may hold values from -48 to 48
- key_vectors: bfloat16 [256, 512, 512], P('lat', 'lon'), may hold values from -4 to 4
- value_vectors: bfloat16 [256, 512, 512], P('lat', 'lon'), may hold values from -6 to 6
- out_cotangent: bfloat16 [256, 512, 512], P('lat', 'lon'), may hold values from -6 to 6
- lat_start: int32 [256], P('lat'), may hold values from 0 to 243, as said below
- lon_start: int32 [512], P('lon'), may hold values from 0 to 511, as said below
- window_bias: float32 [8, 13, 13], replicated, may hold values from -4 to 4
Outputs:
- attention_out: bfloat16 [256, 512, 512], P('lat', 'lon')
- grad_queries: bfloat16 [256, 512, 512], P('lat', 'lon')
- grad_keys: bfloat16 [256, 512, 512], P('lat', 'lon')
- grad_values: bfloat16 [256, 512, 512], P('lat', 'lon')
- grad_window_bias: float32 [8, 13, 13], replicated
Inputs may be any that keep to these rules, and one draw needn't show every extreme that they name: lat_start[i] differs from min(max(i - 6, 0), 243) by at most 2, and by exactly 2 and exactly -2 at some rows. lon_start[j] equals (j - 6 + e) mod 512 with e from -2 to 2; e = 2 and e = -2 both occur.
All inputs are finite; a program needn't handle non-finite values.
Results may differ from a plain program's by a relative error of at most 0.017.
Values may be sent and summed in bfloat16 or wider, within the bound.
No kernel may reach another device: no remote copies, remote signals or barrier semaphores. Data moves between devices by JAX's collectives and lax.ppermute only.
A program may use at most 64 MiB of HBM per device.

v0:
```python
import jax
import jax.numpy as jnp
from jax import lax
from jax.sharding import PartitionSpec as P


def padded_2(value, sides, width, wrap):
    for axis, dim in sides:
        size, length = (lax.axis_size(axis), value.shape[dim])
        up = [(i, (i + 1) % size) for i in range(size if wrap else size - 1)]
        down = [(j, i) for i, j in up]
        last = lax.slice_in_dim(value, length - width, length, axis=dim)
        leading = lax.slice_in_dim(value, 0, width, axis=dim)
        before = lax.ppermute(last, axis, up)
        after = lax.ppermute(leading, axis, down)
        value = jnp.concatenate([before, value, after], axis=dim)
    return value


def place_tables(row_hot, col_hot):
    row_merged = jnp.repeat(row_hot.transpose(1, 2, 0), 24, axis=-1)
    col_merged = jnp.tile(col_hot.transpose(1, 2, 0), (1, 1, 24))
    return (row_merged, col_merged)


def place_bias(window_bias, row_merged, col_hot):
    col_part = jnp.einsum("hpc,ljc->hpjl", window_bias, col_hot)
    col_spread = jnp.tile(col_part, (1, 1, 1, 24))
    bias = jnp.sum(row_merged[None, :, :, None, :] * col_spread[:, None, :, :, :], axis=2)
    return bias.reshape(window_bias.shape[0], 64, 576)


def place_table(dscore, row_merged, col_merged):
    head_count = dscore.shape[0]
    shaped = dscore.reshape(head_count, 8, 8, 576)
    by_row = jnp.sum(shaped[:, :, None, :, :] * row_merged[None, :, :, None, :], axis=1)
    return jnp.einsum("hpjk,jck->hpc", by_row, col_merged)


def inside_mask(row_merged, col_merged):
    row_in = jnp.sum(row_merged, axis=1)
    col_in = jnp.sum(col_merged, axis=1)
    return (row_in[:, None, :] * col_in[None, :, :]).reshape(64, 576) > 0.5


def tile_pass(query_tile, region, grad_tile, rel_rows, rel_cols, window_bias):
    head_count, window, _ = window_bias.shape
    model_width = query_tile.shape[-1]
    head_dim = model_width // head_count
    score_scale = head_dim ** (-0.5)
    query_heads = query_tile.reshape(64, head_count, head_dim)
    key_heads = region[..., :model_width].reshape(576, head_count, head_dim)
    value_heads = region[..., model_width:].reshape(576, head_count, head_dim)
    grad_heads = grad_tile.reshape(64, head_count, head_dim)
    offsets = jnp.arange(24, dtype=jnp.int32)
    places = jnp.arange(window, dtype=jnp.int32)
    row_hot = (offsets[:, None, None] - rel_rows[None, :, None] == places[None, None, :]).astype(
        jnp.float32
    )
    col_hot = (offsets[:, None, None] - rel_cols[None, :, None] == places[None, None, :]).astype(
        jnp.float32
    )
    row_merged, col_merged = place_tables(row_hot, col_hot)
    bias_tile = place_bias(window_bias, row_merged, col_hot)
    inside = inside_mask(row_merged, col_merged)
    scores = (
        jnp.einsum("qhd,khd->hqk", query_heads, key_heads, preferred_element_type=jnp.float32)
        * score_scale
        + bias_tile
    )
    scores = jnp.where(inside[None], scores, -jnp.inf)
    row_peak = jnp.max(scores, axis=-1, keepdims=True)
    weights_raw = jnp.exp(scores - row_peak)
    row_total = jnp.sum(weights_raw, axis=-1, keepdims=True)
    attention = weights_raw / row_total
    rounded_probs = attention.astype(jnp.bfloat16)
    output = jnp.einsum(
        "hqk,khd->qhd", rounded_probs, value_heads, preferred_element_type=jnp.float32
    )
    output = output.astype(jnp.bfloat16).reshape(8, 8, model_width)
    dprobs = jnp.einsum("qhd,khd->hqk", grad_heads, value_heads, preferred_element_type=jnp.float32)
    correction = jnp.sum(attention * dprobs, axis=-1, keepdims=True)
    dscore = attention * (dprobs - correction)
    dscore_round = dscore.astype(jnp.bfloat16)
    grad_query_tile = (
        jnp.einsum("hqk,khd->qhd", dscore_round, key_heads, preferred_element_type=jnp.float32)
        * score_scale
    )
    grad_query_tile = grad_query_tile.astype(jnp.bfloat16).reshape(8, 8, model_width)
    grad_table = place_table(dscore, row_merged, col_merged)
    log_total = (row_peak + jnp.log(row_total))[..., 0]
    statistics = jnp.concatenate((log_total.T, correction[..., 0].T), axis=-1).reshape(
        8, 8, 2 * head_count
    )
    grad_keys = (
        jnp.einsum("hqk,qhd->khd", dscore_round, query_heads, preferred_element_type=jnp.float32)
        * score_scale
    )
    grad_vals = jnp.einsum(
        "hqk,qhd->khd", rounded_probs, grad_heads, preferred_element_type=jnp.float32
    )
    grad_pairs = jnp.concatenate(
        (grad_keys.reshape(24, 24, model_width), grad_vals.reshape(24, 24, model_width)), axis=-1
    )
    return (output, grad_query_tile, grad_pairs, grad_table, statistics)


def rims_of(array, along):
    if along == 0:
        return jnp.concatenate((array[:8], array[-8:]), axis=0)
    return jnp.concatenate((array[:, :8], array[:, -8:]), axis=1)


def settle(array, arrived, along):
    if along == 0:
        inner = array[8:-8]
        inner = inner.at[:8].add(arrived[:8])
        return inner.at[-8:].add(arrived[-8:])
    inner = array[:, 8:-8]
    inner = inner.at[:, :8].add(arrived[:, :8])
    return inner.at[:, -8:].add(arrived[:, -8:])


def per_device(
    queries, key_vectors, value_vectors, out_cotangent, lat_start, lon_start, window_bias
):
    height, breadth, model_width = queries.shape
    lon_total = breadth * lax.axis_size("lon")
    first_row = lax.axis_index("lat") * height
    first_col = lax.axis_index("lon") * breadth
    stacked = jnp.concatenate((key_vectors, value_vectors), axis=-1)
    widened = padded_2(stacked, (("lon", 1),), 8, True)
    padded = padded_2(widened, (("lat", 0),), 8, False)
    across = breadth // 8
    tile_total = height // 8 * across

    def tile_inputs(tile_index):
        tile_row = tile_index // across * 8
        tile_col = tile_index % across * 8
        region = lax.dynamic_slice(padded, (tile_row, tile_col, 0), (24, 24, 2 * model_width))
        query_tile = lax.dynamic_slice(queries, (tile_row, tile_col, 0), (8, 8, model_width))
        grad_tile = lax.dynamic_slice(out_cotangent, (tile_row, tile_col, 0), (8, 8, model_width))
        rel_rows = lax.dynamic_slice_in_dim(lat_start, tile_row, 8, 0) - (first_row + tile_row - 8)
        rel_cols = (lon_start - (first_col + tile_col - 8)) % lon_total
        return (tile_row, tile_col, query_tile, region, grad_tile, rel_rows, rel_cols)

    def visit(tile_index, state):
        accum, output, grad_query, grad_table = state
        tile_row, tile_col, query_tile, region, grad_tile, rel_rows, rel_cols = tile_inputs(
            tile_index
        )
        tile_out, tile_grad, tile_pairs, tile_table, unused = tile_pass(
            query_tile, region, grad_tile, rel_rows, rel_cols, window_bias
        )
        current = lax.dynamic_slice(accum, (tile_row, tile_col, 0), (24, 24, 2 * model_width))
        accum = lax.dynamic_update_slice(accum, current + tile_pairs, (tile_row, tile_col, 0))
        output = lax.dynamic_update_slice(output, tile_out, (tile_row, tile_col, 0))
        grad_query = lax.dynamic_update_slice(grad_query, tile_grad, (tile_row, tile_col, 0))
        return (accum, output, grad_query, grad_table + tile_table)

    start_state = (
        jnp.zeros((height + 16, breadth + 16, 2 * model_width), jnp.float32),
        jnp.zeros(queries.shape, jnp.bfloat16),
        jnp.zeros(queries.shape, jnp.bfloat16),
        jnp.zeros(window_bias.shape, jnp.float32),
    )
    accum, attention_out, grad_queries, grad_table = lax.fori_loop(
        0, tile_total, visit, start_state
    )
    arrived = padded_2(rims_of(accum, 0).astype(jnp.bfloat16), (("lat", 0),), 8, False).astype(
        jnp.float32
    )
    folded = settle(accum, arrived, 0)
    arrived_cols = padded_2(rims_of(folded, 1).astype(jnp.bfloat16), (("lon", 1),), 8, True).astype(
        jnp.float32
    )
    totals = settle(folded, arrived_cols, 1)
    grad_keys = totals[..., :model_width].astype(jnp.bfloat16)
    grad_values = totals[..., model_width:].astype(jnp.bfloat16)
    grad_window_bias = lax.psum(grad_table, ("lat", "lon"))
    return (attention_out, grad_queries, grad_keys, grad_values, grad_window_bias)


def solution(mesh):
    return jax.shard_map(
        per_device,
        mesh=mesh,
        in_specs=(
            P("lat", "lon", None),
            P("lat", "lon", None),
            P("lat", "lon", None),
            P("lat", "lon", None),
            P("lat"),
            P("lon"),
            P(),
        ),
        out_specs=(
            P("lat", "lon", None),
            P("lat", "lon", None),
            P("lat", "lon", None),
            P("lat", "lon", None),
            P(),
        ),
        check_vma=False,
    )
```

profile of v0, /device:TPU:6, one launch (start us, length us, event | category | flops | bytes accessed | tf_op | source)
XLA Modules:
  0.0 476.1 jit_solution(2848843248962723353)
XLA Ops:
  4.5 15.0 %collective-permute-start.1 = (bf16[16,8,1024]{2,1,0:T(8,128)(2,1)S(1)}, bf16[16,8,1024]{2,1,0:T(8,128)(2,1)S(1)}, u32[]{:S(2)}, u32[]{:S(2)}) collective-permute-start(bf16[16,8,1024]{2,1,0:T(8,128)(2,1)S(1)} %constant_dynamic-update-slice_fusion.2), channel_id=1, source_target_pairs={{1,0},{2,1},{3,2},{4,3},{5,4},{6,5},{7,6},{8,7},{9,8},{10,9},{11,1... | collective-permute-start | bytes 786440 | tf_op jit(solution)/shard_map/ppermute | solution.py:15
  23.6 15.6 %collective-permute-start.2 = (bf16[8,24,1024]{2,1,0:T(8,128)(2,1)S(1)}, bf16[8,24,1024]{2,1,0:T(8,128)(2,1)S(1)}, u32[]{:S(2)}, u32[]{:S(2)}) collective-permute-start(bf16[8,24,1024]{2,1,0:T(8,128)(2,1)S(1)} %get-tuple-element.642), channel_id=1, source_target_pairs={{0,64},{64,128},{128,192},{192,256},{256,320},{320,384},{384,448},... | collective-permute-start | bytes 1179656 | tf_op jit(solution)/shard_map/ppermute | solution.py:14
  41.8 2.7 collective-permute-done.2
  44.5 67.9 %collective-permute-done.3 = bf16[8,24,1024]{2,1,0:T(8,128)(2,1)S(1)} collective-permute-done((bf16[8,24,1024]{2,1,0:T(8,128)(2,1)S(1)}, bf16[8,24,1024]{2,1,0:T(8,128)(2,1)S(1)}, u32[]{:S(2)}, u32[]{:S(2)}) %collective-permute-start.3) | collective-permute-done | bytes 393248 | tf_op jit(solution)/shard_map/ppermute | solution.py:15
  117.2 117.5 %while.31 = (s32[]{:T(128)}, f32[32,24,1024]{2,1,0:T(8,128)}, bf16[16,8,512]{2,1,0:T(8,128)(2,1)}, bf16[16,8,512]{2,1,0:T(8,128)(2,1)}, f32[8,13,13]{2,1,0:T(8,1...) while((s32[]{:T(128)}, f32[32,24,1024]{2,1,0:T(8,128)}, ...), condition=%wide.region_8.9_spmd.clone, body=%wide.region_0.8_spmd.clone.sunk | while | flops 261020608 | bytes 77249072 | solution.py:167
  120.2 4.6 tile.54
  124.8 6.6 %tile.55 = f32[8,13,8,576]{3,2,1,0:T(8,128)S(1)} reshape(f32[8,13,8,24,24]{4,3,2,1,0:T(8,128)} %tile.54) | data formatting | bytes 3833856 | tf_op jit(solution)/shard_map/while/body/eval_jaxpr/tile | solution.py:28
  141.5 2.7 reshape.429
  144.2 2.7 copy.91
  152.1 2.6 fusion.110
  160.6 3.9 convolution_bitcast_fusion.5
  168.4 4.1 fusion.112
  178.9 4.6 tile.54
  183.5 6.6 %tile.55 = f32[8,13,8,576]{3,2,1,0:T(8,128)S(1)} reshape(f32[8,13,8,24,24]{4,3,2,1,0:T(8,128)} %tile.54) | data formatting | bytes 3833856 | tf_op jit(solution)/shard_map/while/body/eval_jaxpr/tile | solution.py:28
  200.2 2.7 reshape.429
  202.9 2.7 copy.91
  210.8 2.6 fusion.110
  219.3 3.9 convolution_bitcast_fusion.5
  227.1 4.2 fusion.112
  238.9 3.9 collective-permute-start.5
  243.0 6.5 %collective-permute-done.4 = bf16[8,24,1024]{2,1,0:T(8,128)(2,1)S(1)} collective-permute-done((bf16[8,24,1024]{2,1,0:T(8,128)(2,1)S(1)}, bf16[8,24,1024]{2,1,0:T(8,128)(2,1)S(1)}, u32[]{:S(2)}, u32[]{:S(2)}) %collective-permute-start.4) | collective-permute-done | bytes 393248 | tf_op jit(solution)/shard_map/ppermute | solution.py:14
  249.5 39.2 %collective-permute-done.5 = bf16[8,24,1024]{2,1,0:T(8,128)(2,1)S(1)} collective-permute-done((bf16[8,24,1024]{2,1,0:T(8,128)(2,1)S(1)}, bf16[8,24,1024]{2,1,0:T(8,128)(2,1)S(1)}, u32[]{:S(2)}, u32[]{:S(2)}) %collective-permute-start.5) | collective-permute-done | bytes 393248 | tf_op jit(solution)/shard_map/ppermute | solution.py:15
  291.1 23.8 %collective-permute-start.7 = (bf16[16,8,1024]{2,1,0:T(8,128)(2,1)S(1)}, bf16[16,8,1024]{2,1,0:T(8,128)(2,1)S(1)}, u32[]{:S(2)}, u32[]{:S(2)}) collective-permute-start(bf16[16,8,1024]{2,1,0:T(8,128)(2,1)S(1)} %get-tuple-element.641), channel_id=1, source_target_pairs={{1,0},{2,1},{3,2},{4,3},{5,4},{6,5},{7,6},{8,7},{9,8},{10,9},{11,1... | collective-permute-start | bytes 786440 | tf_op jit(solution)/shard_map/ppermute | solution.py:15
  315.0 160.3 %psum.7 = f32[8,13,13]{2,0,1:T(8,128)} all-reduce(f32[8,13,13]{2,0,1:T(8,128)S(1)} %copy.58), channel_id=1, replica_groups=mesh['lat'=16,'lon'=64] {'lat','lon'}, use_global_device_ids=true, to_apply=%region_9.10 | all-reduce | flops 1352 | bytes 10816 | tf_op jit(solution)/shard_map/psum | solution.py:180
  (178 shorter events, 85.1 us)
Async XLA Ops:
  2.5 38.7 %copy-start.13 = (f32[8,13,13]{2,0,1:T(8,128)S(1)}, f32[8,13,13]{2,0,1:T(8,128)}, u32[]{:S(2)}) copy-start(f32[8,13,13]{2,0,1:T(8,128)} %param.27) | copy-start | bytes 16228
  2.5 19.4 %collective-permute-start = (bf16[16,8,1024]{2,1,0:T(8,128)(2,1)S(1)}, bf16[16,8,1024]{2,1,0:T(8,128)(2,1)S(1)}, u32[]{:S(2)}, u32[]{:S(2)}) collective-permute-start(bf16[16,8,1024]{2,1,0:T(8,128)(2,1)S(1)} %constant_dynamic-update-slice_fusion.2), channel_id=1, source_target_pairs={{0,1},{1,2},{2,3},{3,4},{4,5},{5,6},{6,7},{7,8},{8,9},{9,10},{10,1... | collective-permute-start | bytes 786440 | tf_op jit(solution)/shard_map/ppermute | solution.py:14
  4.5 18.9 %collective-permute-start.1 = (bf16[16,8,1024]{2,1,0:T(8,128)(2,1)S(1)}, bf16[16,8,1024]{2,1,0:T(8,128)(2,1)S(1)}, u32[]{:S(2)}, u32[]{:S(2)}) collective-permute-start(bf16[16,8,1024]{2,1,0:T(8,128)(2,1)S(1)} %constant_dynamic-update-slice_fusion.2), channel_id=1, source_target_pairs={{1,0},{2,1},{3,2},{4,3},{5,4},{6,5},{7,6},{8,7},{9,8},{10,9},{11,1... | collective-permute-start | bytes 786440 | tf_op jit(solution)/shard_map/ppermute | solution.py:15
  23.6 21.0 %collective-permute-start.2 = (bf16[8,24,1024]{2,1,0:T(8,128)(2,1)S(1)}, bf16[8,24,1024]{2,1,0:T(8,128)(2,1)S(1)}, u32[]{:S(2)}, u32[]{:S(2)}) collective-permute-start(bf16[8,24,1024]{2,1,0:T(8,128)(2,1)S(1)} %get-tuple-element.642), channel_id=1, source_target_pairs={{0,64},{64,128},{128,192},{192,256},{256,320},{320,384},{384,448},... | collective-permute-start | bytes 1179656 | tf_op jit(solution)/shard_map/ppermute | solution.py:14
  39.2 73.2 %collective-permute-start.3 = (bf16[8,24,1024]{2,1,0:T(8,128)(2,1)S(1)}, bf16[8,24,1024]{2,1,0:T(8,128)(2,1)S(1)}, u32[]{:S(2)}, u32[]{:S(2)}) collective-permute-start(bf16[8,24,1024]{2,1,0:T(8,128)(2,1)S(1)} %get-tuple-element.643), channel_id=1, source_target_pairs={{64,0},{128,64},{192,128},{256,192},{320,256},{384,320},{448,384},... | collective-permute-start | bytes 1179656 | tf_op jit(solution)/shard_map/ppermute | solution.py:15
  113.7 3.5 copy-start.14
  113.7 3.5 copy-start.15
  139.9 7.0 %copy-start.1 = (f32[8,64,576]{2,1,0:T(8,128)}, f32[8,64,576]{2,1,0:T(8,128)S(1)}, u32[]{:S(2)}) copy-start(f32[8,64,576]{2,1,0:T(8,128)S(1)} %fusion.108) | copy-start | bytes 3538948 | tf_op jit(solution)/shard_map/while
  141.5 9.0 %copy-start.3 = (f32[8,64,576]{2,1,0:T(8,128)}, f32[8,64,576]{2,1,0:T(8,128)S(1)}, u32[]{:S(2)}) copy-start(f32[8,64,576]{2,1,0:T(8,128)S(1)} %get-tuple-element.737) | copy-start | bytes 3538948 | tf_op jit(solution)/shard_map/while
  150.5 1.6 copy-start.5
  155.8 2.0 copy-start.7
  168.4 4.1 copy-start.2
  168.4 4.1 copy-start.4
  198.6 7.0 %copy-start.1 = (f32[8,64,576]{2,1,0:T(8,128)}, f32[8,64,576]{2,1,0:T(8,128)S(1)}, u32[]{:S(2)}) copy-start(f32[8,64,576]{2,1,0:T(8,128)S(1)} %fusion.108) | copy-start | bytes 3538948 | tf_op jit(solution)/shard_map/while
  200.2 9.0 %copy-start.3 = (f32[8,64,576]{2,1,0:T(8,128)}, f32[8,64,576]{2,1,0:T(8,128)S(1)}, u32[]{:S(2)}) copy-start(f32[8,64,576]{2,1,0:T(8,128)S(1)} %get-tuple-element.737) | copy-start | bytes 3538948 | tf_op jit(solution)/shard_map/while
  214.4 2.0 copy-start.7
  227.1 4.2 copy-start.2
  227.1 4.2 copy-start.4
  234.7 8.2 %copy-start = (f32[32,24,1024]{2,1,0:T(8,128)S(1)}, f32[32,24,1024]{2,1,0:T(8,128)}, u32[]{:S(2)}) copy-start(f32[32,24,1024]{2,1,0:T(8,128)} %get-tuple-element.514) | copy-start | bytes 9437188
  237.0 12.4 %collective-permute-start.4 = (bf16[8,24,1024]{2,1,0:T(8,128)(2,1)S(1)}, bf16[8,24,1024]{2,1,0:T(8,128)(2,1)S(1)}, u32[]{:S(2)}, u32[]{:S(2)}) collective-permute-start(bf16[8,24,1024]{2,1,0:T(8,128)(2,1)S(1)} %get-tuple-element.638), channel_id=1, source_target_pairs={{0,64},{64,128},{128,192},{192,256},{256,320},{320,384},{384,448},... | collective-permute-start | bytes 1179656 | tf_op jit(solution)/shard_map/ppermute | solution.py:14
  238.9 49.7 %collective-permute-start.5 = (bf16[8,24,1024]{2,1,0:T(8,128)(2,1)S(1)}, bf16[8,24,1024]{2,1,0:T(8,128)(2,1)S(1)}, u32[]{:S(2)}, u32[]{:S(2)}) collective-permute-start(bf16[8,24,1024]{2,1,0:T(8,128)(2,1)S(1)} %get-tuple-element.639), channel_id=1, source_target_pairs={{64,0},{128,64},{192,128},{256,192},{320,256},{384,320},{448,384},... | collective-permute-start | bytes 1179656 | tf_op jit(solution)/shard_map/ppermute | solution.py:15
  289.0 26.0 %copy-start.12 = (f32[8,13,13]{2,1,0:T(8,128)S(1)}, f32[8,13,13]{2,1,0:T(8,128)}, u32[]{:S(2)}) copy-start(f32[8,13,13]{2,1,0:T(8,128)} %get-tuple-element.515) | copy-start | bytes 16228
  289.2 186.1 %collective-permute-start.6 = (bf16[16,8,1024]{2,1,0:T(8,128)(2,1)S(1)}, bf16[16,8,1024]{2,1,0:T(8,128)(2,1)S(1)}, u32[]{:S(2)}, u32[]{:S(2)}) collective-permute-start(bf16[16,8,1024]{2,1,0:T(8,128)(2,1)S(1)} %get-tuple-element.640), channel_id=1, source_target_pairs={{0,1},{1,2},{2,3},{3,4},{4,5},{5,6},{6,7},{7,8},{8,9},{9,10},{10,1... | collective-permute-start | bytes 786440 | tf_op jit(solution)/shard_map/ppermute | solution.py:14
  291.1 184.2 %collective-permute-start.7 = (bf16[16,8,1024]{2,1,0:T(8,128)(2,1)S(1)}, bf16[16,8,1024]{2,1,0:T(8,128)(2,1)S(1)}, u32[]{:S(2)}, u32[]{:S(2)}) collective-permute-start(bf16[16,8,1024]{2,1,0:T(8,128)(2,1)S(1)} %get-tuple-element.641), channel_id=1, source_target_pairs={{1,0},{2,1},{3,2},{4,3},{5,4},{6,5},{7,6},{8,7},{9,8},{10,9},{11,1... | collective-permute-start | bytes 786440 | tf_op jit(solution)/shard_map/ppermute | solution.py:15
  (11 other events, 9.6 us)
where the time goes:
time: 479 us; the launch traced here: 476 us
  blocking collectives  160 us (33%)
  waiting for transfers between devices  120 us (25%)
  local copies, waits for them, and re-layouts  76 us (16%)
  starting transfers between devices  66.3 us (14%)
  other arithmetic  29.4 us (6%)
  matrix products  22.5 us (5%)
    psum x1, blocking collectives, per_device(): grad_window_bias = lax.psum(grad_table, ('lat', 'lon'))  160 us
    ppermute x4, waiting for transfers between devices, padded_2(): after = lax.ppermute(leading, axis, down)  109 us
    ppermute x4, starting transfers between devices, padded_2(): after = lax.ppermute(leading, axis, down)  44.7 us
    another operation x4, local copies, waits for them, and re-layouts, place_bias(): col_spread = jnp.tile(col_part, (1, 1, 1, 24))  22.2 us
    ppermute x4, starting transfers between devices, padded_2(): before = lax.ppermute(last, axis, up)  21.5 us
    ppermute x4, waiting for transfers between devices, padded_2(): before = lax.ppermute(last, axis, up)  11.5 us
    reshape x4, local copies, waits for them, and re-layouts, tile_pass(): value_heads = region[..., model_width:].reshape(576, head_count, head_dim)  10.8 us
  transfers between devices with their start and end apart: 8, of which 6 were waited for; matrix products, arithmetic and copies ran while one was open for 0% of the time, Pallas kernels for 0%

commit v1 on v0

--- a/solution.py
+++ b/solution.py
@@ -119,6 +119,19 @@
     inner = array[:, 8:-8]
     inner = inner.at[:, :8].add(arrived[:, :8])
     return inner.at[:, -8:].add(arrived[:, -8:])
+
+
+def exchange_sum(value, axis, flip):
+    size = lax.axis_size(axis)
+    pairs = [(i, i ^ flip) for i in range(size)]
+    return value + lax.ppermute(value, axis, pairs)
+
+
+def all_sum(value):
+    for axis, flips in (("lon", (1, 2, 4, 8, 16, 48)), ("lat", (1, 3, 4, 12))):
+        for flip in flips:
+            value = exchange_sum(value, axis, flip)
+    return value
 
 
 def per_device(
@@ -177,7 +190,7 @@
     totals = settle(folded, arrived_cols, 1)
     grad_keys = totals[..., :model_width].astype(jnp.bfloat16)
     grad_values = totals[..., model_width:].astype(jnp.bfloat16)
-    grad_window_bias = lax.psum(grad_table, ("lat", "lon"))
+    grad_window_bias = all_sum(grad_table)
     return (attention_out, grad_queries, grad_keys, grad_values, grad_window_bias)
 
 

time: 479 us -> 406 us (0.85)
  blocking collectives: 160 us -> 0 us
  waiting for transfers between devices: 120 us -> 171 us
  starting transfers between devices: 66.3 us -> 103 us
    psum x1 -> x0, blocking collectives: 160 us -> none  [per_device(): grad_window_bias = lax.psum(grad_table, ('lat', 'lon'))]
    ppermute x0 -> x10, waiting for transfers between devices: none -> 52.5 us  [exchange_sum(): return value + lax.ppermute(value, axis, pairs)]
    ppermute x0 -> x10, starting transfers between devices: none -> 36.5 us  [exchange_sum(): return value + lax.ppermute(value, axis, pairs)]
  transfers between devices with their start and end apart: 8 -> 18, of which waited for: 6 -> 15; matrix products, arithmetic and copies ran while one was open for 0% -> 0% of each run, Pallas kernels for 0% -> 0%
where the time goes in v1:
time: 406 us; the launch traced here: 404 us
  waiting for transfers between devices  171 us (42%)
  starting transfers between devices  103 us (25%)
  local copies, waits for them, and re-layouts  76.2 us (19%)
  other arithmetic  30.2 us (7%)
  matrix products  22.4 us (6%)
    ppermute x4, waiting for transfers between devices, padded_2(): after = lax.ppermute(leading, axis, down)  109 us
    ppermute x10, waiting for transfers between devices, exchange_sum(): return value + lax.ppermute(value, axis, pairs)  52.5 us
    ppermute x4, starting transfers between devices, padded_2(): after = lax.ppermute(leading, axis, down)  44.9 us
    ppermute x10, starting transfers between devices, exchange_sum(): return value + lax.ppermute(value, axis, pairs)  36.5 us
    another operation x4, local copies, waits for them, and re-layouts, place_bias(): col_spread = jnp.tile(col_part, (1, 1, 1, 24))  22.3 us
    ppermute x4, starting transfers between devices, padded_2(): before = lax.ppermute(last, axis, up)  21.5 us
    reshape x4, local copies, waits for them, and re-layouts, tile_pass(): value_heads = region[..., model_width:].reshape(576, head_count, head_dim)  10.8 us
    ppermute x4, waiting for transfers between devices, padded_2(): before = lax.ppermute(last, axis, up)  9.38 us
  transfers between devices with their start and end apart: 18, of which 15 were waited for; matrix products, arithmetic and copies ran while one was open for 0% of the time, Pallas kernels for 0%

profile of v1, /device:TPU:6, one launch (start us, length us, event | category | flops | bytes accessed | tf_op | source)
XLA Modules:
  0.0 403.9 jit_solution(10077050603496700488)
XLA Ops:
  4.5 15.0 %collective-permute-start.1 = (bf16[16,8,1024]{2,1,0:T(8,128)(2,1)S(1)}, bf16[16,8,1024]{2,1,0:T(8,128)(2,1)S(1)}, u32[]{:S(2)}, u32[]{:S(2)}) collective-permute-start(bf16[16,8,1024]{2,1,0:T(8,128)(2,1)S(1)} %constant_dynamic-update-slice_fusion.2), channel_id=1, source_target_pairs={{1,0},{2,1},{3,2},{4,3},{5,4},{6,5},{7,6},{8,7},{9,8},{10,9},{11,1... | collective-permute-start | bytes 786440 | tf_op jit(solution)/shard_map/ppermute | solution.py:15
  23.6 15.6 %collective-permute-start.2 = (bf16[8,24,1024]{2,1,0:T(8,128)(2,1)S(1)}, bf16[8,24,1024]{2,1,0:T(8,128)(2,1)S(1)}, u32[]{:S(2)}, u32[]{:S(2)}) collective-permute-start(bf16[8,24,1024]{2,1,0:T(8,128)(2,1)S(1)} %get-tuple-element.642), channel_id=1, source_target_pairs={{0,64},{64,128},{128,192},{192,256},{256,320},{320,384},{384,448},... | collective-permute-start | bytes 1179656 | tf_op jit(solution)/shard_map/ppermute | solution.py:14
  44.5 67.9 %collective-permute-done.3 = bf16[8,24,1024]{2,1,0:T(8,128)(2,1)S(1)} collective-permute-done((bf16[8,24,1024]{2,1,0:T(8,128)(2,1)S(1)}, bf16[8,24,1024]{2,1,0:T(8,128)(2,1)S(1)}, u32[]{:S(2)}, u32[]{:S(2)}) %collective-permute-start.3) | collective-permute-done | bytes 393248 | tf_op jit(solution)/shard_map/ppermute | solution.py:15
  117.2 117.6 %while.31 = (s32[]{:T(128)}, f32[32,24,1024]{2,1,0:T(8,128)}, bf16[16,8,512]{2,1,0:T(8,128)(2,1)}, bf16[16,8,512]{2,1,0:T(8,128)(2,1)}, f32[8,13,13]{2,1,0:T(8,1...) while((s32[]{:T(128)}, f32[32,24,1024]{2,1,0:T(8,128)}, ...), condition=%wide.region_8.9_spmd.clone, body=%wide.region_0.8_spmd.clone.sunk | while | flops 261020608 | bytes 77249072 | solution.py:180
  120.3 4.6 %tile.54 = f32[8,13,8,24,24]{4,3,2,1,0:T(8,128)} broadcast(f32[8,13,8,24]{3,2,1,0:T(8,128)S(1)} %copy.92), dimensions={0,1,2,4} | broadcast | bytes 1996800 | tf_op jit(solution)/shard_map/while/body/eval_jaxpr/tile | solution.py:28
  124.8 6.6 %tile.55 = f32[8,13,8,576]{3,2,1,0:T(8,128)S(1)} reshape(f32[8,13,8,24,24]{4,3,2,1,0:T(8,128)} %tile.54) | data formatting | bytes 3833856 | tf_op jit(solution)/shard_map/while/body/eval_jaxpr/tile | solution.py:28
  160.7 3.9 convolution_bitcast_fusion.5
  168.5 4.1 %fusion.112 = f32[32,24,1024]{2,1,0:T(8,128)} fusion(f32[32,24,1024]{2,1,0:T(8,128)} %get-tuple-element.766, s32[]{:T(128)S(6)} %select_n.120, f32[24,24,512]{2,1,0:T(8,128)} %reshape.428, f32[24,24,512]{2,1,0:T(8,128)S(1)} %reshape.430), kind=kLoop, calls=%fused_computation.6.clone.1 | loop fusion | flops 1179648 | bytes 7077892 | tf_op jit(solution)/shard_map/while/body/eval_jaxpr/dynamic_update_slice | solution.py:169
  179.0 4.6 %tile.54 = f32[8,13,8,24,24]{4,3,2,1,0:T(8,128)} broadcast(f32[8,13,8,24]{3,2,1,0:T(8,128)S(1)} %copy.92), dimensions={0,1,2,4} | broadcast | bytes 1996800 | tf_op jit(solution)/shard_map/while/body/eval_jaxpr/tile | solution.py:28
  183.6 6.6 %tile.55 = f32[8,13,8,576]{3,2,1,0:T(8,128)S(1)} reshape(f32[8,13,8,24,24]{4,3,2,1,0:T(8,128)} %tile.54) | data formatting | bytes 3833856 | tf_op jit(solution)/shard_map/while/body/eval_jaxpr/tile | solution.py:28
  227.3 4.2 %fusion.112 = f32[32,24,1024]{2,1,0:T(8,128)} fusion(f32[32,24,1024]{2,1,0:T(8,128)} %get-tuple-element.766, s32[]{:T(128)S(6)} %select_n.120, f32[24,24,512]{2,1,0:T(8,128)} %reshape.428, f32[24,24,512]{2,1,0:T(8,128)S(1)} %reshape.430), kind=kLoop, calls=%fused_computation.6.clone.1 | loop fusion | flops 1179648 | bytes 7077892 | tf_op jit(solution)/shard_map/while/body/eval_jaxpr/dynamic_update_slice | solution.py:169
  239.1 4.1 %collective-permute-start.5 = (bf16[8,24,1024]{2,1,0:T(8,128)(2,1)S(1)}, bf16[8,24,1024]{2,1,0:T(8,128)(2,1)S(1)}, u32[]{:S(2)}, u32[]{:S(2)}) collective-permute-start(bf16[8,24,1024]{2,1,0:T(8,128)(2,1)S(1)} %get-tuple-element.639), channel_id=1, source_target_pairs={{64,0},{128,64},{192,128},{256,192},{320,256},{384,320},{448,384},... | collective-permute-start | bytes 1179656 | tf_op jit(solution)/shard_map/ppermute | solution.py:15
  245.3 4.4 %collective-permute-done.4 = bf16[8,24,1024]{2,1,0:T(8,128)(2,1)S(1)} collective-permute-done((bf16[8,24,1024]{2,1,0:T(8,128)(2,1)S(1)}, bf16[8,24,1024]{2,1,0:T(8,128)(2,1)S(1)}, u32[]{:S(2)}, u32[]{:S(2)}) %collective-permute-start.4) | collective-permute-done | bytes 393248 | tf_op jit(solution)/shard_map/ppermute | solution.py:14
  249.6 39.4 %collective-permute-done.5 = bf16[8,24,1024]{2,1,0:T(8,128)(2,1)S(1)} collective-permute-done((bf16[8,24,1024]{2,1,0:T(8,128)(2,1)S(1)}, bf16[8,24,1024]{2,1,0:T(8,128)(2,1)S(1)}, u32[]{:S(2)}, u32[]{:S(2)}) %collective-permute-start.5) | collective-permute-done | bytes 393248 | tf_op jit(solution)/shard_map/ppermute | solution.py:15
  291.4 23.8 %collective-permute-start.7 = (bf16[16,8,1024]{2,1,0:T(8,128)(2,1)S(1)}, bf16[16,8,1024]{2,1,0:T(8,128)(2,1)S(1)}, u32[]{:S(2)}, u32[]{:S(2)}) collective-permute-start(bf16[16,8,1024]{2,1,0:T(8,128)(2,1)S(1)} %get-tuple-element.641), channel_id=1, source_target_pairs={{1,0},{2,1},{3,2},{4,3},{5,4},{6,5},{7,6},{8,7},{9,8},{10,9},{11,1... | collective-permute-start | bytes 786440 | tf_op jit(solution)/shard_map/ppermute | solution.py:15
  317.2 4.1 %collective-permute-done.9 = f32[8,13,13]{2,0,1:T(8,128)S(1)} collective-permute-done((f32[8,13,13]{2,0,1:T(8,128)S(1)}, f32[8,13,13]{2,0,1:T(8,128)S(1)}, u32[]{:S(2)}, u32[]{:S(2)}) %collective-permute-start.9) | collective-permute-done | bytes 5440 | tf_op jit(solution)/shard_map/ppermute | solution.py:127
  323.3 5.8 %collective-permute-done.10 = f32[8,13,13]{2,0,1:T(8,128)S(1)} collective-permute-done((f32[8,13,13]{2,0,1:T(8,128)S(1)}, f32[8,13,13]{2,0,1:T(8,128)S(1)}, u32[]{:S(2)}, u32[]{:S(2)}) %collective-permute-start.10) | collective-permute-done | bytes 5440 | tf_op jit(solution)/shard_map/ppermute | solution.py:127
  331.0 8.7 %collective-permute-done.11 = f32[8,13,13]{2,0,1:T(8,128)S(1)} collective-permute-done((f32[8,13,13]{2,0,1:T(8,128)S(1)}, f32[8,13,13]{2,0,1:T(8,128)S(1)}, u32[]{:S(2)}, u32[]{:S(2)}) %collective-permute-start.11) | collective-permute-done | bytes 5440 | tf_op jit(solution)/shard_map/ppermute | solution.py:127
  341.6 4.1 %collective-permute-done.12 = f32[8,13,13]{2,0,1:T(8,128)S(1)} collective-permute-done((f32[8,13,13]{2,0,1:T(8,128)S(1)}, f32[8,13,13]{2,0,1:T(8,128)S(1)}, u32[]{:S(2)}, u32[]{:S(2)}) %collective-permute-start.12) | collective-permute-done | bytes 5440 | tf_op jit(solution)/shard_map/ppermute | solution.py:127
  347.7 5.3 %collective-permute-done.13 = f32[8,13,13]{2,0,1:T(8,128)S(1)} collective-permute-done((f32[8,13,13]{2,0,1:T(8,128)S(1)}, f32[8,13,13]{2,0,1:T(8,128)S(1)}, u32[]{:S(2)}, u32[]{:S(2)}) %collective-permute-start.13) | collective-permute-done | bytes 5440 | tf_op jit(solution)/shard_map/ppermute | solution.py:127
  354.9 4.1 %collective-permute-done.14 = f32[8,13,13]{2,0,1:T(8,128)S(1)} collective-permute-done((f32[8,13,13]{2,0,1:T(8,128)S(1)}, f32[8,13,13]{2,0,1:T(8,128)S(1)}, u32[]{:S(2)}, u32[]{:S(2)}) %collective-permute-start.14) | collective-permute-done | bytes 5440 | tf_op jit(solution)/shard_map/ppermute | solution.py:127
  360.9 5.3 %collective-permute-done.15 = f32[8,13,13]{2,0,1:T(8,128)S(1)} collective-permute-done((f32[8,13,13]{2,0,1:T(8,128)S(1)}, f32[8,13,13]{2,0,1:T(8,128)S(1)}, u32[]{:S(2)}, u32[]{:S(2)}) %collective-permute-start.15) | collective-permute-done | bytes 5440 | tf_op jit(solution)/shard_map/ppermute | solution.py:127
  366.3 18.8 %collective-permute-start.16 = (f32[8,13,13]{2,0,1:T(8,128)S(1)}, f32[8,13,13]{2,0,1:T(8,128)S(1)}, u32[]{:S(2)}, u32[]{:S(2)}) collective-permute-start(f32[8,13,13]{2,0,1:T(8,128)S(1)} %add.252), channel_id=1, source_target_pairs={{0,256},{64,320},{128,384},{192,448},{256,0},{320,64},{384,128},{4... | collective-permute-start | bytes 16232 | tf_op jit(solution)/shard_map/ppermute | solution.py:127
  390.0 12.5 %collective-permute-done.17 = f32[8,13,13]{2,0,1:T(8,128)S(1)} collective-permute-done((f32[8,13,13]{2,0,1:T(8,128)S(1)}, f32[8,13,13]{2,0,1:T(8,128)S(1)}, u32[]{:S(2)}, u32[]{:S(2)}) %collective-permute-start.17) | collective-permute-done | bytes 5440 | tf_op jit(solution)/shard_map/ppermute | solution.py:127
  (207 shorter events, 129.0 us)
Async XLA Ops:
  2.5 38.7 %copy-start.13 = (f32[8,13,13]{2,0,1:T(8,128)S(1)}, f32[8,13,13]{2,0,1:T(8,128)}, u32[]{:S(2)}) copy-start(f32[8,13,13]{2,0,1:T(8,128)} %param.27) | copy-start | bytes 16228
  2.5 19.4 %collective-permute-start = (bf16[16,8,1024]{2,1,0:T(8,128)(2,1)S(1)}, bf16[16,8,1024]{2,1,0:T(8,128)(2,1)S(1)}, u32[]{:S(2)}, u32[]{:S(2)}) collective-permute-start(bf16[16,8,1024]{2,1,0:T(8,128)(2,1)S(1)} %constant_dynamic-update-slice_fusion.2), channel_id=1, source_target_pairs={{0,1},{1,2},{2,3},{3,4},{4,5},{5,6},{6,7},{7,8},{8,9},{9,10},{10,1... | collective-permute-start | bytes 786440 | tf_op jit(solution)/shard_map/ppermute | solution.py:14
  4.5 18.9 %collective-permute-start.1 = (bf16[16,8,1024]{2,1,0:T(8,128)(2,1)S(1)}, bf16[16,8,1024]{2,1,0:T(8,128)(2,1)S(1)}, u32[]{:S(2)}, u32[]{:S(2)}) collective-permute-start(bf16[16,8,1024]{2,1,0:T(8,128)(2,1)S(1)} %constant_dynamic-update-slice_fusion.2), channel_id=1, source_target_pairs={{1,0},{2,1},{3,2},{4,3},{5,4},{6,5},{7,6},{8,7},{9,8},{10,9},{11,1... | collective-permute-start | bytes 786440 | tf_op jit(solution)/shard_map/ppermute | solution.py:15
  23.6 21.0 %collective-permute-start.2 = (bf16[8,24,1024]{2,1,0:T(8,128)(2,1)S(1)}, bf16[8,24,1024]{2,1,0:T(8,128)(2,1)S(1)}, u32[]{:S(2)}, u32[]{:S(2)}) collective-permute-start(bf16[8,24,1024]{2,1,0:T(8,128)(2,1)S(1)} %get-tuple-element.642), channel_id=1, source_target_pairs={{0,64},{64,128},{128,192},{192,256},{256,320},{320,384},{384,448},... | collective-permute-start | bytes 1179656 | tf_op jit(solution)/shard_map/ppermute | solution.py:14
  39.2 73.2 %collective-permute-start.3 = (bf16[8,24,1024]{2,1,0:T(8,128)(2,1)S(1)}, bf16[8,24,1024]{2,1,0:T(8,128)(2,1)S(1)}, u32[]{:S(2)}, u32[]{:S(2)}) collective-permute-start(bf16[8,24,1024]{2,1,0:T(8,128)(2,1)S(1)} %get-tuple-element.643), channel_id=1, source_target_pairs={{64,0},{128,64},{192,128},{256,192},{320,256},{384,320},{448,384},... | collective-permute-start | bytes 1179656 | tf_op jit(solution)/shard_map/ppermute | solution.py:15
  140.0 7.0 %copy-start.1 = (f32[8,64,576]{2,1,0:T(8,128)}, f32[8,64,576]{2,1,0:T(8,128)S(1)}, u32[]{:S(2)}) copy-start(f32[8,64,576]{2,1,0:T(8,128)S(1)} %fusion.108) | copy-start | bytes 3538948 | tf_op jit(solution)/shard_map/while
  141.6 9.0 %copy-start.3 = (f32[8,64,576]{2,1,0:T(8,128)}, f32[8,64,576]{2,1,0:T(8,128)S(1)}, u32[]{:S(2)}) copy-start(f32[8,64,576]{2,1,0:T(8,128)S(1)} %get-tuple-element.737) | copy-start | bytes 3538948 | tf_op jit(solution)/shard_map/while
  198.8 7.0 %copy-start.1 = (f32[8,64,576]{2,1,0:T(8,128)}, f32[8,64,576]{2,1,0:T(8,128)S(1)}, u32[]{:S(2)}) copy-start(f32[8,64,576]{2,1,0:T(8,128)S(1)} %fusion.108) | copy-start | bytes 3538948 | tf_op jit(solution)/shard_map/while
  200.3 9.0 %copy-start.3 = (f32[8,64,576]{2,1,0:T(8,128)}, f32[8,64,576]{2,1,0:T(8,128)S(1)}, u32[]{:S(2)}) copy-start(f32[8,64,576]{2,1,0:T(8,128)S(1)} %get-tuple-element.737) | copy-start | bytes 3538948 | tf_op jit(solution)/shard_map/while
  234.8 8.3 %copy-start = (f32[32,24,1024]{2,1,0:T(8,128)S(1)}, f32[32,24,1024]{2,1,0:T(8,128)}, u32[]{:S(2)}) copy-start(f32[32,24,1024]{2,1,0:T(8,128)} %get-tuple-element.514) | copy-start | bytes 9437188
  237.2 12.4 %collective-permute-start.4 = (bf16[8,24,1024]{2,1,0:T(8,128)(2,1)S(1)}, bf16[8,24,1024]{2,1,0:T(8,128)(2,1)S(1)}, u32[]{:S(2)}, u32[]{:S(2)}) collective-permute-start(bf16[8,24,1024]{2,1,0:T(8,128)(2,1)S(1)} %get-tuple-element.638), channel_id=1, source_target_pairs={{0,64},{64,128},{128,192},{192,256},{256,320},{320,384},{384,448},... | collective-permute-start | bytes 1179656 | tf_op jit(solution)/shard_map/ppermute | solution.py:14
  239.1 49.9 %collective-permute-start.5 = (bf16[8,24,1024]{2,1,0:T(8,128)(2,1)S(1)}, bf16[8,24,1024]{2,1,0:T(8,128)(2,1)S(1)}, u32[]{:S(2)}, u32[]{:S(2)}) collective-permute-start(bf16[8,24,1024]{2,1,0:T(8,128)(2,1)S(1)} %get-tuple-element.639), channel_id=1, source_target_pairs={{64,0},{128,64},{192,128},{256,192},{320,256},{384,320},{448,384},... | collective-permute-start | bytes 1179656 | tf_op jit(solution)/shard_map/ppermute | solution.py:15
  243.3 71.9 %collective-permute-start.8 = (f32[8,13,13]{2,0,1:T(8,128)S(1)}, f32[8,13,13]{2,0,1:T(8,128)S(1)}, u32[]{:S(2)}, u32[]{:S(2)}) collective-permute-start(f32[8,13,13]{2,0,1:T(8,128)S(1)} %copy.61), channel_id=1, source_target_pairs={{0,1},{1,0},{2,3},{3,2},{4,5},{5,4},{6,7},{7,6},{8,9},{9,8},{10,11... | collective-permute-start | bytes 16232 | tf_op jit(solution)/shard_map/ppermute | solution.py:127
  289.5 113.7 %collective-permute-start.6 = (bf16[16,8,1024]{2,1,0:T(8,128)(2,1)S(1)}, bf16[16,8,1024]{2,1,0:T(8,128)(2,1)S(1)}, u32[]{:S(2)}, u32[]{:S(2)}) collective-permute-start(bf16[16,8,1024]{2,1,0:T(8,128)(2,1)S(1)} %get-tuple-element.640), channel_id=1, source_target_pairs={{0,1},{1,2},{2,3},{3,4},{4,5},{5,6},{6,7},{7,8},{8,9},{9,10},{10,1... | collective-permute-start | bytes 786440 | tf_op jit(solution)/shard_map/ppermute | solution.py:14
  291.4 111.7 %collective-permute-start.7 = (bf16[16,8,1024]{2,1,0:T(8,128)(2,1)S(1)}, bf16[16,8,1024]{2,1,0:T(8,128)(2,1)S(1)}, u32[]{:S(2)}, u32[]{:S(2)}) collective-permute-start(bf16[16,8,1024]{2,1,0:T(8,128)(2,1)S(1)} %get-tuple-element.641), channel_id=1, source_target_pairs={{1,0},{2,1},{3,2},{4,3},{5,4},{6,5},{7,6},{8,7},{9,8},{10,9},{11,1... | collective-permute-start | bytes 786440 | tf_op jit(solution)/shard_map/ppermute | solution.py:15
  315.3 6.0 %collective-permute-start.9 = (f32[8,13,13]{2,0,1:T(8,128)S(1)}, f32[8,13,13]{2,0,1:T(8,128)S(1)}, u32[]{:S(2)}, u32[]{:S(2)}) collective-permute-start(f32[8,13,13]{2,0,1:T(8,128)S(1)} %copy_add_fusion), channel_id=1, source_target_pairs={{0,2},{1,3},{2,0},{3,1},{4,6},{5,7},{6,4},{7,5},{8,10},{9,11},{10,... | collective-permute-start | bytes 16232 | tf_op jit(solution)/shard_map/ppermute | solution.py:127
  321.3 7.7 %collective-permute-start.10 = (f32[8,13,13]{2,0,1:T(8,128)S(1)}, f32[8,13,13]{2,0,1:T(8,128)S(1)}, u32[]{:S(2)}, u32[]{:S(2)}) collective-permute-start(f32[8,13,13]{2,0,1:T(8,128)S(1)} %add.246), channel_id=1, source_target_pairs={{0,4},{1,5},{2,6},{3,7},{4,0},{5,1},{6,2},{7,3},{8,12},{9,13},{10,... | collective-permute-start | bytes 16232 | tf_op jit(solution)/shard_map/ppermute | solution.py:127
  329.0 10.6 %collective-permute-start.11 = (f32[8,13,13]{2,0,1:T(8,128)S(1)}, f32[8,13,13]{2,0,1:T(8,128)S(1)}, u32[]{:S(2)}, u32[]{:S(2)}) collective-permute-start(f32[8,13,13]{2,0,1:T(8,128)S(1)} %add.247), channel_id=1, source_target_pairs={{0,8},{1,9},{2,10},{3,11},{4,12},{5,13},{6,14},{7,15},{8,0},{9,1},... | collective-permute-start | bytes 16232 | tf_op jit(solution)/shard_map/ppermute | solution.py:127
  339.7 6.0 %collective-permute-start.12 = (f32[8,13,13]{2,0,1:T(8,128)S(1)}, f32[8,13,13]{2,0,1:T(8,128)S(1)}, u32[]{:S(2)}, u32[]{:S(2)}) collective-permute-start(f32[8,13,13]{2,0,1:T(8,128)S(1)} %add.248), channel_id=1, source_target_pairs={{0,16},{1,17},{2,18},{3,19},{4,20},{5,21},{6,22},{7,23},{8,24},{9,... | collective-permute-start | bytes 16232 | tf_op jit(solution)/shard_map/ppermute | solution.py:127
  345.7 7.2 %collective-permute-start.13 = (f32[8,13,13]{2,0,1:T(8,128)S(1)}, f32[8,13,13]{2,0,1:T(8,128)S(1)}, u32[]{:S(2)}, u32[]{:S(2)}) collective-permute-start(f32[8,13,13]{2,0,1:T(8,128)S(1)} %add.249), channel_id=1, source_target_pairs={{0,48},{1,49},{2,50},{3,51},{4,52},{5,53},{6,54},{7,55},{8,56},{9,... | collective-permute-start | bytes 16232 | tf_op jit(solution)/shard_map/ppermute | solution.py:127
  353.0 6.0 %collective-permute-start.14 = (f32[8,13,13]{2,0,1:T(8,128)S(1)}, f32[8,13,13]{2,0,1:T(8,128)S(1)}, u32[]{:S(2)}, u32[]{:S(2)}) collective-permute-start(f32[8,13,13]{2,0,1:T(8,128)S(1)} %add.250), channel_id=1, source_target_pairs={{0,64},{64,0},{128,192},{192,128},{256,320},{320,256},{384,448},{4... | collective-permute-start | bytes 16232 | tf_op jit(solution)/shard_map/ppermute | solution.py:127
  359.0 7.2 %collective-permute-start.15 = (f32[8,13,13]{2,0,1:T(8,128)S(1)}, f32[8,13,13]{2,0,1:T(8,128)S(1)}, u32[]{:S(2)}, u32[]{:S(2)}) collective-permute-start(f32[8,13,13]{2,0,1:T(8,128)S(1)} %add.251), channel_id=1, source_target_pairs={{0,192},{64,128},{128,64},{192,0},{256,448},{320,384},{384,320},{4... | collective-permute-start | bytes 16232 | tf_op jit(solution)/shard_map/ppermute | solution.py:127
  366.3 21.4 %collective-permute-start.16 = (f32[8,13,13]{2,0,1:T(8,128)S(1)}, f32[8,13,13]{2,0,1:T(8,128)S(1)}, u32[]{:S(2)}, u32[]{:S(2)}) collective-permute-start(f32[8,13,13]{2,0,1:T(8,128)S(1)} %add.252), channel_id=1, source_target_pairs={{0,256},{64,320},{128,384},{192,448},{256,0},{320,64},{384,128},{4... | collective-permute-start | bytes 16232 | tf_op jit(solution)/shard_map/ppermute | solution.py:127
  387.6 14.8 %collective-permute-start.17 = (f32[8,13,13]{2,0,1:T(8,128)S(1)}, f32[8,13,13]{2,0,1:T(8,128)S(1)}, u32[]{:S(2)}, u32[]{:S(2)}) collective-permute-start(f32[8,13,13]{2,0,1:T(8,128)S(1)} %add.253), channel_id=1, source_target_pairs={{0,768},{64,832},{128,896},{192,960},{256,512},{320,576},{384,640}... | collective-permute-start | bytes 16232 | tf_op jit(solution)/shard_map/ppermute | solution.py:127
  (21 other events, 43.1 us)

commit v2 on v1

--- a/solution.py
+++ b/solution.py
@@ -142,8 +142,8 @@
     first_row = lax.axis_index("lat") * height
     first_col = lax.axis_index("lon") * breadth
     stacked = jnp.concatenate((key_vectors, value_vectors), axis=-1)
-    widened = padded_2(stacked, (("lon", 1),), 8, True)
-    padded = padded_2(widened, (("lat", 0),), 8, False)
+    tall = padded_2(stacked, (("lat", 0),), 8, False)
+    padded = padded_2(tall, (("lon", 1),), 8, True)
     across = breadth // 8
     tile_total = height // 8 * across
 
@@ -180,14 +180,14 @@
     accum, attention_out, grad_queries, grad_table = lax.fori_loop(
         0, tile_total, visit, start_state
     )
-    arrived = padded_2(rims_of(accum, 0).astype(jnp.bfloat16), (("lat", 0),), 8, False).astype(
-        jnp.float32
-    )
-    folded = settle(accum, arrived, 0)
-    arrived_cols = padded_2(rims_of(folded, 1).astype(jnp.bfloat16), (("lon", 1),), 8, True).astype(
-        jnp.float32
-    )
-    totals = settle(folded, arrived_cols, 1)
+    arrived_cols = padded_2(rims_of(accum, 1).astype(jnp.bfloat16), (("lon", 1),), 8, True).astype(
+        jnp.float32
+    )
+    folded = settle(accum, arrived_cols, 1)
+    arrived = padded_2(rims_of(folded, 0).astype(jnp.bfloat16), (("lat", 0),), 8, False).astype(
+        jnp.float32
+    )
+    totals = settle(folded, arrived, 0)
     grad_keys = totals[..., :model_width].astype(jnp.bfloat16)
     grad_values = totals[..., model_width:].astype(jnp.bfloat16)
     grad_window_bias = all_sum(grad_table)

time: 406 us -> 336 us (0.83)
  waiting for transfers between devices: 171 us -> 91 us
  starting transfers between devices: 103 us -> 110 us
    ppermute x4, waiting for transfers between devices: 109 us -> 36.3 us  [padded_2(): after = lax.ppermute(leading, axis, down)]
    ppermute x10, starting transfers between devices: 36.5 us -> 55 us  [exchange_sum(): return value + lax.ppermute(value, axis, pairs)]
    ppermute x4, starting transfers between devices: 44.9 us -> 28.7 us  [padded_2(): after = lax.ppermute(leading, axis, down)]
    ppermute x10, waiting for transfers between devices: 52.5 us -> 43.5 us  [exchange_sum(): return value + lax.ppermute(value, axis, pairs)]
    ppermute x4, starting transfers between devices: 21.5 us -> 26.4 us  [padded_2(): before = lax.ppermute(last, axis, up)]
  transfers between devices with their start and end apart: 18 -> 18, of which waited for: 15 -> 14; matrix products, arithmetic and copies ran while one was open for 0% -> 1% of each run, Pallas kernels for 0% -> 0%
where the time goes in v2:
time: 336 us; the launch traced here: 332 us
  starting transfers between devices  110 us (33%)
  waiting for transfers between devices  91 us (27%)
  local copies, waits for them, and re-layouts  76.1 us (23%)
  other arithmetic  31.2 us (9%)
  matrix products  22.4 us (7%)
    ppermute x10, starting transfers between devices, exchange_sum(): return value + lax.ppermute(value, axis, pairs)  55 us
    ppermute x10, waiting for transfers between devices, exchange_sum(): return value + lax.ppermute(value, axis, pairs)  43.5 us
    ppermute x4, waiting for transfers between devices, padded_2(): after = lax.ppermute(leading, axis, down)  36.3 us
    ppermute x4, starting transfers between devices, padded_2(): after = lax.ppermute(leading, axis, down)  28.7 us
    ppermute x4, starting transfers between devices, padded_2(): before = lax.ppermute(last, axis, up)  26.4 us
    another operation x4, local copies, waits for them, and re-layouts, place_bias(): col_spread = jnp.tile(col_part, (1, 1, 1, 24))  22.3 us
    ppermute x4, waiting for transfers between devices, padded_2(): before = lax.ppermute(last, axis, up)  11.2 us
    reshape x4, local copies, waits for them, and re-layouts, tile_pass(): value_heads = region[..., model_width:].reshape(576, head_count, head_dim)  10.8 us
  transfers between devices with their start and end apart: 18, of which 14 were waited for; matrix products, arithmetic and copies ran while one was open for 1% of the time, Pallas kernels for 0%

profile of v2, /device:TPU:6, one launch (start us, length us, event | category | flops | bytes accessed | tf_op | source)
XLA Modules:
  0.0 332.3 jit_solution(17082728720272225827)
XLA Ops:
  2.5 15.6 %collective-permute-start = (bf16[8,8,1024]{2,1,0:T(8,128)(2,1)S(1)}, bf16[8,8,1024]{2,1,0:T(8,128)(2,1)S(1)}, u32[]{:S(2)}, u32[]{:S(2)}) collective-permute-start(bf16[8,8,1024]{2,1,0:T(8,128)(2,1)S(1)} %get-tuple-element.646), channel_id=1, source_target_pairs={{0,64},{64,128},{128,192},{192,256},{256,320},{320,384},{384,448},... | collective-permute-start | bytes 393224 | tf_op jit(solution)/shard_map/ppermute | solution.py:14
  20.9 34.7 %collective-permute-done.1 = bf16[8,8,1024]{2,1,0:T(8,128)(2,1)S(1)} collective-permute-done((bf16[8,8,1024]{2,1,0:T(8,128)(2,1)S(1)}, bf16[8,8,1024]{2,1,0:T(8,128)(2,1)S(1)}, u32[]{:S(2)}, u32[]{:S(2)}) %collective-permute-start.1) | collective-permute-done | bytes 131104 | tf_op jit(solution)/shard_map/ppermute | solution.py:15
  57.6 12.4 %collective-permute-start.3 = (bf16[32,8,1024]{2,1,0:T(8,128)(2,1)S(1)}, bf16[32,8,1024]{2,1,0:T(8,128)(2,1)S(1)}, u32[]{:S(2)}, u32[]{:S(2)}) collective-permute-start(bf16[32,8,1024]{2,1,0:T(8,128)(2,1)S(1)} %pad_maximum_fusion.4), channel_id=1, source_target_pairs={{1,0},{2,1},{3,2},{4,3},{5,4},{6,5},{7,6},{8,7},{9,8},{10,9},{11,1... | collective-permute-start | bytes 1572872 | tf_op jit(solution)/shard_map/ppermute | solution.py:15
  70.7 4.5 %collective-permute-done.2 = bf16[32,8,1024]{2,1,0:T(8,128)(2,1)S(1)} collective-permute-done((bf16[32,8,1024]{2,1,0:T(8,128)(2,1)S(1)}, bf16[32,8,1024]{2,1,0:T(8,128)(2,1)S(1)}, u32[]{:S(2)}, u32[]{:S(2)}) %collective-permute-start.2) | collective-permute-done | bytes 524320 | tf_op jit(solution)/shard_map/ppermute | solution.py:14
  81.4 117.6 %while.31 = (s32[]{:T(128)}, f32[32,24,1024]{2,1,0:T(8,128)}, bf16[16,8,512]{2,1,0:T(8,128)(2,1)}, bf16[16,8,512]{2,1,0:T(8,128)(2,1)}, f32[8,13,13]{2,1,0:T(8,1...) while((s32[]{:T(128)}, f32[32,24,1024]{2,1,0:T(8,128)}, ...), condition=%wide.region_8.9_spmd.clone, body=%wide.region_0.8_spmd.clone.sunk | while | flops 261020608 | bytes 77249072 | solution.py:180
  84.5 4.6 %tile.54 = f32[8,13,8,24,24]{4,3,2,1,0:T(8,128)} broadcast(f32[8,13,8,24]{3,2,1,0:T(8,128)S(1)} %copy.91), dimensions={0,1,2,4} | broadcast | bytes 1996800 | tf_op jit(solution)/shard_map/while/body/eval_jaxpr/tile | solution.py:28
  89.1 6.6 %tile.55 = f32[8,13,8,576]{3,2,1,0:T(8,128)S(1)} reshape(f32[8,13,8,24,24]{4,3,2,1,0:T(8,128)} %tile.54) | data formatting | bytes 3833856 | tf_op jit(solution)/shard_map/while/body/eval_jaxpr/tile | solution.py:28
  132.7 4.1 %fusion.113 = f32[32,24,1024]{2,1,0:T(8,128)} fusion(f32[32,24,1024]{2,1,0:T(8,128)} %get-tuple-element.768, s32[]{:T(128)S(6)} %select_n.120, f32[24,24,512]{2,1,0:T(8,128)} %reshape.428, f32[24,24,512]{2,1,0:T(8,128)S(1)} %reshape.430), kind=kLoop, calls=%fused_computation.6.clone.1 | loop fusion | flops 1179648 | bytes 7077892 | tf_op jit(solution)/shard_map/while/body/eval_jaxpr/dynamic_update_slice | solution.py:169
  143.3 4.6 %tile.54 = f32[8,13,8,24,24]{4,3,2,1,0:T(8,128)} broadcast(f32[8,13,8,24]{3,2,1,0:T(8,128)S(1)} %copy.91), dimensions={0,1,2,4} | broadcast | bytes 1996800 | tf_op jit(solution)/shard_map/while/body/eval_jaxpr/tile | solution.py:28
  147.8 6.6 %tile.55 = f32[8,13,8,576]{3,2,1,0:T(8,128)S(1)} reshape(f32[8,13,8,24,24]{4,3,2,1,0:T(8,128)} %tile.54) | data formatting | bytes 3833856 | tf_op jit(solution)/shard_map/while/body/eval_jaxpr/tile | solution.py:28
  191.5 4.2 %fusion.113 = f32[32,24,1024]{2,1,0:T(8,128)} fusion(f32[32,24,1024]{2,1,0:T(8,128)} %get-tuple-element.768, s32[]{:T(128)S(6)} %select_n.120, f32[24,24,512]{2,1,0:T(8,128)} %reshape.428, f32[24,24,512]{2,1,0:T(8,128)S(1)} %reshape.430), kind=kLoop, calls=%fused_computation.6.clone.1 | loop fusion | flops 1179648 | bytes 7077892 | tf_op jit(solution)/shard_map/while/body/eval_jaxpr/dynamic_update_slice | solution.py:169
  203.2 12.5 %collective-permute-start.5 = (bf16[32,8,1024]{2,1,0:T(8,128)(2,1)S(1)}, bf16[32,8,1024]{2,1,0:T(8,128)(2,1)S(1)}, u32[]{:S(2)}, u32[]{:S(2)}) collective-permute-start(bf16[32,8,1024]{2,1,0:T(8,128)(2,1)S(1)} %get-tuple-element.641), channel_id=1, source_target_pairs={{1,0},{2,1},{3,2},{4,3},{5,4},{6,5},{7,6},{8,7},{9,8},{10,9},{11,1... | collective-permute-start | bytes 1572872 | tf_op jit(solution)/shard_map/ppermute | solution.py:15
  217.7 5.9 %collective-permute-done.4 = bf16[32,8,1024]{2,1,0:T(8,128)(2,1)S(1)} collective-permute-done((bf16[32,8,1024]{2,1,0:T(8,128)(2,1)S(1)}, bf16[32,8,1024]{2,1,0:T(8,128)(2,1)S(1)}, u32[]{:S(2)}, u32[]{:S(2)}) %collective-permute-start.4) | collective-permute-done | bytes 524320 | tf_op jit(solution)/shard_map/ppermute | solution.py:14
  225.1 6.9 %collective-permute-start.6 = (bf16[8,8,1024]{2,1,0:T(8,128)(2,1)S(1)}, bf16[8,8,1024]{2,1,0:T(8,128)(2,1)S(1)}, u32[]{:S(2)}, u32[]{:S(2)}) collective-permute-start(bf16[8,8,1024]{2,1,0:T(8,128)(2,1)S(1)} %get-tuple-element.642), channel_id=1, source_target_pairs={{0,64},{64,128},{128,192},{192,256},{256,320},{320,384},{384,448},... | collective-permute-start | bytes 393224 | tf_op jit(solution)/shard_map/ppermute | solution.py:14
  235.9 4.1 %collective-permute-done.9 = f32[8,13,13]{2,0,1:T(8,128)S(1)} collective-permute-done((f32[8,13,13]{2,0,1:T(8,128)S(1)}, f32[8,13,13]{2,0,1:T(8,128)S(1)}, u32[]{:S(2)}, u32[]{:S(2)}) %collective-permute-start.9) | collective-permute-done | bytes 5440 | tf_op jit(solution)/shard_map/ppermute | solution.py:127
  242.0 5.2 %collective-permute-done.10 = f32[8,13,13]{2,0,1:T(8,128)S(1)} collective-permute-done((f32[8,13,13]{2,0,1:T(8,128)S(1)}, f32[8,13,13]{2,0,1:T(8,128)S(1)}, u32[]{:S(2)}, u32[]{:S(2)}) %collective-permute-start.10) | collective-permute-done | bytes 5440 | tf_op jit(solution)/shard_map/ppermute | solution.py:127
  249.8 8.5 %collective-permute-done.11 = f32[8,13,13]{2,0,1:T(8,128)S(1)} collective-permute-done((f32[8,13,13]{2,0,1:T(8,128)S(1)}, f32[8,13,13]{2,0,1:T(8,128)S(1)}, u32[]{:S(2)}, u32[]{:S(2)}) %collective-permute-start.11) | collective-permute-done | bytes 5440 | tf_op jit(solution)/shard_map/ppermute | solution.py:127
  264.4 4.5 %collective-permute-start.13 = (f32[8,13,13]{2,0,1:T(8,128)S(1)}, f32[8,13,13]{2,0,1:T(8,128)S(1)}, u32[]{:S(2)}, u32[]{:S(2)}) collective-permute-start(f32[8,13,13]{2,0,1:T(8,128)S(1)} %add.249), channel_id=1, source_target_pairs={{0,48},{1,49},{2,50},{3,51},{4,52},{5,53},{6,54},{7,55},{8,56},{9,... | collective-permute-start | bytes 16232 | tf_op jit(solution)/shard_map/ppermute | solution.py:127
  273.5 4.1 %collective-permute-done.14 = f32[8,13,13]{2,0,1:T(8,128)S(1)} collective-permute-done((f32[8,13,13]{2,0,1:T(8,128)S(1)}, f32[8,13,13]{2,0,1:T(8,128)S(1)}, u32[]{:S(2)}, u32[]{:S(2)}) %collective-permute-start.14) | collective-permute-done | bytes 5440 | tf_op jit(solution)/shard_map/ppermute | solution.py:127
  279.6 5.3 %collective-permute-done.15 = f32[8,13,13]{2,0,1:T(8,128)S(1)} collective-permute-done((f32[8,13,13]{2,0,1:T(8,128)S(1)}, f32[8,13,13]{2,0,1:T(8,128)S(1)}, u32[]{:S(2)}, u32[]{:S(2)}) %collective-permute-start.15) | collective-permute-done | bytes 5440 | tf_op jit(solution)/shard_map/ppermute | solution.py:127
  284.9 26.6 %collective-permute-start.16 = (f32[8,13,13]{2,0,1:T(8,128)S(1)}, f32[8,13,13]{2,0,1:T(8,128)S(1)}, u32[]{:S(2)}, u32[]{:S(2)}) collective-permute-start(f32[8,13,13]{2,0,1:T(8,128)S(1)} %add.252), channel_id=1, source_target_pairs={{0,256},{64,320},{128,384},{192,448},{256,0},{320,64},{384,128},{4... | collective-permute-start | bytes 16232 | tf_op jit(solution)/shard_map/ppermute | solution.py:127
  311.5 4.5 %collective-permute-done.16 = f32[8,13,13]{2,0,1:T(8,128)S(1)} collective-permute-done((f32[8,13,13]{2,0,1:T(8,128)S(1)}, f32[8,13,13]{2,0,1:T(8,128)S(1)}, u32[]{:S(2)}, u32[]{:S(2)}) %collective-permute-start.16) | collective-permute-done | bytes 5440 | tf_op jit(solution)/shard_map/ppermute | solution.py:127
  316.0 9.7 %collective-permute-start.17 = (f32[8,13,13]{2,0,1:T(8,128)S(1)}, f32[8,13,13]{2,0,1:T(8,128)S(1)}, u32[]{:S(2)}, u32[]{:S(2)}) collective-permute-start(f32[8,13,13]{2,0,1:T(8,128)S(1)} %add.253), channel_id=1, source_target_pairs={{0,768},{64,832},{128,896},{192,960},{256,512},{320,576},{384,640}... | collective-permute-start | bytes 16232 | tf_op jit(solution)/shard_map/ppermute | solution.py:127
  325.7 5.1 %collective-permute-done.17 = f32[8,13,13]{2,0,1:T(8,128)S(1)} collective-permute-done((f32[8,13,13]{2,0,1:T(8,128)S(1)}, f32[8,13,13]{2,0,1:T(8,128)S(1)}, u32[]{:S(2)}, u32[]{:S(2)}) %collective-permute-start.17) | collective-permute-done | bytes 5440 | tf_op jit(solution)/shard_map/ppermute | solution.py:127
  (205 shorter events, 130.1 us)
Async XLA Ops:
  0.6 69.4 %copy-start.12 = (f32[8,13,13]{2,0,1:T(8,128)S(1)}, f32[8,13,13]{2,0,1:T(8,128)}, u32[]{:S(2)}) copy-start(f32[8,13,13]{2,0,1:T(8,128)} %param.27) | copy-start | bytes 16228
  2.5 18.4 %collective-permute-start = (bf16[8,8,1024]{2,1,0:T(8,128)(2,1)S(1)}, bf16[8,8,1024]{2,1,0:T(8,128)(2,1)S(1)}, u32[]{:S(2)}, u32[]{:S(2)}) collective-permute-start(bf16[8,8,1024]{2,1,0:T(8,128)(2,1)S(1)} %get-tuple-element.646), channel_id=1, source_target_pairs={{0,64},{64,128},{128,192},{192,256},{256,320},{320,384},{384,448},... | collective-permute-start | bytes 393224 | tf_op jit(solution)/shard_map/ppermute | solution.py:14
  18.2 37.5 %collective-permute-start.1 = (bf16[8,8,1024]{2,1,0:T(8,128)(2,1)S(1)}, bf16[8,8,1024]{2,1,0:T(8,128)(2,1)S(1)}, u32[]{:S(2)}, u32[]{:S(2)}) collective-permute-start(bf16[8,8,1024]{2,1,0:T(8,128)(2,1)S(1)} %get-tuple-element.647), channel_id=1, source_target_pairs={{64,0},{128,64},{192,128},{256,192},{320,256},{384,320},{448,384},... | collective-permute-start | bytes 393224 | tf_op jit(solution)/shard_map/ppermute | solution.py:15
  55.7 19.4 %collective-permute-start.2 = (bf16[32,8,1024]{2,1,0:T(8,128)(2,1)S(1)}, bf16[32,8,1024]{2,1,0:T(8,128)(2,1)S(1)}, u32[]{:S(2)}, u32[]{:S(2)}) collective-permute-start(bf16[32,8,1024]{2,1,0:T(8,128)(2,1)S(1)} %pad_maximum_fusion.4), channel_id=1, source_target_pairs={{0,1},{1,2},{2,3},{3,4},{4,5},{5,6},{6,7},{7,8},{8,9},{9,10},{10,1... | collective-permute-start | bytes 1572872 | tf_op jit(solution)/shard_map/ppermute | solution.py:14
  57.6 19.0 %collective-permute-start.3 = (bf16[32,8,1024]{2,1,0:T(8,128)(2,1)S(1)}, bf16[32,8,1024]{2,1,0:T(8,128)(2,1)S(1)}, u32[]{:S(2)}, u32[]{:S(2)}) collective-permute-start(bf16[32,8,1024]{2,1,0:T(8,128)(2,1)S(1)} %pad_maximum_fusion.4), channel_id=1, source_target_pairs={{1,0},{2,1},{3,2},{4,3},{5,4},{6,5},{7,6},{8,7},{9,8},{10,9},{11,1... | collective-permute-start | bytes 1572872 | tf_op jit(solution)/shard_map/ppermute | solution.py:15
  104.2 7.0 %copy-start = (f32[8,64,576]{2,1,0:T(8,128)}, f32[8,64,576]{2,1,0:T(8,128)S(1)}, u32[]{:S(2)}) copy-start(f32[8,64,576]{2,1,0:T(8,128)S(1)} %fusion.109) | copy-start | bytes 3538948 | tf_op jit(solution)/shard_map/while
  105.8 9.0 %copy-start.2 = (f32[8,64,576]{2,1,0:T(8,128)}, f32[8,64,576]{2,1,0:T(8,128)S(1)}, u32[]{:S(2)}) copy-start(f32[8,64,576]{2,1,0:T(8,128)S(1)} %get-tuple-element.739) | copy-start | bytes 3538948 | tf_op jit(solution)/shard_map/while
  163.0 7.0 %copy-start = (f32[8,64,576]{2,1,0:T(8,128)}, f32[8,64,576]{2,1,0:T(8,128)S(1)}, u32[]{:S(2)}) copy-start(f32[8,64,576]{2,1,0:T(8,128)S(1)} %fusion.109) | copy-start | bytes 3538948 | tf_op jit(solution)/shard_map/while
  164.5 9.0 %copy-start.2 = (f32[8,64,576]{2,1,0:T(8,128)}, f32[8,64,576]{2,1,0:T(8,128)S(1)}, u32[]{:S(2)}) copy-start(f32[8,64,576]{2,1,0:T(8,128)S(1)} %get-tuple-element.739) | copy-start | bytes 3538948 | tf_op jit(solution)/shard_map/while
  201.2 14.6 %copy-start.7 = (f32[8,13,13]{2,1,0:T(8,128)S(1)}, f32[8,13,13]{2,1,0:T(8,128)}, u32[]{:S(2)}) copy-start(f32[8,13,13]{2,1,0:T(8,128)} %get-tuple-element.515) | copy-start | bytes 16228
  201.3 22.3 %collective-permute-start.4 = (bf16[32,8,1024]{2,1,0:T(8,128)(2,1)S(1)}, bf16[32,8,1024]{2,1,0:T(8,128)(2,1)S(1)}, u32[]{:S(2)}, u32[]{:S(2)}) collective-permute-start(bf16[32,8,1024]{2,1,0:T(8,128)(2,1)S(1)} %get-tuple-element.640), channel_id=1, source_target_pairs={{0,1},{1,2},{2,3},{3,4},{4,5},{5,6},{6,7},{7,8},{8,9},{9,10},{10,1... | collective-permute-start | bytes 1572872 | tf_op jit(solution)/shard_map/ppermute | solution.py:14
  203.2 20.4 %collective-permute-start.5 = (bf16[32,8,1024]{2,1,0:T(8,128)(2,1)S(1)}, bf16[32,8,1024]{2,1,0:T(8,128)(2,1)S(1)}, u32[]{:S(2)}, u32[]{:S(2)}) collective-permute-start(bf16[32,8,1024]{2,1,0:T(8,128)(2,1)S(1)} %get-tuple-element.641), channel_id=1, source_target_pairs={{1,0},{2,1},{3,2},{4,3},{5,4},{6,5},{7,6},{8,7},{9,8},{10,9},{11,1... | collective-permute-start | bytes 1572872 | tf_op jit(solution)/shard_map/ppermute | solution.py:15
  215.8 18.2 %collective-permute-start.8 = (f32[8,13,13]{2,0,1:T(8,128)S(1)}, f32[8,13,13]{2,0,1:T(8,128)S(1)}, u32[]{:S(2)}, u32[]{:S(2)}) collective-permute-start(f32[8,13,13]{2,0,1:T(8,128)S(1)} %copy.60), channel_id=1, source_target_pairs={{0,1},{1,0},{2,3},{3,2},{4,5},{5,4},{6,7},{7,6},{8,9},{9,8},{10,11... | collective-permute-start | bytes 16232 | tf_op jit(solution)/shard_map/ppermute | solution.py:127
  225.1 106.3 %collective-permute-start.6 = (bf16[8,8,1024]{2,1,0:T(8,128)(2,1)S(1)}, bf16[8,8,1024]{2,1,0:T(8,128)(2,1)S(1)}, u32[]{:S(2)}, u32[]{:S(2)}) collective-permute-start(bf16[8,8,1024]{2,1,0:T(8,128)(2,1)S(1)} %get-tuple-element.642), channel_id=1, source_target_pairs={{0,64},{64,128},{128,192},{192,256},{256,320},{320,384},{384,448},... | collective-permute-start | bytes 393224 | tf_op jit(solution)/shard_map/ppermute | solution.py:14
  232.0 99.4 %collective-permute-start.7 = (bf16[8,8,1024]{2,1,0:T(8,128)(2,1)S(1)}, bf16[8,8,1024]{2,1,0:T(8,128)(2,1)S(1)}, u32[]{:S(2)}, u32[]{:S(2)}) collective-permute-start(bf16[8,8,1024]{2,1,0:T(8,128)(2,1)S(1)} %get-tuple-element.643), channel_id=1, source_target_pairs={{64,0},{128,64},{192,128},{256,192},{320,256},{384,320},{448,384},... | collective-permute-start | bytes 393224 | tf_op jit(solution)/shard_map/ppermute | solution.py:15
  234.0 6.1 %collective-permute-start.9 = (f32[8,13,13]{2,0,1:T(8,128)S(1)}, f32[8,13,13]{2,0,1:T(8,128)S(1)}, u32[]{:S(2)}, u32[]{:S(2)}) collective-permute-start(f32[8,13,13]{2,0,1:T(8,128)S(1)} %copy_add_fusion), channel_id=1, source_target_pairs={{0,2},{1,3},{2,0},{3,1},{4,6},{5,7},{6,4},{7,5},{8,10},{9,11},{10,... | collective-permute-start | bytes 16232 | tf_op jit(solution)/shard_map/ppermute | solution.py:127
  240.1 7.2 %collective-permute-start.10 = (f32[8,13,13]{2,0,1:T(8,128)S(1)}, f32[8,13,13]{2,0,1:T(8,128)S(1)}, u32[]{:S(2)}, u32[]{:S(2)}) collective-permute-start(f32[8,13,13]{2,0,1:T(8,128)S(1)} %add.246), channel_id=1, source_target_pairs={{0,4},{1,5},{2,6},{3,7},{4,0},{5,1},{6,2},{7,3},{8,12},{9,13},{10,... | collective-permute-start | bytes 16232 | tf_op jit(solution)/shard_map/ppermute | solution.py:127
  247.3 11.0 %collective-permute-start.11 = (f32[8,13,13]{2,0,1:T(8,128)S(1)}, f32[8,13,13]{2,0,1:T(8,128)S(1)}, u32[]{:S(2)}, u32[]{:S(2)}) collective-permute-start(f32[8,13,13]{2,0,1:T(8,128)S(1)} %add.247), channel_id=1, source_target_pairs={{0,8},{1,9},{2,10},{3,11},{4,12},{5,13},{6,14},{7,15},{8,0},{9,1},... | collective-permute-start | bytes 16232 | tf_op jit(solution)/shard_map/ppermute | solution.py:127
  258.3 6.0 %collective-permute-start.12 = (f32[8,13,13]{2,0,1:T(8,128)S(1)}, f32[8,13,13]{2,0,1:T(8,128)S(1)}, u32[]{:S(2)}, u32[]{:S(2)}) collective-permute-start(f32[8,13,13]{2,0,1:T(8,128)S(1)} %add.248), channel_id=1, source_target_pairs={{0,16},{1,17},{2,18},{3,19},{4,20},{5,21},{6,22},{7,23},{8,24},{9,... | collective-permute-start | bytes 16232 | tf_op jit(solution)/shard_map/ppermute | solution.py:127
  264.4 7.2 %collective-permute-start.13 = (f32[8,13,13]{2,0,1:T(8,128)S(1)}, f32[8,13,13]{2,0,1:T(8,128)S(1)}, u32[]{:S(2)}, u32[]{:S(2)}) collective-permute-start(f32[8,13,13]{2,0,1:T(8,128)S(1)} %add.249), channel_id=1, source_target_pairs={{0,48},{1,49},{2,50},{3,51},{4,52},{5,53},{6,54},{7,55},{8,56},{9,... | collective-permute-start | bytes 16232 | tf_op jit(solution)/shard_map/ppermute | solution.py:127
  271.6 6.0 %collective-permute-start.14 = (f32[8,13,13]{2,0,1:T(8,128)S(1)}, f32[8,13,13]{2,0,1:T(8,128)S(1)}, u32[]{:S(2)}, u32[]{:S(2)}) collective-permute-start(f32[8,13,13]{2,0,1:T(8,128)S(1)} %add.250), channel_id=1, source_target_pairs={{0,64},{64,0},{128,192},{192,128},{256,320},{320,256},{384,448},{4... | collective-permute-start | bytes 16232 | tf_op jit(solution)/shard_map/ppermute | solution.py:127
  277.6 7.2 %collective-permute-start.15 = (f32[8,13,13]{2,0,1:T(8,128)S(1)}, f32[8,13,13]{2,0,1:T(8,128)S(1)}, u32[]{:S(2)}, u32[]{:S(2)}) collective-permute-start(f32[8,13,13]{2,0,1:T(8,128)S(1)} %add.251), channel_id=1, source_target_pairs={{0,192},{64,128},{128,64},{192,0},{256,448},{320,384},{384,320},{4... | collective-permute-start | bytes 16232 | tf_op jit(solution)/shard_map/ppermute | solution.py:127
  284.9 31.1 %collective-permute-start.16 = (f32[8,13,13]{2,0,1:T(8,128)S(1)}, f32[8,13,13]{2,0,1:T(8,128)S(1)}, u32[]{:S(2)}, u32[]{:S(2)}) collective-permute-start(f32[8,13,13]{2,0,1:T(8,128)S(1)} %add.252), channel_id=1, source_target_pairs={{0,256},{64,320},{128,384},{192,448},{256,0},{320,64},{384,128},{4... | collective-permute-start | bytes 16232 | tf_op jit(solution)/shard_map/ppermute | solution.py:127
  316.0 14.7 %collective-permute-start.17 = (f32[8,13,13]{2,0,1:T(8,128)S(1)}, f32[8,13,13]{2,0,1:T(8,128)S(1)}, u32[]{:S(2)}, u32[]{:S(2)}) collective-permute-start(f32[8,13,13]{2,0,1:T(8,128)S(1)} %add.253), channel_id=1, source_target_pairs={{0,768},{64,832},{128,896},{192,960},{256,512},{320,576},{384,640}... | collective-permute-start | bytes 16232 | tf_op jit(solution)/shard_map/ppermute | solution.py:127
  (20 other events, 38.9 us)

commit v3 on v2

v3 whole, which is shorter than its diff:
```python
import jax
import jax.numpy as jnp
from jax import lax
from jax.sharding import PartitionSpec as P


def padded_2(value, sides, width, wrap):
    for axis, dim in sides:
        size, length = (lax.axis_size(axis), value.shape[dim])
        up = [(i, (i + 1) % size) for i in range(size if wrap else size - 1)]
        down = [(j, i) for i, j in up]
        last = lax.slice_in_dim(value, length - width, length, axis=dim)
        leading = lax.slice_in_dim(value, 0, width, axis=dim)
        before = lax.ppermute(last, axis, up)
        after = lax.ppermute(leading, axis, down)
        value = jnp.concatenate([before, value, after], axis=dim)
    return value


def rims_of(array, along):
    if along == 0:
        return jnp.concatenate((array[:8], array[-8:]), axis=0)
    return jnp.concatenate((array[:, :8], array[:, -8:]), axis=1)


def settle(array, arrived, along):
    if along == 0:
        inner = array[8:-8]
        inner = inner.at[:8].add(arrived[:8])
        return inner.at[-8:].add(arrived[-8:])
    inner = array[:, 8:-8]
    inner = inner.at[:, :8].add(arrived[:, :8])
    return inner.at[:, -8:].add(arrived[:, -8:])


def exchange_sum(value, axis, flip):
    size = lax.axis_size(axis)
    pairs = [(i, i ^ flip) for i in range(size)]
    return value + lax.ppermute(value, axis, pairs)


def all_sum(value):
    for axis, flips in (("lon", (1, 2, 4, 8, 16, 48)), ("lat", (1, 3, 4, 12))):
        for flip in flips:
            value = exchange_sum(value, axis, flip)
    return value


def per_device(
    queries, key_vectors, value_vectors, out_cotangent, lat_start, lon_start, window_bias
):
    height, breadth, model_width = queries.shape
    head_count, window, _ = window_bias.shape
    head_dim = model_width // head_count
    score_scale = head_dim ** (-0.5)
    lon_total = breadth * lax.axis_size("lon")
    first_row = lax.axis_index("lat") * height
    first_col = lax.axis_index("lon") * breadth
    stacked = jnp.concatenate((key_vectors, value_vectors), axis=-1)
    tall = padded_2(stacked, (("lat", 0),), 8, False)
    padded = padded_2(tall, (("lon", 1),), 8, True)
    rows, cols = height + 16, breadth + 16
    cells, keys = height * breadth, rows * cols
    exact = lax.Precision.HIGHEST

    rel_rows = lat_start - (first_row - 8)
    rel_cols = (lon_start - (first_col - 8)) % lon_total
    places = jnp.arange(window, dtype=jnp.int32)
    row_hot = (
        jnp.arange(rows, dtype=jnp.int32)[None, :, None] - rel_rows[:, None, None] == places
    ).astype(jnp.float32)
    col_hot = (
        jnp.arange(cols, dtype=jnp.int32)[None, :, None] - rel_cols[:, None, None] == places
    ).astype(jnp.float32)
    half_bias = jnp.einsum("hab,ira->hirb", window_bias, row_hot, precision=exact)
    bias = jnp.einsum("hirb,jcb->hijrc", half_bias, col_hot, precision=exact)
    bias = bias.reshape(head_count, cells, keys)
    inside = jnp.sum(row_hot, -1)[:, None, :, None] * jnp.sum(col_hot, -1)[None, :, None, :]
    inside = inside.reshape(cells, keys) > 0.5

    query_heads = queries.reshape(cells, head_count, head_dim)
    key_heads = padded[..., :model_width].reshape(keys, head_count, head_dim)
    value_heads = padded[..., model_width:].reshape(keys, head_count, head_dim)
    grad_heads = out_cotangent.reshape(cells, head_count, head_dim)
    scores = (
        jnp.einsum("qhd,khd->hqk", query_heads, key_heads, preferred_element_type=jnp.float32)
        * score_scale
        + bias
    )
    scores = jnp.where(inside[None], scores, -jnp.inf)
    row_peak = jnp.max(scores, axis=-1, keepdims=True)
    weights_raw = jnp.exp(scores - row_peak)
    row_total = jnp.sum(weights_raw, axis=-1, keepdims=True)
    attention = weights_raw / row_total
    rounded_probs = attention.astype(jnp.bfloat16)
    output = jnp.einsum(
        "hqk,khd->qhd", rounded_probs, value_heads, preferred_element_type=jnp.float32
    )
    attention_out = output.astype(jnp.bfloat16).reshape(height, breadth, model_width)
    dprobs = jnp.einsum("qhd,khd->hqk", grad_heads, value_heads, preferred_element_type=jnp.float32)
    correction = jnp.sum(attention * dprobs, axis=-1, keepdims=True)
    dscore = attention * (dprobs - correction)
    dscore_round = dscore.astype(jnp.bfloat16)
    grad_query = (
        jnp.einsum("hqk,khd->qhd", dscore_round, key_heads, preferred_element_type=jnp.float32)
        * score_scale
    )
    grad_queries = grad_query.astype(jnp.bfloat16).reshape(height, breadth, model_width)
    by_col = jnp.einsum(
        "hijrc,jcb->hirb",
        dscore.reshape(head_count, height, breadth, rows, cols),
        col_hot,
        precision=exact,
    )
    grad_table = jnp.einsum("hirb,ira->hab", by_col, row_hot, precision=exact)
    grad_keys = (
        jnp.einsum("hqk,qhd->khd", dscore_round, query_heads, preferred_element_type=jnp.float32)
        * score_scale
    )
    grad_vals = jnp.einsum(
        "hqk,qhd->khd", rounded_probs, grad_heads, preferred_element_type=jnp.float32
    )
    accum = jnp.concatenate(
        (grad_keys.reshape(rows, cols, model_width), grad_vals.reshape(rows, cols, model_width)),
        axis=-1,
    )
    arrived_cols = padded_2(rims_of(accum, 1).astype(jnp.bfloat16), (("lon", 1),), 8, True).astype(
        jnp.float32
    )
    folded = settle(accum, arrived_cols, 1)
    arrived = padded_2(rims_of(folded, 0).astype(jnp.bfloat16), (("lat", 0),), 8, False).astype(
        jnp.float32
    )
    totals = settle(folded, arrived, 0)
    grad_keys = totals[..., :model_width].astype(jnp.bfloat16)
    grad_values = totals[..., model_width:].astype(jnp.bfloat16)
    grad_window_bias = all_sum(grad_table)
    return (attention_out, grad_queries, grad_keys, grad_values, grad_window_bias)


def solution(mesh):
    return jax.shard_map(
        per_device,
        mesh=mesh,
        in_specs=(
            P("lat", "lon", None),
            P("lat", "lon", None),
            P("lat", "lon", None),
            P("lat", "lon", None),
            P("lat"),
            P("lon"),
            P(),
        ),
        out_specs=(
            P("lat", "lon", None),
            P("lat", "lon", None),
            P("lat", "lon", None),
            P("lat", "lon", None),
            P(),
        ),
        check_vma=False,
    )
```

time: 336 us -> 354 us (1.054)
  local copies, waits for them, and re-layouts: 76.1 us -> 99.4 us
  matrix products: 22.4 us -> 45.3 us
  other arithmetic: 31.2 us -> 13.2 us
  starting transfers between devices: 110 us -> 98.1 us
  waiting for transfers between devices: 91 us -> 95 us
    reshape x24 -> x15, local copies, waits for them, and re-layouts: 20.4 us -> 59.7 us  [the longest x2 16.6 us: per_device(): bias = bias.reshape(head_count, cells, keys)]
    another operation x10 -> x0, local copies, waits for them, and re-layouts: 24.6 us -> none  [the longest x4 22.3 us: place_bias(): col_spread = jnp.tile(col_part, (1, 1, 1, 24))]
    dot_general x16 -> x10, matrix products: 22.4 us -> 45.3 us  [the longest x1 19.8 us: per_device(): jnp.einsum('hijrc,jcb->hirb', dscore.reshape(head_count, height, breadth,...]
    ppermute x10, starting transfers between devices: 55 us -> 37.4 us  [exchange_sum(): return value + lax.ppermute(value, axis, pairs)]
    ppermute x4, waiting for transfers between devices: 36.3 us -> 50.9 us  [padded_2(): after = lax.ppermute(leading, axis, down)]
    transpose x4 -> x2, local copies, waits for them, and re-layouts: 5.11 us -> 18.6 us  [the longest x1 15.2 us: per_device(): bias = jnp.einsum('hirb,jcb->hijrc', half_bias, col_hot, precision=exact)]
    ppermute x4, waiting for transfers between devices: 11.2 us -> 0.01 us  [padded_2(): before = lax.ppermute(last, axis, up)]
    dynamic_update_slice x2 -> x0, other arithmetic: 8.33 us -> none  [visit(): lax.dynamic_update_slice(accum, current + tile_pairs, (tile_row, tile_col...]
  transfers between devices with their start and end apart: 18 -> 18, of which waited for: 14 -> 11; matrix products, arithmetic and copies ran while one was open for 1% -> 24% of each run, Pallas kernels for 0% -> 0%
where the time goes in v3:
time: 354 us; the launch traced here: 352 us
  local copies, waits for them, and re-layouts  99.4 us (28%)
  starting transfers between devices  98.1 us (28%)
  waiting for transfers between devices  95 us (27%)
  matrix products  45.3 us (13%)
  other arithmetic  13.2 us (4%)
    ppermute x4, waiting for transfers between devices, padded_2(): after = lax.ppermute(leading, axis, down)  50.9 us
    ppermute x10, waiting for transfers between devices, exchange_sum(): return value + lax.ppermute(value, axis, pairs)  44 us
    ppermute x10, starting transfers between devices, exchange_sum(): return value + lax.ppermute(value, axis, pairs)  37.4 us
    ppermute x4, starting transfers between devices, padded_2(): before = lax.ppermute(last, axis, up)  32.1 us
    ppermute x4, starting transfers between devices, padded_2(): after = lax.ppermute(leading, axis, down)  28.6 us
    dot_general x1, matrix products, per_device(): jnp.einsum('hijrc,jcb->hirb', dscore.reshape(head_count, height, breadth,...  19.8 us
    reshape x2, local copies, waits for them, and re-layouts, per_device(): bias = bias.reshape(head_count, cells, keys)  16.6 us
    transpose x1, local copies, waits for them, and re-layouts, per_device(): bias = jnp.einsum('hirb,jcb->hijrc', half_bias, col_hot, precision=exact)  15.2 us
  transfers between devices with their start and end apart: 18, of which 11 were waited for; matrix products, arithmetic and copies ran while one was open for 24% of the time, Pallas kernels for 0%

profile of v3, /device:TPU:6, one launch (start us, length us, event | category | flops | bytes accessed | tf_op | source)
XLA Modules:
  0.0 352.1 jit_solution(4275377966986935038)
XLA Ops:
  2.5 15.6 %collective-permute-start = (bf16[8,8,1024]{2,1,0:T(8,128)(2,1)S(1)}, bf16[8,8,1024]{2,1,0:T(8,128)(2,1)S(1)}, u32[]{:S(2)}, u32[]{:S(2)}) collective-permute-start(bf16[8,8,1024]{2,1,0:T(8,128)(2,1)S(1)} %get-tuple-element.89), channel_id=1, source_target_pairs={{0,64},{64,128},{128,192},{192,256},{256,320},{320,384},{384,448},... | collective-permute-start | bytes 393224 | tf_op jit(solution)/shard_map/ppermute | solution.py:14
  22.2 33.4 %collective-permute-done.1 = bf16[8,8,1024]{2,1,0:T(8,128)(2,1)S(1)} collective-permute-done((bf16[8,8,1024]{2,1,0:T(8,128)(2,1)S(1)}, bf16[8,8,1024]{2,1,0:T(8,128)(2,1)S(1)}, u32[]{:S(2)}, u32[]{:S(2)}) %collective-permute-start.1) | collective-permute-done | bytes 131104 | tf_op jit(solution)/shard_map/ppermute | solution.py:15
  58.5 12.4 %collective-permute-start.3 = (bf16[32,8,1024]{2,1,0:T(8,128)(2,1)}, bf16[32,8,1024]{2,1,0:T(8,128)(2,1)}, u32[]{:S(2)}, u32[]{:S(2)}) collective-permute-start(bf16[32,8,1024]{2,1,0:T(8,128)(2,1)} %pad_maximum_fusion.4), channel_id=1, source_target_pairs={{1,0},{2,1},{3,2},{4,3},{5,4},{6,5},{7,6},{8,7},{9,8},{10,9},{11,1... | collective-permute-start | bytes 1572872 | tf_op jit(solution)/shard_map/ppermute | solution.py:15
  70.8 7.9 %convolution_bitcast_fusion = f32[8,16,8,32,24]{3,4,1,0,2:T(8,128)} fusion(f32[8,16,32,13,1]{2,3,1,0,4:T(8,128)S(1)} %convolution_bitcast_fusion.3, s32[8,24]{1,0:T(8,128)S(1)} %iota_subtract_fusion.1), kind=kOutput, calls=%fused_computation.1 | convolution fusion | flops 122685888 | bytes 3359488 | tf_op jit(solution)/shard_map/hirb,jcb->hijrc/dot_general | solution.py:76
  78.8 15.2 %copy.31 = f32[8,16,8,32,24]{4,3,2,1,0:T(8,128)} copy(f32[8,16,8,32,24]{3,4,1,0,2:T(8,128)} %convolution_bitcast_fusion) | data formatting | bytes 6291456 | tf_op jit(solution)/shard_map/hirb,jcb->hijrc/transpose | solution.py:76
  94.0 14.3 %reshape.238 = f32[8,128,768]{2,1,0:T(8,128)} reshape(f32[8,16,8,32,24]{4,3,2,1,0:T(8,128)} %copy.31) | data formatting | bytes 6291456 | tf_op jit(solution)/shard_map/reshape | solution.py:77
  151.3 5.0 %convolution_bitcast_fusion.1 = f32[768,8,64]{0,2,1:T(8,128)} fusion(bf16[128,8,64]{0,2,1:T(8,128)(2,1)S(1)} %copy-done.10, f32[8,128]{1,0:T(8,128)S(1)} %get-tuple-element.91, f32[8,128,768]{1,2,0:T(8,128)} %copy-done.2), kind=kOutput, calls=%fused_computation.13 | convolution fusion | flops 103024384 | bytes 4853760 | tf_op jit(solution)/shard_map/hqk,qhd->khd/dot_general | solution.py:120
  156.3 14.4 %reshape.244 = f32[8,16,8,32,24]{4,3,2,1,0:T(8,128)} reshape(f32[8,128,768]{2,1,0:T(8,128)} %copy.47) | data formatting | bytes 6291456 | tf_op jit(solution)/shard_map/reshape | solution.py:111
  183.9 3.8 %reshape.243 = f32[32,24,512]{2,1,0:T(8,128)} reshape(f32[768,8,64]{2,1,0:T(8,128)} %copy.46) | data formatting | bytes 3145728 | tf_op jit(solution)/shard_map/reshape | solution.py:124
  194.6 12.4 %collective-permute-start.5 = (bf16[32,8,1024]{2,1,0:T(8,128)(2,1)S(1)}, bf16[32,8,1024]{2,1,0:T(8,128)(2,1)S(1)}, u32[]{:S(2)}, u32[]{:S(2)}) collective-permute-start(bf16[32,8,1024]{2,1,0:T(8,128)(2,1)S(1)} %get-tuple-element.82), channel_id=1, source_target_pairs={{1,0},{2,1},{3,2},{4,3},{5,4},{6,5},{7,6},{8,7},{9,8},{10,9},{11,1... | collective-permute-start | bytes 1572872 | tf_op jit(solution)/shard_map/ppermute | solution.py:15
  207.0 19.8 %convolution_bitcast_fusion.2 = f32[8,16,32,13]{2,3,1,0:T(8,128)S(1)} fusion(f32[8,16,8,32,24]{4,3,2,1,0:T(8,128)} %reshape.244, s32[8,24]{1,0:T(8,128)S(1)} %iota_subtract_fusion.1), kind=kOutput, calls=%fused_computation.14 | convolution fusion | flops 122685888 | bytes 3359488 | tf_op jit(solution)/shard_map/hijrc,jcb->hirb/dot_general | solution.py:109
  233.9 4.2 %collective-permute-done.9 = f32[8,13,13]{2,1,0:T(8,128)S(1)} collective-permute-done((f32[8,13,13]{2,1,0:T(8,128)S(1)}, f32[8,13,13]{2,1,0:T(8,128)S(1)}, u32[]{:S(2)}, u32[]{:S(2)}) %collective-permute-start.9) | collective-permute-done | bytes 5440 | tf_op jit(solution)/shard_map/ppermute | solution.py:39
  240.0 5.5 %collective-permute-done.10 = f32[8,13,13]{2,1,0:T(8,128)S(1)} collective-permute-done((f32[8,13,13]{2,1,0:T(8,128)S(1)}, f32[8,13,13]{2,1,0:T(8,128)S(1)}, u32[]{:S(2)}, u32[]{:S(2)}) %collective-permute-start.10) | collective-permute-done | bytes 5440 | tf_op jit(solution)/shard_map/ppermute | solution.py:39
  247.4 9.6 %collective-permute-done.11 = f32[8,13,13]{2,1,0:T(8,128)S(1)} collective-permute-done((f32[8,13,13]{2,1,0:T(8,128)S(1)}, f32[8,13,13]{2,1,0:T(8,128)S(1)}, u32[]{:S(2)}, u32[]{:S(2)}) %collective-permute-start.11) | collective-permute-done | bytes 5440 | tf_op jit(solution)/shard_map/ppermute | solution.py:39
  259.0 4.2 %collective-permute-done.12 = f32[8,13,13]{2,1,0:T(8,128)S(1)} collective-permute-done((f32[8,13,13]{2,1,0:T(8,128)S(1)}, f32[8,13,13]{2,1,0:T(8,128)S(1)}, u32[]{:S(2)}, u32[]{:S(2)}) %collective-permute-start.12) | collective-permute-done | bytes 5440 | tf_op jit(solution)/shard_map/ppermute | solution.py:39
  265.7 4.9 %collective-permute-done.13 = f32[8,13,13]{2,1,0:T(8,128)S(1)} collective-permute-done((f32[8,13,13]{2,1,0:T(8,128)S(1)}, f32[8,13,13]{2,1,0:T(8,128)S(1)}, u32[]{:S(2)}, u32[]{:S(2)}) %collective-permute-start.13) | collective-permute-done | bytes 5440 | tf_op jit(solution)/shard_map/ppermute | solution.py:39
  272.5 4.2 %collective-permute-done.14 = f32[8,13,13]{2,1,0:T(8,128)S(1)} collective-permute-done((f32[8,13,13]{2,1,0:T(8,128)S(1)}, f32[8,13,13]{2,1,0:T(8,128)S(1)}, u32[]{:S(2)}, u32[]{:S(2)}) %collective-permute-start.14) | collective-permute-done | bytes 5440 | tf_op jit(solution)/shard_map/ppermute | solution.py:39
  278.7 5.4 %collective-permute-done.15 = f32[8,13,13]{2,1,0:T(8,128)S(1)} collective-permute-done((f32[8,13,13]{2,1,0:T(8,128)S(1)}, f32[8,13,13]{2,1,0:T(8,128)S(1)}, u32[]{:S(2)}, u32[]{:S(2)}) %collective-permute-start.15) | collective-permute-done | bytes 5440 | tf_op jit(solution)/shard_map/ppermute | solution.py:39
  284.2 15.9 %collective-permute-start.16 = (f32[8,13,13]{2,1,0:T(8,128)S(1)}, f32[8,13,13]{2,1,0:T(8,128)S(1)}, u32[]{:S(2)}, u32[]{:S(2)}) collective-permute-start(f32[8,13,13]{2,1,0:T(8,128)S(1)} %add.86), channel_id=1, source_target_pairs={{0,256},{64,320},{128,384},{192,448},{256,0},{320,64},{384,128},{4... | collective-permute-start | bytes 16232 | tf_op jit(solution)/shard_map/ppermute | solution.py:39
  300.5 4.7 %collective-permute-done.16 = f32[8,13,13]{2,1,0:T(8,128)S(1)} collective-permute-done((f32[8,13,13]{2,1,0:T(8,128)S(1)}, f32[8,13,13]{2,1,0:T(8,128)S(1)}, u32[]{:S(2)}, u32[]{:S(2)}) %collective-permute-start.16) | collective-permute-done | bytes 5440 | tf_op jit(solution)/shard_map/ppermute | solution.py:39
  305.2 5.5 %collective-permute-start.17 = (f32[8,13,13]{2,1,0:T(8,128)S(1)}, f32[8,13,13]{2,1,0:T(8,128)S(1)}, u32[]{:S(2)}, u32[]{:S(2)}) collective-permute-start(f32[8,13,13]{2,1,0:T(8,128)S(1)} %add.87), channel_id=1, source_target_pairs={{0,768},{64,832},{128,896},{192,960},{256,512},{320,576},{384,640}... | collective-permute-start | bytes 16232 | tf_op jit(solution)/shard_map/ppermute | solution.py:39
  312.3 12.6 %collective-permute-start.6 = (bf16[8,8,1024]{2,1,0:T(8,128)(2,1)S(1)}, bf16[8,8,1024]{2,1,0:T(8,128)(2,1)S(1)}, u32[]{:S(2)}, u32[]{:S(2)}) collective-permute-start(bf16[8,8,1024]{2,1,0:T(8,128)(2,1)S(1)} %get-tuple-element.85), channel_id=1, source_target_pairs={{0,64},{64,128},{128,192},{192,256},{256,320},{320,384},{384,448},... | collective-permute-start | bytes 393224 | tf_op jit(solution)/shard_map/ppermute | solution.py:14
  326.9 3.9 %fusion.5 = bf16[128,8,64]{0,2,1:T(8,128)(2,1)S(1)} fusion(bf16[768,8,64]{0,2,1:T(8,128)(2,1)S(1)} %copy-done.6, f32[8,128]{1,0:T(8,128)S(1)} %get-tuple-element.91, f32[8,128,768]{1,2,0:T(8,128)} %copy-done.2), kind=kOutput, calls=%fused_computation.19 | convolution fusion | flops 103089920 | bytes 4067328 | tf_op jit(solution)/shard_map/hqk,khd->qhd/dot_general | solution.py:96
  333.7 17.5 %collective-permute-done.7 = bf16[8,8,1024]{2,1,0:T(8,128)(2,1)S(1)} collective-permute-done((bf16[8,8,1024]{2,1,0:T(8,128)(2,1)S(1)}, bf16[8,8,1024]{2,1,0:T(8,128)(2,1)S(1)}, u32[]{:S(2)}, u32[]{:S(2)}) %collective-permute-start.7) | collective-permute-done | bytes 131104 | tf_op jit(solution)/shard_map/ppermute | solution.py:15
  (104 shorter events, 98.4 us)
Async XLA Ops:
  0.6 21.0 %copy-start = (f32[8,13,13]{2,0,1:T(8,128)S(1)}, f32[8,13,13]{2,0,1:T(8,128)}, u32[]{:S(2)}) copy-start(f32[8,13,13]{2,0,1:T(8,128)} %param.25) | copy-start | bytes 16228
  2.5 19.7 %collective-permute-start = (bf16[8,8,1024]{2,1,0:T(8,128)(2,1)S(1)}, bf16[8,8,1024]{2,1,0:T(8,128)(2,1)S(1)}, u32[]{:S(2)}, u32[]{:S(2)}) collective-permute-start(bf16[8,8,1024]{2,1,0:T(8,128)(2,1)S(1)} %get-tuple-element.89), channel_id=1, source_target_pairs={{0,64},{64,128},{128,192},{192,256},{256,320},{320,384},{384,448},... | collective-permute-start | bytes 393224 | tf_op jit(solution)/shard_map/ppermute | solution.py:14
  18.2 37.5 %collective-permute-start.1 = (bf16[8,8,1024]{2,1,0:T(8,128)(2,1)S(1)}, bf16[8,8,1024]{2,1,0:T(8,128)(2,1)S(1)}, u32[]{:S(2)}, u32[]{:S(2)}) collective-permute-start(bf16[8,8,1024]{2,1,0:T(8,128)(2,1)S(1)} %get-tuple-element.90), channel_id=1, source_target_pairs={{64,0},{128,64},{192,128},{256,192},{320,256},{384,320},{448,384},... | collective-permute-start | bytes 393224 | tf_op jit(solution)/shard_map/ppermute | solution.py:15
  22.2 56.5 %copy-start.7 = (bf16[8,8,1024]{2,1,0:T(8,128)(2,1)}, bf16[8,8,1024]{2,1,0:T(8,128)(2,1)S(1)}, u32[]{:S(2)}) copy-start(bf16[8,8,1024]{2,1,0:T(8,128)(2,1)S(1)} %collective-permute-done) | copy-start | bytes 393220
  55.7 23.1 %copy-start.8 = (bf16[8,8,1024]{2,1,0:T(8,128)(2,1)}, bf16[8,8,1024]{2,1,0:T(8,128)(2,1)S(1)}, u32[]{:S(2)}) copy-start(bf16[8,8,1024]{2,1,0:T(8,128)(2,1)S(1)} %collective-permute-done.1) | copy-start | bytes 393220
  56.6 67.2 %collective-permute-start.2 = (bf16[32,8,1024]{2,1,0:T(8,128)(2,1)}, bf16[32,8,1024]{2,1,0:T(8,128)(2,1)}, u32[]{:S(2)}, u32[]{:S(2)}) collective-permute-start(bf16[32,8,1024]{2,1,0:T(8,128)(2,1)} %pad_maximum_fusion.4), channel_id=1, source_target_pairs={{0,1},{1,2},{2,3},{3,4},{4,5},{5,6},{6,7},{7,8},{8,9},{9,10},{10,1... | collective-permute-start | bytes 1572872 | tf_op jit(solution)/shard_map/ppermute | solution.py:14
  58.5 65.3 %collective-permute-start.3 = (bf16[32,8,1024]{2,1,0:T(8,128)(2,1)}, bf16[32,8,1024]{2,1,0:T(8,128)(2,1)}, u32[]{:S(2)}, u32[]{:S(2)}) collective-permute-start(bf16[32,8,1024]{2,1,0:T(8,128)(2,1)} %pad_maximum_fusion.4), channel_id=1, source_target_pairs={{1,0},{2,1},{3,2},{4,3},{5,4},{6,5},{7,6},{8,7},{9,8},{10,9},{11,1... | collective-permute-start | bytes 1572872 | tf_op jit(solution)/shard_map/ppermute | solution.py:15
  192.7 118.1 %collective-permute-start.4 = (bf16[32,8,1024]{2,1,0:T(8,128)(2,1)S(1)}, bf16[32,8,1024]{2,1,0:T(8,128)(2,1)S(1)}, u32[]{:S(2)}, u32[]{:S(2)}) collective-permute-start(bf16[32,8,1024]{2,1,0:T(8,128)(2,1)S(1)} %get-tuple-element.81), channel_id=1, source_target_pairs={{0,1},{1,2},{2,3},{3,4},{4,5},{5,6},{6,7},{7,8},{8,9},{9,10},{10,1... | collective-permute-start | bytes 1572872 | tf_op jit(solution)/shard_map/ppermute | solution.py:14
  194.6 116.2 %collective-permute-start.5 = (bf16[32,8,1024]{2,1,0:T(8,128)(2,1)S(1)}, bf16[32,8,1024]{2,1,0:T(8,128)(2,1)S(1)}, u32[]{:S(2)}, u32[]{:S(2)}) collective-permute-start(bf16[32,8,1024]{2,1,0:T(8,128)(2,1)S(1)} %get-tuple-element.82), channel_id=1, source_target_pairs={{1,0},{2,1},{3,2},{4,3},{5,4},{6,5},{7,6},{8,7},{9,8},{10,9},{11,1... | collective-permute-start | bytes 1572872 | tf_op jit(solution)/shard_map/ppermute | solution.py:15
  226.8 73.3 %copy-start.4 = (bf16[768,8,64]{0,2,1:T(8,128)(2,1)S(1)}, bf16[768,8,64]{0,2,1:T(8,128)(2,1)}, u32[]{:S(2)}) copy-start(bf16[768,8,64]{0,2,1:T(8,128)(2,1)} %copy.29) | copy-start | bytes 2359300
  228.8 3.2 collective-permute-start.8
  231.9 6.2 %collective-permute-start.9 = (f32[8,13,13]{2,1,0:T(8,128)S(1)}, f32[8,13,13]{2,1,0:T(8,128)S(1)}, u32[]{:S(2)}, u32[]{:S(2)}) collective-permute-start(f32[8,13,13]{2,1,0:T(8,128)S(1)} %add.79), channel_id=1, source_target_pairs={{0,2},{1,3},{2,0},{3,1},{4,6},{5,7},{6,4},{7,5},{8,10},{9,11},{10,... | collective-permute-start | bytes 16232 | tf_op jit(solution)/shard_map/ppermute | solution.py:39
  238.1 7.4 %collective-permute-start.10 = (f32[8,13,13]{2,1,0:T(8,128)S(1)}, f32[8,13,13]{2,1,0:T(8,128)S(1)}, u32[]{:S(2)}, u32[]{:S(2)}) collective-permute-start(f32[8,13,13]{2,1,0:T(8,128)S(1)} %add.80), channel_id=1, source_target_pairs={{0,4},{1,5},{2,6},{3,7},{4,0},{5,1},{6,2},{7,3},{8,12},{9,13},{10,... | collective-permute-start | bytes 16232 | tf_op jit(solution)/shard_map/ppermute | solution.py:39
  245.5 11.5 %collective-permute-start.11 = (f32[8,13,13]{2,1,0:T(8,128)S(1)}, f32[8,13,13]{2,1,0:T(8,128)S(1)}, u32[]{:S(2)}, u32[]{:S(2)}) collective-permute-start(f32[8,13,13]{2,1,0:T(8,128)S(1)} %add.81), channel_id=1, source_target_pairs={{0,8},{1,9},{2,10},{3,11},{4,12},{5,13},{6,14},{7,15},{8,0},{9,1},... | collective-permute-start | bytes 16232 | tf_op jit(solution)/shard_map/ppermute | solution.py:39
  257.0 6.2 %collective-permute-start.12 = (f32[8,13,13]{2,1,0:T(8,128)S(1)}, f32[8,13,13]{2,1,0:T(8,128)S(1)}, u32[]{:S(2)}, u32[]{:S(2)}) collective-permute-start(f32[8,13,13]{2,1,0:T(8,128)S(1)} %add.82), channel_id=1, source_target_pairs={{0,16},{1,17},{2,18},{3,19},{4,20},{5,21},{6,22},{7,23},{8,24},{9,... | collective-permute-start | bytes 16232 | tf_op jit(solution)/shard_map/ppermute | solution.py:39
  263.2 7.4 %collective-permute-start.13 = (f32[8,13,13]{2,1,0:T(8,128)S(1)}, f32[8,13,13]{2,1,0:T(8,128)S(1)}, u32[]{:S(2)}, u32[]{:S(2)}) collective-permute-start(f32[8,13,13]{2,1,0:T(8,128)S(1)} %add.83), channel_id=1, source_target_pairs={{0,48},{1,49},{2,50},{3,51},{4,52},{5,53},{6,54},{7,55},{8,56},{9,... | collective-permute-start | bytes 16232 | tf_op jit(solution)/shard_map/ppermute | solution.py:39
  270.6 6.2 %collective-permute-start.14 = (f32[8,13,13]{2,1,0:T(8,128)S(1)}, f32[8,13,13]{2,1,0:T(8,128)S(1)}, u32[]{:S(2)}, u32[]{:S(2)}) collective-permute-start(f32[8,13,13]{2,1,0:T(8,128)S(1)} %add.84), channel_id=1, source_target_pairs={{0,64},{64,0},{128,192},{192,128},{256,320},{320,256},{384,448},{4... | collective-permute-start | bytes 16232 | tf_op jit(solution)/shard_map/ppermute | solution.py:39
  276.8 7.4 %collective-permute-start.15 = (f32[8,13,13]{2,1,0:T(8,128)S(1)}, f32[8,13,13]{2,1,0:T(8,128)S(1)}, u32[]{:S(2)}, u32[]{:S(2)}) collective-permute-start(f32[8,13,13]{2,1,0:T(8,128)S(1)} %add.85), channel_id=1, source_target_pairs={{0,192},{64,128},{128,64},{192,0},{256,448},{320,384},{384,320},{4... | collective-permute-start | bytes 16232 | tf_op jit(solution)/shard_map/ppermute | solution.py:39
  284.2 21.1 %collective-permute-start.16 = (f32[8,13,13]{2,1,0:T(8,128)S(1)}, f32[8,13,13]{2,1,0:T(8,128)S(1)}, u32[]{:S(2)}, u32[]{:S(2)}) collective-permute-start(f32[8,13,13]{2,1,0:T(8,128)S(1)} %add.86), channel_id=1, source_target_pairs={{0,256},{64,320},{128,384},{192,448},{256,0},{320,64},{384,128},{4... | collective-permute-start | bytes 16232 | tf_op jit(solution)/shard_map/ppermute | solution.py:39
  300.5 26.4 %copy-start.6 = (bf16[768,8,64]{0,2,1:T(8,128)(2,1)S(1)}, bf16[768,8,64]{0,2,1:T(8,128)(2,1)}, u32[]{:S(2)}) copy-start(bf16[768,8,64]{0,2,1:T(8,128)(2,1)} %copy.33) | copy-start | bytes 2359300
  305.2 27.8 %collective-permute-start.17 = (f32[8,13,13]{2,1,0:T(8,128)S(1)}, f32[8,13,13]{2,1,0:T(8,128)S(1)}, u32[]{:S(2)}, u32[]{:S(2)}) collective-permute-start(f32[8,13,13]{2,1,0:T(8,128)S(1)} %add.87), channel_id=1, source_target_pairs={{0,768},{64,832},{128,896},{192,960},{256,512},{320,576},{384,640}... | collective-permute-start | bytes 16232 | tf_op jit(solution)/shard_map/ppermute | solution.py:39
  312.3 21.4 %collective-permute-start.6 = (bf16[8,8,1024]{2,1,0:T(8,128)(2,1)S(1)}, bf16[8,8,1024]{2,1,0:T(8,128)(2,1)S(1)}, u32[]{:S(2)}, u32[]{:S(2)}) collective-permute-start(bf16[8,8,1024]{2,1,0:T(8,128)(2,1)S(1)} %get-tuple-element.85), channel_id=1, source_target_pairs={{0,64},{64,128},{128,192},{192,256},{256,320},{320,384},{384,448},... | collective-permute-start | bytes 393224 | tf_op jit(solution)/shard_map/ppermute | solution.py:14
  325.0 26.3 %collective-permute-start.7 = (bf16[8,8,1024]{2,1,0:T(8,128)(2,1)S(1)}, bf16[8,8,1024]{2,1,0:T(8,128)(2,1)S(1)}, u32[]{:S(2)}, u32[]{:S(2)}) collective-permute-start(bf16[8,8,1024]{2,1,0:T(8,128)(2,1)S(1)} %get-tuple-element.86), channel_id=1, source_target_pairs={{64,0},{128,64},{192,128},{256,192},{320,256},{384,320},{448,384},... | collective-permute-start | bytes 393224 | tf_op jit(solution)/shard_map/ppermute | solution.py:15
  326.9 25.2 %copy-start.1 = (f32[8,13,13]{2,0,1:T(8,128)S(1)}, f32[8,13,13]{2,0,1:T(8,128)}, u32[]{:S(2)}) copy-start(f32[8,13,13]{2,0,1:T(8,128)} %param.25) | copy-start | bytes 16228
  (5 other events, 28.4 us)

commit v4 on v3

--- a/solution.py
+++ b/solution.py
@@ -66,17 +66,17 @@
     rel_rows = lat_start - (first_row - 8)
     rel_cols = (lon_start - (first_col - 8)) % lon_total
     places = jnp.arange(window, dtype=jnp.int32)
-    row_hot = (
-        jnp.arange(rows, dtype=jnp.int32)[None, :, None] - rel_rows[:, None, None] == places
-    ).astype(jnp.float32)
-    col_hot = (
-        jnp.arange(cols, dtype=jnp.int32)[None, :, None] - rel_cols[:, None, None] == places
-    ).astype(jnp.float32)
-    half_bias = jnp.einsum("hab,ira->hirb", window_bias, row_hot, precision=exact)
-    bias = jnp.einsum("hirb,jcb->hijrc", half_bias, col_hot, precision=exact)
+    key_index = jnp.arange(keys, dtype=jnp.int32)
+    row_off = (key_index // cols)[None, :] - rel_rows[:, None]
+    col_off = (key_index % cols)[None, :] - rel_cols[:, None]
+    row_hot = (row_off[:, None, :] == places[None, :, None]).astype(jnp.float32)
+    col_hot = (col_off[:, None, :] == places[None, :, None]).astype(jnp.float32)
+    half_bias = jnp.sum(window_bias[:, None, :, :, None] * row_hot[None, :, :, None, :], axis=2)
+    bias = jnp.sum(half_bias[:, :, None, :, :] * col_hot[None, None, :, :, :], axis=3)
     bias = bias.reshape(head_count, cells, keys)
-    inside = jnp.sum(row_hot, -1)[:, None, :, None] * jnp.sum(col_hot, -1)[None, :, None, :]
-    inside = inside.reshape(cells, keys) > 0.5
+    row_in = (row_off >= 0) & (row_off < window)
+    col_in = (col_off >= 0) & (col_off < window)
+    inside = (row_in[:, None, :] & col_in[None, :, :]).reshape(cells, keys)
 
     query_heads = queries.reshape(cells, head_count, head_dim)
     key_heads = padded[..., :model_width].reshape(keys, head_count, head_dim)
@@ -106,13 +106,9 @@
         * score_scale
     )
     grad_queries = grad_query.astype(jnp.bfloat16).reshape(height, breadth, model_width)
-    by_col = jnp.einsum(
-        "hijrc,jcb->hirb",
-        dscore.reshape(head_count, height, breadth, rows, cols),
-        col_hot,
-        precision=exact,
-    )
-    grad_table = jnp.einsum("hirb,ira->hab", by_col, row_hot, precision=exact)
+    grad_cells = dscore.reshape(head_count, height, breadth, keys)
+    by_col = jnp.sum(grad_cells[:, :, :, None, :] * col_hot[None, None, :, :, :], axis=2)
+    grad_table = jnp.einsum("hibk,iak->hab", by_col, row_hot, precision=exact)
     grad_keys = (
         jnp.einsum("hqk,qhd->khd", dscore_round, query_heads, preferred_element_type=jnp.float32)
         * score_scale

time: 354 us -> 274 us (0.77)
  local copies, waits for them, and re-layouts: 99.4 us -> 30.9 us
  other arithmetic: 13.2 us -> 37.3 us
  matrix products: 45.3 us -> 26.9 us
  starting transfers between devices: 98.1 us -> 89.2 us
  waiting for transfers between devices: 95 us -> 87.4 us
    reshape x3 -> x0, local copies, waits for them, and re-layouts: 31.1 us -> none  [the longest x2 16.6 us: per_device(): bias = bias.reshape(head_count, cells, keys)]
    reduce_sum x2 -> x3, other arithmetic: 0.06 us -> 27.6 us  [the longest x1 15.2 us: per_device(): jnp.sum(grad_cells[:, :, :, None, :] * col_hot[None, None, :, :, :], axis=2)]
    dot_general x4 -> x1, matrix products: 30.3 us -> 11 us  [per_device(): grad_table = jnp.einsum('hibk,iak->hab', by_col, row_hot, precision=exact)]
    ppermute x4, waiting for transfers between devices: 50.9 us -> 35.1 us  [padded_2(): after = lax.ppermute(leading, axis, down)]
    transpose x1 -> x0, local copies, waits for them, and re-layouts: 15.2 us -> none  [per_device(): bias = jnp.einsum('hirb,jcb->hijrc', half_bias, col_hot, precision=exact)]
    ppermute x4, starting transfers between devices: 28.6 us -> 18.3 us  [padded_2(): after = lax.ppermute(leading, axis, down)]
    ppermute x4, waiting for transfers between devices: 0.01 us -> 8.64 us  [padded_2(): before = lax.ppermute(last, axis, up)]
    gt x2 -> x0, local copies, waits for them, and re-layouts: 4.72 us -> none  [per_device(): inside = inside.reshape(cells, keys) > 0.5]
  transfers between devices with their start and end apart: 18 -> 18, of which waited for: 11 -> 13; matrix products, arithmetic and copies ran while one was open for 24% -> 22% of each run, Pallas kernels for 0% -> 0%
where the time goes in v4:
time: 274 us; the launch traced here: 273 us
  starting transfers between devices  89.2 us (33%)
  waiting for transfers between devices  87.4 us (32%)
  other arithmetic  37.3 us (14%)
  local copies, waits for them, and re-layouts  30.9 us (11%)
  matrix products  26.9 us (10%)
    ppermute x10, waiting for transfers between devices, exchange_sum(): return value + lax.ppermute(value, axis, pairs)  43.7 us
    ppermute x10, starting transfers between devices, exchange_sum(): return value + lax.ppermute(value, axis, pairs)  37.7 us
    ppermute x4, waiting for transfers between devices, padded_2(): after = lax.ppermute(leading, axis, down)  35.1 us
    ppermute x4, starting transfers between devices, padded_2(): before = lax.ppermute(last, axis, up)  33.2 us
    ppermute x4, starting transfers between devices, padded_2(): after = lax.ppermute(leading, axis, down)  18.3 us
    reduce_sum x1, other arithmetic, per_device(): jnp.sum(grad_cells[:, :, :, None, :] * col_hot[None, None, :, :, :], axis=2)  15.2 us
    dot_general x1, matrix products, per_device(): grad_table = jnp.einsum('hibk,iak->hab', by_col, row_hot, precision=exact)  11 us
    ppermute x4, waiting for transfers between devices, padded_2(): before = lax.ppermute(last, axis, up)  8.64 us
  transfers between devices with their start and end apart: 18, of which 13 were waited for; matrix products, arithmetic and copies ran while one was open for 22% of the time, Pallas kernels for 0%

profile of v4, /device:TPU:6, one launch (start us, length us, event | category | flops | bytes accessed | tf_op | source)
XLA Modules:
  0.0 272.9 jit_solution(6532118040545232932)
XLA Ops:
  2.5 15.6 %collective-permute-start = (bf16[8,8,1024]{2,1,0:T(8,128)(2,1)S(1)}, bf16[8,8,1024]{2,1,0:T(8,128)(2,1)S(1)}, u32[]{:S(2)}, u32[]{:S(2)}) collective-permute-start(bf16[8,8,1024]{2,1,0:T(8,128)(2,1)S(1)} %get-tuple-element.96), channel_id=1, source_target_pairs={{0,64},{64,128},{128,192},{192,256},{256,320},{320,384},{384,448},... | collective-permute-start | bytes 393224 | tf_op jit(solution)/shard_map/ppermute | solution.py:14
  27.0 6.5 %multiply_reduce_fusion = f32[8,16,13,768]{3,1,2,0:T(8,128)S(1)} fusion(f32[16,13,768]{2,0,1:T(8,128)S(1)} %copy.41, f32[8,13,13]{2,1,0:T(8,128)S(1)} %copy.40), kind=kLoop, calls=%fused_computation.1 | loop fusion | flops 31948800 | bytes 5756192 | tf_op jit(solution)/shard_map/reduce_sum | solution.py:74
  37.1 18.4 %collective-permute-done.1 = bf16[8,8,1024]{2,1,0:T(8,128)(2,1)S(1)} collective-permute-done((bf16[8,8,1024]{2,1,0:T(8,128)(2,1)S(1)}, bf16[8,8,1024]{2,1,0:T(8,128)(2,1)S(1)}, u32[]{:S(2)}, u32[]{:S(2)}) %collective-permute-start.1) | collective-permute-done | bytes 131104 | tf_op jit(solution)/shard_map/ppermute | solution.py:15
  60.2 5.9 %multiply_reduce_fusion.2 = f32[8,16,8,768]{3,2,1,0:T(8,128)} fusion(f32[8,13,768]{2,0,1:T(8,128)S(1)} %fusion.16, f32[8,16,13,768]{3,2,1,0:T(8,128)S(1)} %copy.42), kind=kLoop, calls=%fused_computation.3 | loop fusion | flops 19660800 | bytes 8577024 | tf_op jit(solution)/shard_map/reduce_sum | solution.py:75
  68.1 8.6 %collective-permute-done.2 = bf16[32,8,1024]{2,1,0:T(8,128)(2,1)S(1)} collective-permute-done((bf16[32,8,1024]{2,1,0:T(8,128)(2,1)S(1)}, bf16[32,8,1024]{2,1,0:T(8,128)(2,1)S(1)}, u32[]{:S(2)}, u32[]{:S(2)}) %collective-permute-start.2) | collective-permute-done | bytes 524320 | tf_op jit(solution)/shard_map/ppermute | solution.py:14
  87.7 4.1 %convolution_bitcast_fusion = f32[768,8,64]{0,2,1:T(8,128)} fusion(bf16[128,8,64]{0,2,1:T(8,128)(2,1)} %copy.46, f32[8,128]{1,0:T(8,128)S(1)} %get-tuple-element.98, f32[8,128,768]{2,1,0:T(8,128)S(1)} %fusion.3), kind=kOutput, calls=%fused_computation.14 | convolution fusion | flops 103024384 | bytes 4853760 | tf_op jit(solution)/shard_map/hqk,qhd->khd/dot_general | solution.py:116
  95.8 3.1 %fusion.1 = (f32[8,128]{1,0:T(8,128)S(1)}, f32[8,768,128]{1,2,0:T(8,128)S(1)}) fusion(f32[8,128,768]{2,1,0:T(8,128)} %get-tuple-element.99, f32[8,128]{1,0:T(8,128)S(1)} %get-tuple-element.98, bf16[768,8,64]{0,2,1:T(8,128)(2,1)} %copy.43, bf16[128,8,64]{0,2,1:T(8,128)(2,1)} %copy.46), kind=kOutput, calls=%fused_computation.6 | convolution fusion | flops 103021568 | bytes 7217152 | tf_op jit(solution)/shard_map/qhd,khd->hqk/dot_general | solution.py:100
  104.0 3.9 %reshape.311 = f32[32,24,512]{2,1,0:T(8,128)} reshape(f32[768,8,64]{2,1,0:T(8,128)} %copy.50) | data formatting | bytes 3145728 | tf_op jit(solution)/shard_map/reshape | solution.py:120
  112.0 12.6 %collective-permute-start.5 = (bf16[32,8,1024]{2,1,0:T(8,128)(2,1)S(1)}, bf16[32,8,1024]{2,1,0:T(8,128)(2,1)S(1)}, u32[]{:S(2)}, u32[]{:S(2)}) collective-permute-start(bf16[32,8,1024]{2,1,0:T(8,128)(2,1)S(1)} %get-tuple-element.89), channel_id=1, source_target_pairs={{1,0},{2,1},{3,2},{4,3},{5,4},{6,5},{7,6},{8,7},{9,8},{10,9},{11,1... | collective-permute-start | bytes 1572872 | tf_op jit(solution)/shard_map/ppermute | solution.py:15
  124.6 15.2 %multiply_reduce_fusion.1 = f32[8,16,13,768]{3,2,1,0:T(8,128)S(1)} fusion(f32[8,16,8,768]{3,2,1,0:T(8,128)S(1)} %copy-done.1, f32[8,13,768]{2,0,1:T(8,128)S(1)} %fusion.16), kind=kLoop, calls=%fused_computation.2 | loop fusion | flops 19169280 | bytes 8577024 | tf_op jit(solution)/shard_map/reduce_sum | solution.py:110
  139.8 11.0 %convolution_bitcast_fusion.1 = f32[8,13,13]{2,1,0:T(8,128)S(1)} fusion(f32[8,16,13,768]{3,2,1,0:T(8,128)S(1)} %multiply_reduce_fusion.1, s32[16,768]{1,0:T(8,128)S(1)} %broadcast_subtract_fusion), kind=kOutput, calls=%fused_computation.22 | convolution fusion | flops 199520256 | bytes 5166368 | tf_op jit(solution)/shard_map/hibk,iak->hab/dot_general | solution.py:111
  155.9 4.2 %collective-permute-done.9 = f32[8,13,13]{2,1,0:T(8,128)S(1)} collective-permute-done((f32[8,13,13]{2,1,0:T(8,128)S(1)}, f32[8,13,13]{2,1,0:T(8,128)S(1)}, u32[]{:S(2)}, u32[]{:S(2)}) %collective-permute-start.9) | collective-permute-done | bytes 5440 | tf_op jit(solution)/shard_map/ppermute | solution.py:39
  162.1 5.5 %collective-permute-done.10 = f32[8,13,13]{2,1,0:T(8,128)S(1)} collective-permute-done((f32[8,13,13]{2,1,0:T(8,128)S(1)}, f32[8,13,13]{2,1,0:T(8,128)S(1)}, u32[]{:S(2)}, u32[]{:S(2)}) %collective-permute-start.10) | collective-permute-done | bytes 5440 | tf_op jit(solution)/shard_map/ppermute | solution.py:39
  169.5 9.6 %collective-permute-done.11 = f32[8,13,13]{2,1,0:T(8,128)S(1)} collective-permute-done((f32[8,13,13]{2,1,0:T(8,128)S(1)}, f32[8,13,13]{2,1,0:T(8,128)S(1)}, u32[]{:S(2)}, u32[]{:S(2)}) %collective-permute-start.11) | collective-permute-done | bytes 5440 | tf_op jit(solution)/shard_map/ppermute | solution.py:39
  181.0 4.2 %collective-permute-done.12 = f32[8,13,13]{2,1,0:T(8,128)S(1)} collective-permute-done((f32[8,13,13]{2,1,0:T(8,128)S(1)}, f32[8,13,13]{2,1,0:T(8,128)S(1)}, u32[]{:S(2)}, u32[]{:S(2)}) %collective-permute-start.12) | collective-permute-done | bytes 5440 | tf_op jit(solution)/shard_map/ppermute | solution.py:39
  187.8 4.9 %collective-permute-done.13 = f32[8,13,13]{2,1,0:T(8,128)S(1)} collective-permute-done((f32[8,13,13]{2,1,0:T(8,128)S(1)}, f32[8,13,13]{2,1,0:T(8,128)S(1)}, u32[]{:S(2)}, u32[]{:S(2)}) %collective-permute-start.13) | collective-permute-done | bytes 5440 | tf_op jit(solution)/shard_map/ppermute | solution.py:39
  194.6 4.2 %collective-permute-done.14 = f32[8,13,13]{2,1,0:T(8,128)S(1)} collective-permute-done((f32[8,13,13]{2,1,0:T(8,128)S(1)}, f32[8,13,13]{2,1,0:T(8,128)S(1)}, u32[]{:S(2)}, u32[]{:S(2)}) %collective-permute-start.14) | collective-permute-done | bytes 5440 | tf_op jit(solution)/shard_map/ppermute | solution.py:39
  200.7 5.4 %collective-permute-done.15 = f32[8,13,13]{2,1,0:T(8,128)S(1)} collective-permute-done((f32[8,13,13]{2,1,0:T(8,128)S(1)}, f32[8,13,13]{2,1,0:T(8,128)S(1)}, u32[]{:S(2)}, u32[]{:S(2)}) %collective-permute-start.15) | collective-permute-done | bytes 5440 | tf_op jit(solution)/shard_map/ppermute | solution.py:39
  206.2 15.9 %collective-permute-start.16 = (f32[8,13,13]{2,1,0:T(8,128)S(1)}, f32[8,13,13]{2,1,0:T(8,128)S(1)}, u32[]{:S(2)}, u32[]{:S(2)}) collective-permute-start(f32[8,13,13]{2,1,0:T(8,128)S(1)} %add.102), channel_id=1, source_target_pairs={{0,256},{64,320},{128,384},{192,448},{256,0},{320,64},{384,128},{4... | collective-permute-start | bytes 16232 | tf_op jit(solution)/shard_map/ppermute | solution.py:39
  222.8 4.4 %collective-permute-done.16 = f32[8,13,13]{2,1,0:T(8,128)S(1)} collective-permute-done((f32[8,13,13]{2,1,0:T(8,128)S(1)}, f32[8,13,13]{2,1,0:T(8,128)S(1)}, u32[]{:S(2)}, u32[]{:S(2)}) %collective-permute-start.16) | collective-permute-done | bytes 5440 | tf_op jit(solution)/shard_map/ppermute | solution.py:39
  227.9 5.8 %collective-permute-start.17 = (f32[8,13,13]{2,1,0:T(8,128)}, f32[8,13,13]{2,1,0:T(8,128)}, u32[]{:S(2)}, u32[]{:S(2)}) collective-permute-start(f32[8,13,13]{2,1,0:T(8,128)} %add.103), channel_id=1, source_target_pairs={{0,768},{64,832},{128,896},{192,960},{256,512},{320,576},{384,640}... | collective-permute-start | bytes 16232 | tf_op jit(solution)/shard_map/ppermute | solution.py:39
  234.0 12.9 %collective-permute-start.6 = (bf16[8,8,1024]{2,1,0:T(8,128)(2,1)S(1)}, bf16[8,8,1024]{2,1,0:T(8,128)(2,1)S(1)}, u32[]{:S(2)}, u32[]{:S(2)}) collective-permute-start(bf16[8,8,1024]{2,1,0:T(8,128)(2,1)S(1)} %get-tuple-element.92), channel_id=1, source_target_pairs={{0,64},{64,128},{128,192},{192,256},{256,320},{320,384},{384,448},... | collective-permute-start | bytes 393224 | tf_op jit(solution)/shard_map/ppermute | solution.py:14
  248.9 4.8 %fusion.7 = bf16[128,8,64]{0,2,1:T(8,128)(2,1)S(1)} fusion(bf16[768,8,64]{0,2,1:T(8,128)(2,1)S(1)} %copy-done.6, f32[8,128]{1,0:T(8,128)S(1)} %get-tuple-element.98, f32[8,128,768]{2,1,0:T(8,128)} %copy-done), kind=kOutput, calls=%fused_computation.20 | convolution fusion | flops 103089920 | bytes 4067328 | tf_op jit(solution)/shard_map/hqk,khd->qhd/dot_general | solution.py:96
  257.4 14.6 %collective-permute-done.7 = bf16[8,8,1024]{2,1,0:T(8,128)(2,1)S(1)} collective-permute-done((bf16[8,8,1024]{2,1,0:T(8,128)(2,1)S(1)}, bf16[8,8,1024]{2,1,0:T(8,128)(2,1)S(1)}, u32[]{:S(2)}, u32[]{:S(2)}) %collective-permute-start.7) | collective-permute-done | bytes 131104 | tf_op jit(solution)/shard_map/ppermute | solution.py:15
  (96 shorter events, 70.3 us)
Async XLA Ops:
  2.5 34.6 %collective-permute-start = (bf16[8,8,1024]{2,1,0:T(8,128)(2,1)S(1)}, bf16[8,8,1024]{2,1,0:T(8,128)(2,1)S(1)}, u32[]{:S(2)}, u32[]{:S(2)}) collective-permute-start(bf16[8,8,1024]{2,1,0:T(8,128)(2,1)S(1)} %get-tuple-element.96), channel_id=1, source_target_pairs={{0,64},{64,128},{128,192},{192,256},{256,320},{320,384},{384,448},... | collective-permute-start | bytes 393224 | tf_op jit(solution)/shard_map/ppermute | solution.py:14
  18.1 37.4 %collective-permute-start.1 = (bf16[8,8,1024]{2,1,0:T(8,128)(2,1)S(1)}, bf16[8,8,1024]{2,1,0:T(8,128)(2,1)S(1)}, u32[]{:S(2)}, u32[]{:S(2)}) collective-permute-start(bf16[8,8,1024]{2,1,0:T(8,128)(2,1)S(1)} %get-tuple-element.97), channel_id=1, source_target_pairs={{64,0},{128,64},{192,128},{256,192},{320,256},{384,320},{448,384},... | collective-permute-start | bytes 393224 | tf_op jit(solution)/shard_map/ppermute | solution.py:15
  55.6 12.5 %collective-permute-start.3 = (bf16[32,8,1024]{2,1,0:T(8,128)(2,1)S(1)}, bf16[32,8,1024]{2,1,0:T(8,128)(2,1)S(1)}, u32[]{:S(2)}, u32[]{:S(2)}) collective-permute-start(bf16[32,8,1024]{2,1,0:T(8,128)(2,1)S(1)} %pad_maximum_fusion.4), channel_id=1, source_target_pairs={{1,0},{2,1},{3,2},{4,3},{5,4},{6,5},{7,6},{8,7},{9,8},{10,9},{11,1... | collective-permute-start | bytes 1572872 | tf_op jit(solution)/shard_map/ppermute | solution.py:15
  57.6 19.2 %collective-permute-start.2 = (bf16[32,8,1024]{2,1,0:T(8,128)(2,1)S(1)}, bf16[32,8,1024]{2,1,0:T(8,128)(2,1)S(1)}, u32[]{:S(2)}, u32[]{:S(2)}) collective-permute-start(bf16[32,8,1024]{2,1,0:T(8,128)(2,1)S(1)} %pad_maximum_fusion.4), channel_id=1, source_target_pairs={{0,1},{1,2},{2,3},{3,4},{4,5},{5,6},{6,7},{7,8},{8,9},{9,10},{10,1... | collective-permute-start | bytes 1572872 | tf_op jit(solution)/shard_map/ppermute | solution.py:14
  85.0 2.7 copy-start
  95.8 3.1 %copy-start.2 = (f32[8,128,768]{2,1,0:T(8,128)S(1)}, f32[8,128,768]{2,1,0:T(8,128)}, u32[]{:S(2)}) copy-start(f32[8,128,768]{2,1,0:T(8,128)} %get-tuple-element.99) | copy-start | bytes 9437188
  104.0 5.4 %copy-start.4 = (f32[32,24,512]{2,1,0:T(8,128)S(1)}, f32[32,24,512]{2,1,0:T(8,128)}, u32[]{:S(2)}) copy-start(f32[32,24,512]{2,1,0:T(8,128)} %reshape.312) | copy-start | bytes 4718596
  109.6 15.0 %copy-start.1 = (f32[8,16,8,768]{3,2,1,0:T(8,128)S(1)}, f32[8,16,8,768]{3,2,1,0:T(8,128)}, u32[]{:S(2)}) copy-start(f32[8,16,8,768]{3,2,1,0:T(8,128)} %get-tuple-element.86) | copy-start | bytes 9437188
  109.9 123.8 %collective-permute-start.4 = (bf16[32,8,1024]{2,1,0:T(8,128)(2,1)S(1)}, bf16[32,8,1024]{2,1,0:T(8,128)(2,1)S(1)}, u32[]{:S(2)}, u32[]{:S(2)}) collective-permute-start(bf16[32,8,1024]{2,1,0:T(8,128)(2,1)S(1)} %get-tuple-element.88), channel_id=1, source_target_pairs={{0,1},{1,2},{2,3},{3,4},{4,5},{5,6},{6,7},{7,8},{8,9},{9,10},{10,1... | collective-permute-start | bytes 1572872 | tf_op jit(solution)/shard_map/ppermute | solution.py:14
  112.0 121.7 %collective-permute-start.5 = (bf16[32,8,1024]{2,1,0:T(8,128)(2,1)S(1)}, bf16[32,8,1024]{2,1,0:T(8,128)(2,1)S(1)}, u32[]{:S(2)}, u32[]{:S(2)}) collective-permute-start(bf16[32,8,1024]{2,1,0:T(8,128)(2,1)S(1)} %get-tuple-element.89), channel_id=1, source_target_pairs={{1,0},{2,1},{3,2},{4,3},{5,4},{6,5},{7,6},{8,7},{9,8},{10,9},{11,1... | collective-permute-start | bytes 1572872 | tf_op jit(solution)/shard_map/ppermute | solution.py:15
  139.8 82.4 %copy-start.3 = (bf16[768,8,64]{0,2,1:T(8,128)(2,1)S(1)}, bf16[768,8,64]{0,2,1:T(8,128)(2,1)}, u32[]{:S(2)}) copy-start(bf16[768,8,64]{0,2,1:T(8,128)(2,1)} %copy.38) | copy-start | bytes 2359300
  150.8 3.2 %collective-permute-start.8 = (f32[8,13,13]{2,1,0:T(8,128)S(1)}, f32[8,13,13]{2,1,0:T(8,128)S(1)}, u32[]{:S(2)}, u32[]{:S(2)}) collective-permute-start(f32[8,13,13]{2,1,0:T(8,128)S(1)} %convolution_bitcast_fusion.1), channel_id=1, source_target_pairs={{0,1},{1,0},{2,3},{3,2},{4,5},{5,4},{6,7},{7,6},{8,9},{9,8},{10,11... | collective-permute-start | bytes 16232 | tf_op jit(solution)/shard_map/ppermute | solution.py:39
  154.0 6.2 %collective-permute-start.9 = (f32[8,13,13]{2,1,0:T(8,128)S(1)}, f32[8,13,13]{2,1,0:T(8,128)S(1)}, u32[]{:S(2)}, u32[]{:S(2)}) collective-permute-start(f32[8,13,13]{2,1,0:T(8,128)S(1)} %add.95), channel_id=1, source_target_pairs={{0,2},{1,3},{2,0},{3,1},{4,6},{5,7},{6,4},{7,5},{8,10},{9,11},{10,... | collective-permute-start | bytes 16232 | tf_op jit(solution)/shard_map/ppermute | solution.py:39
  160.2 7.4 %collective-permute-start.10 = (f32[8,13,13]{2,1,0:T(8,128)S(1)}, f32[8,13,13]{2,1,0:T(8,128)S(1)}, u32[]{:S(2)}, u32[]{:S(2)}) collective-permute-start(f32[8,13,13]{2,1,0:T(8,128)S(1)} %add.96), channel_id=1, source_target_pairs={{0,4},{1,5},{2,6},{3,7},{4,0},{5,1},{6,2},{7,3},{8,12},{9,13},{10,... | collective-permute-start | bytes 16232 | tf_op jit(solution)/shard_map/ppermute | solution.py:39
  167.5 11.5 %collective-permute-start.11 = (f32[8,13,13]{2,1,0:T(8,128)S(1)}, f32[8,13,13]{2,1,0:T(8,128)S(1)}, u32[]{:S(2)}, u32[]{:S(2)}) collective-permute-start(f32[8,13,13]{2,1,0:T(8,128)S(1)} %add.97), channel_id=1, source_target_pairs={{0,8},{1,9},{2,10},{3,11},{4,12},{5,13},{6,14},{7,15},{8,0},{9,1},... | collective-permute-start | bytes 16232 | tf_op jit(solution)/shard_map/ppermute | solution.py:39
  179.1 6.2 %collective-permute-start.12 = (f32[8,13,13]{2,1,0:T(8,128)S(1)}, f32[8,13,13]{2,1,0:T(8,128)S(1)}, u32[]{:S(2)}, u32[]{:S(2)}) collective-permute-start(f32[8,13,13]{2,1,0:T(8,128)S(1)} %add.98), channel_id=1, source_target_pairs={{0,16},{1,17},{2,18},{3,19},{4,20},{5,21},{6,22},{7,23},{8,24},{9,... | collective-permute-start | bytes 16232 | tf_op jit(solution)/shard_map/ppermute | solution.py:39
  185.3 7.4 %collective-permute-start.13 = (f32[8,13,13]{2,1,0:T(8,128)S(1)}, f32[8,13,13]{2,1,0:T(8,128)S(1)}, u32[]{:S(2)}, u32[]{:S(2)}) collective-permute-start(f32[8,13,13]{2,1,0:T(8,128)S(1)} %add.99), channel_id=1, source_target_pairs={{0,48},{1,49},{2,50},{3,51},{4,52},{5,53},{6,54},{7,55},{8,56},{9,... | collective-permute-start | bytes 16232 | tf_op jit(solution)/shard_map/ppermute | solution.py:39
  192.6 6.2 %collective-permute-start.14 = (f32[8,13,13]{2,1,0:T(8,128)S(1)}, f32[8,13,13]{2,1,0:T(8,128)S(1)}, u32[]{:S(2)}, u32[]{:S(2)}) collective-permute-start(f32[8,13,13]{2,1,0:T(8,128)S(1)} %add.100), channel_id=1, source_target_pairs={{0,64},{64,0},{128,192},{192,128},{256,320},{320,256},{384,448},{4... | collective-permute-start | bytes 16232 | tf_op jit(solution)/shard_map/ppermute | solution.py:39
  198.8 7.4 %collective-permute-start.15 = (f32[8,13,13]{2,1,0:T(8,128)S(1)}, f32[8,13,13]{2,1,0:T(8,128)S(1)}, u32[]{:S(2)}, u32[]{:S(2)}) collective-permute-start(f32[8,13,13]{2,1,0:T(8,128)S(1)} %add.101), channel_id=1, source_target_pairs={{0,192},{64,128},{128,64},{192,0},{256,448},{320,384},{384,320},{4... | collective-permute-start | bytes 16232 | tf_op jit(solution)/shard_map/ppermute | solution.py:39
  206.2 21.1 %collective-permute-start.16 = (f32[8,13,13]{2,1,0:T(8,128)S(1)}, f32[8,13,13]{2,1,0:T(8,128)S(1)}, u32[]{:S(2)}, u32[]{:S(2)}) collective-permute-start(f32[8,13,13]{2,1,0:T(8,128)S(1)} %add.102), channel_id=1, source_target_pairs={{0,256},{64,320},{128,384},{192,448},{256,0},{320,64},{384,128},{4... | collective-permute-start | bytes 16232 | tf_op jit(solution)/shard_map/ppermute | solution.py:39
  222.8 26.0 %copy-start.6 = (bf16[768,8,64]{0,2,1:T(8,128)(2,1)S(1)}, bf16[768,8,64]{0,2,1:T(8,128)(2,1)}, u32[]{:S(2)}) copy-start(bf16[768,8,64]{0,2,1:T(8,128)(2,1)} %copy.43) | copy-start | bytes 2359300
  227.9 27.9 %collective-permute-start.17 = (f32[8,13,13]{2,1,0:T(8,128)}, f32[8,13,13]{2,1,0:T(8,128)}, u32[]{:S(2)}, u32[]{:S(2)}) collective-permute-start(f32[8,13,13]{2,1,0:T(8,128)} %add.103), channel_id=1, source_target_pairs={{0,768},{64,832},{128,896},{192,960},{256,512},{320,576},{384,640}... | collective-permute-start | bytes 16232 | tf_op jit(solution)/shard_map/ppermute | solution.py:39
  234.0 23.4 %collective-permute-start.6 = (bf16[8,8,1024]{2,1,0:T(8,128)(2,1)S(1)}, bf16[8,8,1024]{2,1,0:T(8,128)(2,1)S(1)}, u32[]{:S(2)}, u32[]{:S(2)}) collective-permute-start(bf16[8,8,1024]{2,1,0:T(8,128)(2,1)S(1)} %get-tuple-element.92), channel_id=1, source_target_pairs={{0,64},{64,128},{128,192},{192,256},{256,320},{320,384},{384,448},... | collective-permute-start | bytes 393224 | tf_op jit(solution)/shard_map/ppermute | solution.py:14
  246.9 25.1 %collective-permute-start.7 = (bf16[8,8,1024]{2,1,0:T(8,128)(2,1)S(1)}, bf16[8,8,1024]{2,1,0:T(8,128)(2,1)S(1)}, u32[]{:S(2)}, u32[]{:S(2)}) collective-permute-start(bf16[8,8,1024]{2,1,0:T(8,128)(2,1)S(1)} %get-tuple-element.93), channel_id=1, source_target_pairs={{64,0},{128,64},{192,128},{256,192},{320,256},{384,320},{448,384},... | collective-permute-start | bytes 393224 | tf_op jit(solution)/shard_map/ppermute | solution.py:15
  (1 other events, 2.3 us)

commit v5 on v4

--- a/solution.py
+++ b/solution.py
@@ -101,14 +101,18 @@
     correction = jnp.sum(attention * dprobs, axis=-1, keepdims=True)
     dscore = attention * (dprobs - correction)
     dscore_round = dscore.astype(jnp.bfloat16)
+    grad_cells = dscore.reshape(head_count, height, breadth, keys)
+    by_col = jnp.sum(grad_cells[:, :, :, None, :] * col_hot[None, None, :, :, :], axis=2)
+    grad_table = jnp.einsum("hibk,iak->hab", by_col, row_hot, precision=exact)
+    grad_window_bias = all_sum(grad_table)
+    grad_table, dscore_round, rounded_probs = lax.optimization_barrier(
+        (grad_table, dscore_round, rounded_probs)
+    )
     grad_query = (
         jnp.einsum("hqk,khd->qhd", dscore_round, key_heads, preferred_element_type=jnp.float32)
         * score_scale
     )
     grad_queries = grad_query.astype(jnp.bfloat16).reshape(height, breadth, model_width)
-    grad_cells = dscore.reshape(head_count, height, breadth, keys)
-    by_col = jnp.sum(grad_cells[:, :, :, None, :] * col_hot[None, None, :, :, :], axis=2)
-    grad_table = jnp.einsum("hibk,iak->hab", by_col, row_hot, precision=exact)
     grad_keys = (
         jnp.einsum("hqk,qhd->khd", dscore_round, query_heads, preferred_element_type=jnp.float32)
         * score_scale
@@ -130,7 +134,6 @@
     totals = settle(folded, arrived, 0)
     grad_keys = totals[..., :model_width].astype(jnp.bfloat16)
     grad_values = totals[..., model_width:].astype(jnp.bfloat16)
-    grad_window_bias = all_sum(grad_table)
     return (attention_out, grad_queries, grad_keys, grad_values, grad_window_bias)
 
 

time: 274 us -> 295 us (1.077)
  the two profiles are of different devices: /device:TPU:6 before, /device:TPU:46 now
where the time goes in v5:
time: 295 us; the launch traced here: 294 us
  starting transfers between devices  95.8 us (32%)
  waiting for transfers between devices  85.7 us (29%)
  local copies, waits for them, and re-layouts  45.6 us (15%)
  other arithmetic  38.3 us (13%)
  matrix products  27.1 us (9%)
    ppermute x10, starting transfers between devices, exchange_sum(): return value + lax.ppermute(value, axis, pairs)  52.5 us
    ppermute x10, waiting for transfers between devices, exchange_sum(): return value + lax.ppermute(value, axis, pairs)  38.9 us
    ppermute x4, waiting for transfers between devices, padded_2(): after = lax.ppermute(leading, axis, down)  36.6 us
    ppermute x4, starting transfers between devices, padded_2(): before = lax.ppermute(last, axis, up)  33.9 us
    reduce_sum x1, other arithmetic, per_device(): jnp.sum(grad_cells[:, :, :, None, :] * col_hot[None, None, :, :, :], axis=2)  16.5 us
    dot_general x1, matrix products, per_device(): grad_table = jnp.einsum('hibk,iak->hab', by_col, row_hot, precision=exact)  11 us
    ppermute x4, waiting for transfers between devices, padded_2(): before = lax.ppermute(last, axis, up)  10.2 us
    ppermute x4, starting transfers between devices, padded_2(): after = lax.ppermute(leading, axis, down)  9.4 us
  transfers between devices with their start and end apart: 18, of which 12 were waited for; matrix products, arithmetic and copies ran while one was open for 10% of the time, Pallas kernels for 0%

profile of v5, /device:TPU:46, one launch (start us, length us, event | category | flops | bytes accessed | tf_op | source)
XLA Modules:
  0.0 293.7 jit_solution(259907215963245702)
XLA Ops:
  2.5 15.6 %collective-permute-start = (bf16[8,8,1024]{2,1,0:T(8,128)(2,1)S(1)}, bf16[8,8,1024]{2,1,0:T(8,128)(2,1)S(1)}, u32[]{:S(2)}, u32[]{:S(2)}) collective-permute-start(bf16[8,8,1024]{2,1,0:T(8,128)(2,1)S(1)} %get-tuple-element.98), channel_id=1, source_target_pairs={{0,64},{64,128},{128,192},{192,256},{256,320},{320,384},{384,448},... | collective-permute-start | bytes 393224 | tf_op jit(solution)/shard_map/ppermute | solution.py:14
  26.4 6.5 %multiply_reduce_fusion = f32[8,16,13,768]{3,1,2,0:T(8,128)S(1)} fusion(f32[16,13,768]{2,0,1:T(8,128)S(1)} %copy.41, f32[8,13,13]{2,1,0:T(8,128)S(1)} %copy.40), kind=kLoop, calls=%fused_computation.2 | loop fusion | flops 31948800 | bytes 5756192 | tf_op jit(solution)/shard_map/reduce_sum | solution.py:74
  36.6 14.7 %collective-permute-done.1 = bf16[8,8,1024]{2,1,0:T(8,128)(2,1)S(1)} collective-permute-done((bf16[8,8,1024]{2,1,0:T(8,128)(2,1)S(1)}, bf16[8,8,1024]{2,1,0:T(8,128)(2,1)S(1)}, u32[]{:S(2)}, u32[]{:S(2)}) %collective-permute-start.1) | collective-permute-done | bytes 131104 | tf_op jit(solution)/shard_map/ppermute | solution.py:15
  56.0 4.3 %multiply_reduce_fusion.2 = f32[8,16,8,768]{3,2,1,0:T(8,128)S(1)} fusion(f32[8,13,768]{2,0,1:T(8,128)S(1)} %fusion.13, f32[8,16,13,768]{3,2,1,0:T(8,128)S(1)} %copy.42), kind=kLoop, calls=%fused_computation.4 | loop fusion | flops 19660800 | bytes 8577024 | tf_op jit(solution)/shard_map/reduce_sum | solution.py:75
  60.3 10.2 %collective-permute-done.2 = bf16[32,8,1024]{2,1,0:T(8,128)(2,1)S(1)} collective-permute-done((bf16[32,8,1024]{2,1,0:T(8,128)(2,1)S(1)}, bf16[32,8,1024]{2,1,0:T(8,128)(2,1)S(1)}, u32[]{:S(2)}, u32[]{:S(2)}) %collective-permute-start.2) | collective-permute-done | bytes 524320 | tf_op jit(solution)/shard_map/ppermute | solution.py:14
  83.8 4.1 %fusion.34 = (f32[8,128]{1,0:T(8,128)S(1)}, f32[8,128,768]{2,1,0:T(8,128)}) fusion(f32[8,16,8,768]{3,2,1,0:T(8,128)S(1)} %multiply_reduce_fusion.2, bf16[768,8,64]{0,2,1:T(8,128)(2,1)} %copy.38, bf16[128,8,64]{0,2,1:T(8,128)(2,1)S(1)} %copy.39, pred[128,768]{1,0:T(8,128)(4,1)S(1)} %copy-done.13), kind=kOutput, calls=%fused_computation.74 | convolution fusion | flops 104596224 | bytes 7311360 | tf_op jit(solution)/shard_map/sub | solution.py:92
  90.0 7.6 %fusion.35 = (bf16[8,128,768]{2,1,0:T(8,128)(2,1)S(1)}, f32[8,128,768]{2,1,0:T(8,128)}) fusion(bf16[768,8,64]{0,2,1:T(8,128)(2,1)} %copy.43, bf16[128,8,64]{0,2,1:T(8,128)(2,1)} %copy.46, f32[8,128,768]{2,1,0:T(8,128)} %get-tuple-element.101, f32[8,128]{1,0:T(8,128)S(1)} %get-tuple-element.100), kind=kOutput, calls=%fused_computation.75 | convolution fusion | flops 206046976 | bytes 8785920 | tf_op jit(solution)/shard_map/sub | solution.py:102
  97.6 16.5 %multiply_reduce_fusion.1 = f32[8,16,13,768]{3,2,1,0:T(8,128)S(1)} fusion(f32[8,16,8,768]{3,2,1,0:T(8,128)} %bitcast.54, f32[8,13,768]{2,0,1:T(8,128)S(1)} %copy-done.3), kind=kLoop, calls=%fused_computation.3 | loop fusion | flops 19169280 | bytes 8577024 | tf_op jit(solution)/shard_map/reduce_sum | solution.py:105
  114.1 11.0 %convolution_bitcast_fusion.1 = f32[8,13,13]{2,1,0:T(8,128)S(1)} fusion(f32[8,16,13,768]{3,2,1,0:T(8,128)S(1)} %multiply_reduce_fusion.1, s32[16,768]{1,0:T(8,128)S(1)} %copy-done.12), kind=kOutput, calls=%fused_computation.21 | convolution fusion | flops 199520256 | bytes 5166368 | tf_op jit(solution)/shard_map/hibk,iak->hab/dot_general | solution.py:106
  131.5 3.8 %reshape.311 = f32[32,24,512]{2,1,0:T(8,128)} reshape(f32[768,8,64]{2,1,0:T(8,128)} %copy.50) | data formatting | bytes 3145728 | tf_op jit(solution)/shard_map/reshape | solution.py:124
  141.3 3.7 %reshape.312 = f32[32,24,512]{2,1,0:T(8,128)} reshape(f32[768,8,64]{2,1,0:T(8,128)} %copy.52) | data formatting | bytes 3145728 | tf_op jit(solution)/shard_map/reshape | solution.py:124
  151.9 3.6 %collective-permute-start.5 = (bf16[32,8,1024]{2,1,0:T(8,128)(2,1)S(1)}, bf16[32,8,1024]{2,1,0:T(8,128)(2,1)S(1)}, u32[]{:S(2)}, u32[]{:S(2)}) collective-permute-start(bf16[32,8,1024]{2,1,0:T(8,128)(2,1)S(1)} %get-tuple-element.91), channel_id=1, source_target_pairs={{1,0},{2,1},{3,2},{4,3},{5,4},{6,5},{7,6},{8,7},{9,8},{10,9},{11,1... | collective-permute-start | bytes 1572872 | tf_op jit(solution)/shard_map/ppermute | solution.py:15
  158.7 14.6 %collective-permute-start.9 = (f32[8,13,13]{2,1,0:T(8,128)S(1)}, f32[8,13,13]{2,1,0:T(8,128)S(1)}, u32[]{:S(2)}, u32[]{:S(2)}) collective-permute-start(f32[8,13,13]{2,1,0:T(8,128)S(1)} %add.95), channel_id=1, source_target_pairs={{0,2},{1,3},{2,0},{3,1},{4,6},{5,7},{6,4},{7,5},{8,10},{9,11},{10,... | collective-permute-start | bytes 16232 | tf_op jit(solution)/shard_map/ppermute | solution.py:39
  178.8 5.2 %collective-permute-done.10 = f32[8,13,13]{2,1,0:T(8,128)S(1)} collective-permute-done((f32[8,13,13]{2,1,0:T(8,128)S(1)}, f32[8,13,13]{2,1,0:T(8,128)S(1)}, u32[]{:S(2)}, u32[]{:S(2)}) %collective-permute-start.10) | collective-permute-done | bytes 5440 | tf_op jit(solution)/shard_map/ppermute | solution.py:39
  185.9 8.8 %collective-permute-done.11 = f32[8,13,13]{2,1,0:T(8,128)S(1)} collective-permute-done((f32[8,13,13]{2,1,0:T(8,128)S(1)}, f32[8,13,13]{2,1,0:T(8,128)S(1)}, u32[]{:S(2)}, u32[]{:S(2)}) %collective-permute-start.11) | collective-permute-done | bytes 5440 | tf_op jit(solution)/shard_map/ppermute | solution.py:39
  194.7 4.8 %collective-permute-start.12 = (f32[8,13,13]{2,1,0:T(8,128)S(1)}, f32[8,13,13]{2,1,0:T(8,128)S(1)}, u32[]{:S(2)}, u32[]{:S(2)}) collective-permute-start(f32[8,13,13]{2,1,0:T(8,128)S(1)} %add.98), channel_id=1, source_target_pairs={{0,16},{1,17},{2,18},{3,19},{4,20},{5,21},{6,22},{7,23},{8,24},{9,... | collective-permute-start | bytes 16232 | tf_op jit(solution)/shard_map/ppermute | solution.py:39
  204.4 3.5 %collective-permute-done.13 = f32[8,13,13]{2,1,0:T(8,128)S(1)} collective-permute-done((f32[8,13,13]{2,1,0:T(8,128)S(1)}, f32[8,13,13]{2,1,0:T(8,128)S(1)}, u32[]{:S(2)}, u32[]{:S(2)}) %collective-permute-start.13) | collective-permute-done | bytes 5440 | tf_op jit(solution)/shard_map/ppermute | solution.py:39
  209.9 4.2 %collective-permute-done.14 = f32[8,13,13]{2,1,0:T(8,128)S(1)} collective-permute-done((f32[8,13,13]{2,1,0:T(8,128)S(1)}, f32[8,13,13]{2,1,0:T(8,128)S(1)}, u32[]{:S(2)}, u32[]{:S(2)}) %collective-permute-start.14) | collective-permute-done | bytes 5440 | tf_op jit(solution)/shard_map/ppermute | solution.py:39
  216.0 5.4 %collective-permute-done.15 = f32[8,13,13]{2,1,0:T(8,128)S(1)} collective-permute-done((f32[8,13,13]{2,1,0:T(8,128)S(1)}, f32[8,13,13]{2,1,0:T(8,128)S(1)}, u32[]{:S(2)}, u32[]{:S(2)}) %collective-permute-start.15) | collective-permute-done | bytes 5440 | tf_op jit(solution)/shard_map/ppermute | solution.py:39
  221.5 15.9 %collective-permute-start.16 = (f32[8,13,13]{2,1,0:T(8,128)S(1)}, f32[8,13,13]{2,1,0:T(8,128)S(1)}, u32[]{:S(2)}, u32[]{:S(2)}) collective-permute-start(f32[8,13,13]{2,1,0:T(8,128)S(1)} %add.102), channel_id=1, source_target_pairs={{0,256},{64,320},{128,384},{192,448},{256,0},{320,64},{384,128},{4... | collective-permute-start | bytes 16232 | tf_op jit(solution)/shard_map/ppermute | solution.py:39
  238.1 4.8 %collective-permute-done.16 = f32[8,13,13]{2,1,0:T(8,128)S(1)} collective-permute-done((f32[8,13,13]{2,1,0:T(8,128)S(1)}, f32[8,13,13]{2,1,0:T(8,128)S(1)}, u32[]{:S(2)}, u32[]{:S(2)}) %collective-permute-start.16) | collective-permute-done | bytes 5440 | tf_op jit(solution)/shard_map/ppermute | solution.py:39
  243.6 4.9 %collective-permute-start.17 = (f32[8,13,13]{2,1,0:T(8,128)}, f32[8,13,13]{2,1,0:T(8,128)}, u32[]{:S(2)}, u32[]{:S(2)}) collective-permute-start(f32[8,13,13]{2,1,0:T(8,128)} %add.103), channel_id=1, source_target_pairs={{0,768},{64,832},{128,896},{192,960},{256,512},{320,576},{384,640}... | collective-permute-start | bytes 16232 | tf_op jit(solution)/shard_map/ppermute | solution.py:39
  250.1 13.7 %collective-permute-start.6 = (bf16[8,8,1024]{2,1,0:T(8,128)(2,1)S(1)}, bf16[8,8,1024]{2,1,0:T(8,128)(2,1)S(1)}, u32[]{:S(2)}, u32[]{:S(2)}) collective-permute-start(bf16[8,8,1024]{2,1,0:T(8,128)(2,1)S(1)} %get-tuple-element.94), channel_id=1, source_target_pairs={{0,64},{64,128},{128,192},{192,256},{256,320},{320,384},{384,448},... | collective-permute-start | bytes 393224 | tf_op jit(solution)/shard_map/ppermute | solution.py:14
  270.1 21.8 %collective-permute-done.7 = bf16[8,8,1024]{2,1,0:T(8,128)(2,1)} collective-permute-done((bf16[8,8,1024]{2,1,0:T(8,128)(2,1)S(1)}, bf16[8,8,1024]{2,1,0:T(8,128)(2,1)}, u32[]{:S(2)}, u32[]{:S(2)}) %collective-permute-start.7) | collective-permute-done | bytes 131104 | tf_op jit(solution)/shard_map/ppermute | solution.py:15
  (109 shorter events, 83.1 us)
Async XLA Ops:
  2.5 34.1 %collective-permute-start = (bf16[8,8,1024]{2,1,0:T(8,128)(2,1)S(1)}, bf16[8,8,1024]{2,1,0:T(8,128)(2,1)S(1)}, u32[]{:S(2)}, u32[]{:S(2)}) collective-permute-start(bf16[8,8,1024]{2,1,0:T(8,128)(2,1)S(1)} %get-tuple-element.98), channel_id=1, source_target_pairs={{0,64},{64,128},{128,192},{192,256},{256,320},{320,384},{384,448},... | collective-permute-start | bytes 393224 | tf_op jit(solution)/shard_map/ppermute | solution.py:14
  18.1 33.2 %collective-permute-start.1 = (bf16[8,8,1024]{2,1,0:T(8,128)(2,1)S(1)}, bf16[8,8,1024]{2,1,0:T(8,128)(2,1)S(1)}, u32[]{:S(2)}, u32[]{:S(2)}) collective-permute-start(bf16[8,8,1024]{2,1,0:T(8,128)(2,1)S(1)} %get-tuple-element.99), channel_id=1, source_target_pairs={{64,0},{128,64},{192,128},{256,192},{320,256},{384,320},{448,384},... | collective-permute-start | bytes 393224 | tf_op jit(solution)/shard_map/ppermute | solution.py:15
  23.9 59.9 %copy-start.4 = (bf16[128,8,64]{0,2,1:T(8,128)(2,1)}, bf16[128,8,64]{0,2,1:T(8,128)(2,1)S(1)}, u32[]{:S(2)}) copy-start(bf16[128,8,64]{0,2,1:T(8,128)(2,1)S(1)} %copy.39) | copy-start | bytes 393220
  25.9 30.0 %copy-start.2 = (f32[8,13,768]{2,0,1:T(8,128)}, f32[8,13,768]{2,0,1:T(8,128)S(1)}, u32[]{:S(2)}) copy-start(f32[8,13,768]{2,0,1:T(8,128)S(1)} %fusion.13) | copy-start | bytes 958468
  36.6 16.7 %copy-start.7 = (bf16[8,8,1024]{2,1,0:T(8,128)(2,1)}, bf16[8,8,1024]{2,1,0:T(8,128)(2,1)S(1)}, u32[]{:S(2)}) copy-start(bf16[8,8,1024]{2,1,0:T(8,128)(2,1)S(1)} %collective-permute-done) | copy-start | bytes 393220
  51.4 8.8 %collective-permute-start.3 = (bf16[32,8,1024]{2,1,0:T(8,128)(2,1)S(1)}, bf16[32,8,1024]{2,1,0:T(8,128)(2,1)S(1)}, u32[]{:S(2)}, u32[]{:S(2)}) collective-permute-start(bf16[32,8,1024]{2,1,0:T(8,128)(2,1)S(1)} %pad_maximum_fusion.4), channel_id=1, source_target_pairs={{1,0},{2,1},{3,2},{4,3},{5,4},{6,5},{7,6},{8,7},{9,8},{10,9},{11,1... | collective-permute-start | bytes 1572872 | tf_op jit(solution)/shard_map/ppermute | solution.py:15
  53.4 17.1 %collective-permute-start.2 = (bf16[32,8,1024]{2,1,0:T(8,128)(2,1)S(1)}, bf16[32,8,1024]{2,1,0:T(8,128)(2,1)S(1)}, u32[]{:S(2)}, u32[]{:S(2)}) collective-permute-start(bf16[32,8,1024]{2,1,0:T(8,128)(2,1)S(1)} %pad_maximum_fusion.4), channel_id=1, source_target_pairs={{0,1},{1,2},{2,3},{3,4},{4,5},{5,6},{6,7},{7,8},{8,9},{9,10},{10,1... | collective-permute-start | bytes 1572872 | tf_op jit(solution)/shard_map/ppermute | solution.py:14
  97.6 16.5 %copy-start.12 = (s32[16,768]{1,0:T(8,128)S(1)}, s32[16,768]{1,0:T(8,128)}, u32[]{:S(2)}) copy-start(s32[16,768]{1,0:T(8,128)} %copy-done.11) | copy-start | bytes 147460
  147.7 89.7 %copy-start.1 = (bf16[768,8,64]{0,2,1:T(8,128)(2,1)S(1)}, bf16[768,8,64]{0,2,1:T(8,128)(2,1)}, u32[]{:S(2)}) copy-start(bf16[768,8,64]{0,2,1:T(8,128)(2,1)} %copy.43) | copy-start | bytes 2359300
  150.0 98.5 %collective-permute-start.4 = (bf16[32,8,1024]{2,1,0:T(8,128)(2,1)S(1)}, bf16[32,8,1024]{2,1,0:T(8,128)(2,1)S(1)}, u32[]{:S(2)}, u32[]{:S(2)}) collective-permute-start(bf16[32,8,1024]{2,1,0:T(8,128)(2,1)S(1)} %get-tuple-element.90), channel_id=1, source_target_pairs={{0,1},{1,2},{2,3},{3,4},{4,5},{5,6},{6,7},{7,8},{8,9},{9,10},{10,1... | collective-permute-start | bytes 1572872 | tf_op jit(solution)/shard_map/ppermute | solution.py:14
  151.9 96.6 %collective-permute-start.5 = (bf16[32,8,1024]{2,1,0:T(8,128)(2,1)S(1)}, bf16[32,8,1024]{2,1,0:T(8,128)(2,1)S(1)}, u32[]{:S(2)}, u32[]{:S(2)}) collective-permute-start(bf16[32,8,1024]{2,1,0:T(8,128)(2,1)S(1)} %get-tuple-element.91), channel_id=1, source_target_pairs={{1,0},{2,1},{3,2},{4,3},{5,4},{6,5},{7,6},{8,7},{9,8},{10,9},{11,1... | collective-permute-start | bytes 1572872 | tf_op jit(solution)/shard_map/ppermute | solution.py:15
  155.6 3.1 %collective-permute-start.8 = (f32[8,13,13]{2,1,0:T(8,128)S(1)}, f32[8,13,13]{2,1,0:T(8,128)S(1)}, u32[]{:S(2)}, u32[]{:S(2)}) collective-permute-start(f32[8,13,13]{2,1,0:T(8,128)S(1)} %convolution_bitcast_fusion.1), channel_id=1, source_target_pairs={{0,1},{1,0},{2,3},{3,2},{4,5},{5,4},{6,7},{7,6},{8,9},{9,8},{10,11... | collective-permute-start | bytes 16232 | tf_op jit(solution)/shard_map/ppermute | solution.py:39
  158.7 18.1 %collective-permute-start.9 = (f32[8,13,13]{2,1,0:T(8,128)S(1)}, f32[8,13,13]{2,1,0:T(8,128)S(1)}, u32[]{:S(2)}, u32[]{:S(2)}) collective-permute-start(f32[8,13,13]{2,1,0:T(8,128)S(1)} %add.95), channel_id=1, source_target_pairs={{0,2},{1,3},{2,0},{3,1},{4,6},{5,7},{6,4},{7,5},{8,10},{9,11},{10,... | collective-permute-start | bytes 16232 | tf_op jit(solution)/shard_map/ppermute | solution.py:39
  176.9 7.1 %collective-permute-start.10 = (f32[8,13,13]{2,1,0:T(8,128)S(1)}, f32[8,13,13]{2,1,0:T(8,128)S(1)}, u32[]{:S(2)}, u32[]{:S(2)}) collective-permute-start(f32[8,13,13]{2,1,0:T(8,128)S(1)} %add.96), channel_id=1, source_target_pairs={{0,4},{1,5},{2,6},{3,7},{4,0},{5,1},{6,2},{7,3},{8,12},{9,13},{10,... | collective-permute-start | bytes 16232 | tf_op jit(solution)/shard_map/ppermute | solution.py:39
  183.9 10.8 %collective-permute-start.11 = (f32[8,13,13]{2,1,0:T(8,128)S(1)}, f32[8,13,13]{2,1,0:T(8,128)S(1)}, u32[]{:S(2)}, u32[]{:S(2)}) collective-permute-start(f32[8,13,13]{2,1,0:T(8,128)S(1)} %add.97), channel_id=1, source_target_pairs={{0,8},{1,9},{2,10},{3,11},{4,12},{5,13},{6,14},{7,15},{8,0},{9,1},... | collective-permute-start | bytes 16232 | tf_op jit(solution)/shard_map/ppermute | solution.py:39
  194.7 7.0 %collective-permute-start.12 = (f32[8,13,13]{2,1,0:T(8,128)S(1)}, f32[8,13,13]{2,1,0:T(8,128)S(1)}, u32[]{:S(2)}, u32[]{:S(2)}) collective-permute-start(f32[8,13,13]{2,1,0:T(8,128)S(1)} %add.98), channel_id=1, source_target_pairs={{0,16},{1,17},{2,18},{3,19},{4,20},{5,21},{6,22},{7,23},{8,24},{9,... | collective-permute-start | bytes 16232 | tf_op jit(solution)/shard_map/ppermute | solution.py:39
  201.8 6.2 %collective-permute-start.13 = (f32[8,13,13]{2,1,0:T(8,128)S(1)}, f32[8,13,13]{2,1,0:T(8,128)S(1)}, u32[]{:S(2)}, u32[]{:S(2)}) collective-permute-start(f32[8,13,13]{2,1,0:T(8,128)S(1)} %add.99), channel_id=1, source_target_pairs={{0,48},{1,49},{2,50},{3,51},{4,52},{5,53},{6,54},{7,55},{8,56},{9,... | collective-permute-start | bytes 16232 | tf_op jit(solution)/shard_map/ppermute | solution.py:39
  207.9 6.2 %collective-permute-start.14 = (f32[8,13,13]{2,1,0:T(8,128)S(1)}, f32[8,13,13]{2,1,0:T(8,128)S(1)}, u32[]{:S(2)}, u32[]{:S(2)}) collective-permute-start(f32[8,13,13]{2,1,0:T(8,128)S(1)} %add.100), channel_id=1, source_target_pairs={{0,64},{64,0},{128,192},{192,128},{256,320},{320,256},{384,448},{4... | collective-permute-start | bytes 16232 | tf_op jit(solution)/shard_map/ppermute | solution.py:39
  214.1 7.4 %collective-permute-start.15 = (f32[8,13,13]{2,1,0:T(8,128)S(1)}, f32[8,13,13]{2,1,0:T(8,128)S(1)}, u32[]{:S(2)}, u32[]{:S(2)}) collective-permute-start(f32[8,13,13]{2,1,0:T(8,128)S(1)} %add.101), channel_id=1, source_target_pairs={{0,192},{64,128},{128,64},{192,0},{256,448},{320,384},{384,320},{4... | collective-permute-start | bytes 16232 | tf_op jit(solution)/shard_map/ppermute | solution.py:39
  221.5 21.4 %collective-permute-start.16 = (f32[8,13,13]{2,1,0:T(8,128)S(1)}, f32[8,13,13]{2,1,0:T(8,128)S(1)}, u32[]{:S(2)}, u32[]{:S(2)}) collective-permute-start(f32[8,13,13]{2,1,0:T(8,128)S(1)} %add.102), channel_id=1, source_target_pairs={{0,256},{64,320},{128,384},{192,448},{256,0},{320,64},{384,128},{4... | collective-permute-start | bytes 16232 | tf_op jit(solution)/shard_map/ppermute | solution.py:39
  238.1 27.6 %copy-start = (bf16[768,8,64]{0,2,1:T(8,128)(2,1)S(1)}, bf16[768,8,64]{0,2,1:T(8,128)(2,1)}, u32[]{:S(2)}) copy-start(bf16[768,8,64]{0,2,1:T(8,128)(2,1)} %copy.38) | copy-start | bytes 2359300
  243.6 24.9 %collective-permute-start.17 = (f32[8,13,13]{2,1,0:T(8,128)}, f32[8,13,13]{2,1,0:T(8,128)}, u32[]{:S(2)}, u32[]{:S(2)}) collective-permute-start(f32[8,13,13]{2,1,0:T(8,128)} %add.103), channel_id=1, source_target_pairs={{0,768},{64,832},{128,896},{192,960},{256,512},{320,576},{384,640}... | collective-permute-start | bytes 16232 | tf_op jit(solution)/shard_map/ppermute | solution.py:39
  250.1 20.0 %collective-permute-start.6 = (bf16[8,8,1024]{2,1,0:T(8,128)(2,1)S(1)}, bf16[8,8,1024]{2,1,0:T(8,128)(2,1)S(1)}, u32[]{:S(2)}, u32[]{:S(2)}) collective-permute-start(bf16[8,8,1024]{2,1,0:T(8,128)(2,1)S(1)} %get-tuple-element.94), channel_id=1, source_target_pairs={{0,64},{64,128},{128,192},{192,256},{256,320},{320,384},{384,448},... | collective-permute-start | bytes 393224 | tf_op jit(solution)/shard_map/ppermute | solution.py:14
  263.8 28.1 %collective-permute-start.7 = (bf16[8,8,1024]{2,1,0:T(8,128)(2,1)S(1)}, bf16[8,8,1024]{2,1,0:T(8,128)(2,1)}, u32[]{:S(2)}, u32[]{:S(2)}) collective-permute-start(bf16[8,8,1024]{2,1,0:T(8,128)(2,1)S(1)} %get-tuple-element.95), channel_id=1, source_target_pairs={{64,0},{128,64},{192,128},{256,192},{320,256},{384,320},{448,384},... | collective-permute-start | bytes 393224 | tf_op jit(solution)/shard_map/ppermute | solution.py:15
  (8 other events, 71.1 us)

commit v6 on v4

--- a/solution.py
+++ b/solution.py
@@ -108,7 +108,9 @@
     grad_queries = grad_query.astype(jnp.bfloat16).reshape(height, breadth, model_width)
     grad_cells = dscore.reshape(head_count, height, breadth, keys)
     by_col = jnp.sum(grad_cells[:, :, :, None, :] * col_hot[None, None, :, :, :], axis=2)
-    grad_table = jnp.einsum("hibk,iak->hab", by_col, row_hot, precision=exact)
+    grad_table = jnp.einsum(
+        "hibk,iak->hab", by_col, row_hot, precision=lax.Precision.HIGH
+    )
     grad_keys = (
         jnp.einsum("hqk,qhd->khd", dscore_round, query_heads, preferred_element_type=jnp.float32)
         * score_scale

time: 274 us -> 270 us (0.985)
  matrix products: 26.9 us -> 23.3 us
    dot_general x1, matrix products: 11 us -> 7.39 us  [per_device(): jnp.einsum('hibk,iak->hab', by_col, row_hot, precision=lax.Precision.HIGH)]
  transfers between devices with their start and end apart: 18 -> 18, of which waited for: 13 -> 13; matrix products, arithmetic and copies ran while one was open for 22% -> 21% of each run, Pallas kernels for 0% -> 0%
where the time goes in v6:
time: 270 us; the launch traced here: 269 us
  starting transfers between devices  89.2 us (33%)
  waiting for transfers between devices  87.4 us (32%)
  other arithmetic  37.3 us (14%)
  local copies, waits for them, and re-layouts  30.9 us (11%)
  matrix products  23.3 us (9%)
    ppermute x10, waiting for transfers between devices, exchange_sum(): return value + lax.ppermute(value, axis, pairs)  43.7 us
    ppermute x10, starting transfers between devices, exchange_sum(): return value + lax.ppermute(value, axis, pairs)  37.7 us
    ppermute x4, waiting for transfers between devices, padded_2(): after = lax.ppermute(leading, axis, down)  35.1 us
    ppermute x4, starting transfers between devices, padded_2(): before = lax.ppermute(last, axis, up)  33.2 us
    ppermute x4, starting transfers between devices, padded_2(): after = lax.ppermute(leading, axis, down)  18.3 us
    reduce_sum x1, other arithmetic, per_device(): jnp.sum(grad_cells[:, :, :, None, :] * col_hot[None, None, :, :, :], axis=2)  15.2 us
    ppermute x4, waiting for transfers between devices, padded_2(): before = lax.ppermute(last, axis, up)  8.64 us
    dot_general x1, matrix products, per_device(): jnp.einsum('hibk,iak->hab', by_col, row_hot, precision=lax.Precision.HIGH)  7.39 us
  transfers between devices with their start and end apart: 18, of which 13 were waited for; matrix products, arithmetic and copies ran while one was open for 21% of the time, Pallas kernels for 0%

profile of v6, /device:TPU:6, one launch (start us, length us, event | category | flops | bytes accessed | tf_op | source)
XLA Modules:
  0.0 269.2 jit_solution(13597186658176448224)
XLA Ops:
  2.5 15.6 %collective-permute-start = (bf16[8,8,1024]{2,1,0:T(8,128)(2,1)S(1)}, bf16[8,8,1024]{2,1,0:T(8,128)(2,1)S(1)}, u32[]{:S(2)}, u32[]{:S(2)}) collective-permute-start(bf16[8,8,1024]{2,1,0:T(8,128)(2,1)S(1)} %get-tuple-element.96), channel_id=1, source_target_pairs={{0,64},{64,128},{128,192},{192,256},{256,320},{320,384},{384,448},... | collective-permute-start | bytes 393224 | tf_op jit(solution)/shard_map/ppermute | solution.py:14
  27.0 6.5 %multiply_reduce_fusion = f32[8,16,13,768]{3,1,2,0:T(8,128)S(1)} fusion(f32[16,13,768]{2,0,1:T(8,128)S(1)} %copy.41, f32[8,13,13]{2,1,0:T(8,128)S(1)} %copy.40), kind=kLoop, calls=%fused_computation.1 | loop fusion | flops 31948800 | bytes 5756192 | tf_op jit(solution)/shard_map/reduce_sum | solution.py:74
  37.1 18.4 %collective-permute-done.1 = bf16[8,8,1024]{2,1,0:T(8,128)(2,1)S(1)} collective-permute-done((bf16[8,8,1024]{2,1,0:T(8,128)(2,1)S(1)}, bf16[8,8,1024]{2,1,0:T(8,128)(2,1)S(1)}, u32[]{:S(2)}, u32[]{:S(2)}) %collective-permute-start.1) | collective-permute-done | bytes 131104 | tf_op jit(solution)/shard_map/ppermute | solution.py:15
  60.2 5.9 %multiply_reduce_fusion.2 = f32[8,16,8,768]{3,2,1,0:T(8,128)} fusion(f32[8,13,768]{2,0,1:T(8,128)S(1)} %fusion.16, f32[8,16,13,768]{3,2,1,0:T(8,128)S(1)} %copy.42), kind=kLoop, calls=%fused_computation.3 | loop fusion | flops 19660800 | bytes 8577024 | tf_op jit(solution)/shard_map/reduce_sum | solution.py:75
  68.1 8.6 %collective-permute-done.2 = bf16[32,8,1024]{2,1,0:T(8,128)(2,1)S(1)} collective-permute-done((bf16[32,8,1024]{2,1,0:T(8,128)(2,1)S(1)}, bf16[32,8,1024]{2,1,0:T(8,128)(2,1)S(1)}, u32[]{:S(2)}, u32[]{:S(2)}) %collective-permute-start.2) | collective-permute-done | bytes 524320 | tf_op jit(solution)/shard_map/ppermute | solution.py:14
  87.7 4.1 %convolution_bitcast_fusion = f32[768,8,64]{0,2,1:T(8,128)} fusion(bf16[128,8,64]{0,2,1:T(8,128)(2,1)} %copy.46, f32[8,128]{1,0:T(8,128)S(1)} %get-tuple-element.98, f32[8,128,768]{2,1,0:T(8,128)S(1)} %fusion.3), kind=kOutput, calls=%fused_computation.14 | convolution fusion | flops 103024384 | bytes 4853760 | tf_op jit(solution)/shard_map/hqk,qhd->khd/dot_general | solution.py:118
  95.8 3.1 %fusion.1 = (f32[8,128]{1,0:T(8,128)S(1)}, f32[8,768,128]{1,2,0:T(8,128)S(1)}) fusion(f32[8,128,768]{2,1,0:T(8,128)} %get-tuple-element.99, f32[8,128]{1,0:T(8,128)S(1)} %get-tuple-element.98, bf16[768,8,64]{0,2,1:T(8,128)(2,1)} %copy.43, bf16[128,8,64]{0,2,1:T(8,128)(2,1)} %copy.46), kind=kOutput, calls=%fused_computation.6 | convolution fusion | flops 103021568 | bytes 7217152 | tf_op jit(solution)/shard_map/qhd,khd->hqk/dot_general | solution.py:100
  104.0 3.9 %reshape.311 = f32[32,24,512]{2,1,0:T(8,128)} reshape(f32[768,8,64]{2,1,0:T(8,128)} %copy.50) | data formatting | bytes 3145728 | tf_op jit(solution)/shard_map/reshape | solution.py:122
  112.0 12.6 %collective-permute-start.5 = (bf16[32,8,1024]{2,1,0:T(8,128)(2,1)S(1)}, bf16[32,8,1024]{2,1,0:T(8,128)(2,1)S(1)}, u32[]{:S(2)}, u32[]{:S(2)}) collective-permute-start(bf16[32,8,1024]{2,1,0:T(8,128)(2,1)S(1)} %get-tuple-element.89), channel_id=1, source_target_pairs={{1,0},{2,1},{3,2},{4,3},{5,4},{6,5},{7,6},{8,7},{9,8},{10,9},{11,1... | collective-permute-start | bytes 1572872 | tf_op jit(solution)/shard_map/ppermute | solution.py:15
  124.6 15.2 %multiply_reduce_fusion.1 = f32[8,16,13,768]{3,2,1,0:T(8,128)S(1)} fusion(f32[8,16,8,768]{3,2,1,0:T(8,128)S(1)} %copy-done.1, f32[8,13,768]{2,0,1:T(8,128)S(1)} %fusion.16), kind=kLoop, calls=%fused_computation.2 | loop fusion | flops 19169280 | bytes 8577024 | tf_op jit(solution)/shard_map/reduce_sum | solution.py:110
  139.8 7.4 %convolution_bitcast_fusion.1 = f32[8,13,13]{2,1,0:T(8,128)S(1)} fusion(f32[8,16,13,768]{3,2,1,0:T(8,128)S(1)} %multiply_reduce_fusion.1, s32[16,768]{1,0:T(8,128)S(1)} %broadcast_subtract_fusion), kind=kOutput, calls=%fused_computation.22 | convolution fusion | flops 99840000 | bytes 5166368 | tf_op jit(solution)/shard_map/hibk,iak->hab/dot_general | solution.py:111
  152.3 4.2 %collective-permute-done.9 = f32[8,13,13]{2,1,0:T(8,128)S(1)} collective-permute-done((f32[8,13,13]{2,1,0:T(8,128)S(1)}, f32[8,13,13]{2,1,0:T(8,128)S(1)}, u32[]{:S(2)}, u32[]{:S(2)}) %collective-permute-start.9) | collective-permute-done | bytes 5440 | tf_op jit(solution)/shard_map/ppermute | solution.py:39
  158.4 5.5 %collective-permute-done.10 = f32[8,13,13]{2,1,0:T(8,128)S(1)} collective-permute-done((f32[8,13,13]{2,1,0:T(8,128)S(1)}, f32[8,13,13]{2,1,0:T(8,128)S(1)}, u32[]{:S(2)}, u32[]{:S(2)}) %collective-permute-start.10) | collective-permute-done | bytes 5440 | tf_op jit(solution)/shard_map/ppermute | solution.py:39
  165.8 9.6 %collective-permute-done.11 = f32[8,13,13]{2,1,0:T(8,128)S(1)} collective-permute-done((f32[8,13,13]{2,1,0:T(8,128)S(1)}, f32[8,13,13]{2,1,0:T(8,128)S(1)}, u32[]{:S(2)}, u32[]{:S(2)}) %collective-permute-start.11) | collective-permute-done | bytes 5440 | tf_op jit(solution)/shard_map/ppermute | solution.py:39
  177.4 4.2 %collective-permute-done.12 = f32[8,13,13]{2,1,0:T(8,128)S(1)} collective-permute-done((f32[8,13,13]{2,1,0:T(8,128)S(1)}, f32[8,13,13]{2,1,0:T(8,128)S(1)}, u32[]{:S(2)}, u32[]{:S(2)}) %collective-permute-start.12) | collective-permute-done | bytes 5440 | tf_op jit(solution)/shard_map/ppermute | solution.py:39
  184.1 4.9 %collective-permute-done.13 = f32[8,13,13]{2,1,0:T(8,128)S(1)} collective-permute-done((f32[8,13,13]{2,1,0:T(8,128)S(1)}, f32[8,13,13]{2,1,0:T(8,128)S(1)}, u32[]{:S(2)}, u32[]{:S(2)}) %collective-permute-start.13) | collective-permute-done | bytes 5440 | tf_op jit(solution)/shard_map/ppermute | solution.py:39
  190.9 4.2 %collective-permute-done.14 = f32[8,13,13]{2,1,0:T(8,128)S(1)} collective-permute-done((f32[8,13,13]{2,1,0:T(8,128)S(1)}, f32[8,13,13]{2,1,0:T(8,128)S(1)}, u32[]{:S(2)}, u32[]{:S(2)}) %collective-permute-start.14) | collective-permute-done | bytes 5440 | tf_op jit(solution)/shard_map/ppermute | solution.py:39
  197.1 5.4 %collective-permute-done.15 = f32[8,13,13]{2,1,0:T(8,128)S(1)} collective-permute-done((f32[8,13,13]{2,1,0:T(8,128)S(1)}, f32[8,13,13]{2,1,0:T(8,128)S(1)}, u32[]{:S(2)}, u32[]{:S(2)}) %collective-permute-start.15) | collective-permute-done | bytes 5440 | tf_op jit(solution)/shard_map/ppermute | solution.py:39
  202.6 15.9 %collective-permute-start.16 = (f32[8,13,13]{2,1,0:T(8,128)S(1)}, f32[8,13,13]{2,1,0:T(8,128)S(1)}, u32[]{:S(2)}, u32[]{:S(2)}) collective-permute-start(f32[8,13,13]{2,1,0:T(8,128)S(1)} %add.102), channel_id=1, source_target_pairs={{0,256},{64,320},{128,384},{192,448},{256,0},{320,64},{384,128},{4... | collective-permute-start | bytes 16232 | tf_op jit(solution)/shard_map/ppermute | solution.py:39
  219.2 4.4 %collective-permute-done.16 = f32[8,13,13]{2,1,0:T(8,128)S(1)} collective-permute-done((f32[8,13,13]{2,1,0:T(8,128)S(1)}, f32[8,13,13]{2,1,0:T(8,128)S(1)}, u32[]{:S(2)}, u32[]{:S(2)}) %collective-permute-start.16) | collective-permute-done | bytes 5440 | tf_op jit(solution)/shard_map/ppermute | solution.py:39
  224.2 5.8 %collective-permute-start.17 = (f32[8,13,13]{2,1,0:T(8,128)}, f32[8,13,13]{2,1,0:T(8,128)}, u32[]{:S(2)}, u32[]{:S(2)}) collective-permute-start(f32[8,13,13]{2,1,0:T(8,128)} %add.103), channel_id=1, source_target_pairs={{0,768},{64,832},{128,896},{192,960},{256,512},{320,576},{384,640}... | collective-permute-start | bytes 16232 | tf_op jit(solution)/shard_map/ppermute | solution.py:39
  230.4 12.9 %collective-permute-start.6 = (bf16[8,8,1024]{2,1,0:T(8,128)(2,1)S(1)}, bf16[8,8,1024]{2,1,0:T(8,128)(2,1)S(1)}, u32[]{:S(2)}, u32[]{:S(2)}) collective-permute-start(bf16[8,8,1024]{2,1,0:T(8,128)(2,1)S(1)} %get-tuple-element.92), channel_id=1, source_target_pairs={{0,64},{64,128},{128,192},{192,256},{256,320},{320,384},{384,448},... | collective-permute-start | bytes 393224 | tf_op jit(solution)/shard_map/ppermute | solution.py:14
  245.2 4.8 %fusion.7 = bf16[128,8,64]{0,2,1:T(8,128)(2,1)S(1)} fusion(bf16[768,8,64]{0,2,1:T(8,128)(2,1)S(1)} %copy-done.6, f32[8,128]{1,0:T(8,128)S(1)} %get-tuple-element.98, f32[8,128,768]{2,1,0:T(8,128)} %copy-done), kind=kOutput, calls=%fused_computation.20 | convolution fusion | flops 103089920 | bytes 4067328 | tf_op jit(solution)/shard_map/hqk,khd->qhd/dot_general | solution.py:96
  253.8 14.6 %collective-permute-done.7 = bf16[8,8,1024]{2,1,0:T(8,128)(2,1)S(1)} collective-permute-done((bf16[8,8,1024]{2,1,0:T(8,128)(2,1)S(1)}, bf16[8,8,1024]{2,1,0:T(8,128)(2,1)S(1)}, u32[]{:S(2)}, u32[]{:S(2)}) %collective-permute-start.7) | collective-permute-done | bytes 131104 | tf_op jit(solution)/shard_map/ppermute | solution.py:15
  (96 shorter events, 70.3 us)
Async XLA Ops:
  2.5 34.6 %collective-permute-start = (bf16[8,8,1024]{2,1,0:T(8,128)(2,1)S(1)}, bf16[8,8,1024]{2,1,0:T(8,128)(2,1)S(1)}, u32[]{:S(2)}, u32[]{:S(2)}) collective-permute-start(bf16[8,8,1024]{2,1,0:T(8,128)(2,1)S(1)} %get-tuple-element.96), channel_id=1, source_target_pairs={{0,64},{64,128},{128,192},{192,256},{256,320},{320,384},{384,448},... | collective-permute-start | bytes 393224 | tf_op jit(solution)/shard_map/ppermute | solution.py:14
  18.1 37.4 %collective-permute-start.1 = (bf16[8,8,1024]{2,1,0:T(8,128)(2,1)S(1)}, bf16[8,8,1024]{2,1,0:T(8,128)(2,1)S(1)}, u32[]{:S(2)}, u32[]{:S(2)}) collective-permute-start(bf16[8,8,1024]{2,1,0:T(8,128)(2,1)S(1)} %get-tuple-element.97), channel_id=1, source_target_pairs={{64,0},{128,64},{192,128},{256,192},{320,256},{384,320},{448,384},... | collective-permute-start | bytes 393224 | tf_op jit(solution)/shard_map/ppermute | solution.py:15
  55.6 12.5 %collective-permute-start.3 = (bf16[32,8,1024]{2,1,0:T(8,128)(2,1)S(1)}, bf16[32,8,1024]{2,1,0:T(8,128)(2,1)S(1)}, u32[]{:S(2)}, u32[]{:S(2)}) collective-permute-start(bf16[32,8,1024]{2,1,0:T(8,128)(2,1)S(1)} %pad_maximum_fusion.4), channel_id=1, source_target_pairs={{1,0},{2,1},{3,2},{4,3},{5,4},{6,5},{7,6},{8,7},{9,8},{10,9},{11,1... | collective-permute-start | bytes 1572872 | tf_op jit(solution)/shard_map/ppermute | solution.py:15
  57.6 19.2 %collective-permute-start.2 = (bf16[32,8,1024]{2,1,0:T(8,128)(2,1)S(1)}, bf16[32,8,1024]{2,1,0:T(8,128)(2,1)S(1)}, u32[]{:S(2)}, u32[]{:S(2)}) collective-permute-start(bf16[32,8,1024]{2,1,0:T(8,128)(2,1)S(1)} %pad_maximum_fusion.4), channel_id=1, source_target_pairs={{0,1},{1,2},{2,3},{3,4},{4,5},{5,6},{6,7},{7,8},{8,9},{9,10},{10,1... | collective-permute-start | bytes 1572872 | tf_op jit(solution)/shard_map/ppermute | solution.py:14
  85.0 2.7 copy-start
  95.8 3.1 %copy-start.2 = (f32[8,128,768]{2,1,0:T(8,128)S(1)}, f32[8,128,768]{2,1,0:T(8,128)}, u32[]{:S(2)}) copy-start(f32[8,128,768]{2,1,0:T(8,128)} %get-tuple-element.99) | copy-start | bytes 9437188
  104.0 5.4 %copy-start.4 = (f32[32,24,512]{2,1,0:T(8,128)S(1)}, f32[32,24,512]{2,1,0:T(8,128)}, u32[]{:S(2)}) copy-start(f32[32,24,512]{2,1,0:T(8,128)} %reshape.312) | copy-start | bytes 4718596
  109.6 15.0 %copy-start.1 = (f32[8,16,8,768]{3,2,1,0:T(8,128)S(1)}, f32[8,16,8,768]{3,2,1,0:T(8,128)}, u32[]{:S(2)}) copy-start(f32[8,16,8,768]{3,2,1,0:T(8,128)} %get-tuple-element.86) | copy-start | bytes 9437188
  109.9 120.1 %collective-permute-start.4 = (bf16[32,8,1024]{2,1,0:T(8,128)(2,1)S(1)}, bf16[32,8,1024]{2,1,0:T(8,128)(2,1)S(1)}, u32[]{:S(2)}, u32[]{:S(2)}) collective-permute-start(bf16[32,8,1024]{2,1,0:T(8,128)(2,1)S(1)} %get-tuple-element.88), channel_id=1, source_target_pairs={{0,1},{1,2},{2,3},{3,4},{4,5},{5,6},{6,7},{7,8},{8,9},{9,10},{10,1... | collective-permute-start | bytes 1572872 | tf_op jit(solution)/shard_map/ppermute | solution.py:14
  112.0 118.1 %collective-permute-start.5 = (bf16[32,8,1024]{2,1,0:T(8,128)(2,1)S(1)}, bf16[32,8,1024]{2,1,0:T(8,128)(2,1)S(1)}, u32[]{:S(2)}, u32[]{:S(2)}) collective-permute-start(bf16[32,8,1024]{2,1,0:T(8,128)(2,1)S(1)} %get-tuple-element.89), channel_id=1, source_target_pairs={{1,0},{2,1},{3,2},{4,3},{5,4},{6,5},{7,6},{8,7},{9,8},{10,9},{11,1... | collective-permute-start | bytes 1572872 | tf_op jit(solution)/shard_map/ppermute | solution.py:15
  139.8 78.7 %copy-start.3 = (bf16[768,8,64]{0,2,1:T(8,128)(2,1)S(1)}, bf16[768,8,64]{0,2,1:T(8,128)(2,1)}, u32[]{:S(2)}) copy-start(bf16[768,8,64]{0,2,1:T(8,128)(2,1)} %copy.38) | copy-start | bytes 2359300
  147.2 3.2 %collective-permute-start.8 = (f32[8,13,13]{2,1,0:T(8,128)S(1)}, f32[8,13,13]{2,1,0:T(8,128)S(1)}, u32[]{:S(2)}, u32[]{:S(2)}) collective-permute-start(f32[8,13,13]{2,1,0:T(8,128)S(1)} %convolution_bitcast_fusion.1), channel_id=1, source_target_pairs={{0,1},{1,0},{2,3},{3,2},{4,5},{5,4},{6,7},{7,6},{8,9},{9,8},{10,11... | collective-permute-start | bytes 16232 | tf_op jit(solution)/shard_map/ppermute | solution.py:39
  150.3 6.2 %collective-permute-start.9 = (f32[8,13,13]{2,1,0:T(8,128)S(1)}, f32[8,13,13]{2,1,0:T(8,128)S(1)}, u32[]{:S(2)}, u32[]{:S(2)}) collective-permute-start(f32[8,13,13]{2,1,0:T(8,128)S(1)} %add.95), channel_id=1, source_target_pairs={{0,2},{1,3},{2,0},{3,1},{4,6},{5,7},{6,4},{7,5},{8,10},{9,11},{10,... | collective-permute-start | bytes 16232 | tf_op jit(solution)/shard_map/ppermute | solution.py:39
  156.5 7.4 %collective-permute-start.10 = (f32[8,13,13]{2,1,0:T(8,128)S(1)}, f32[8,13,13]{2,1,0:T(8,128)S(1)}, u32[]{:S(2)}, u32[]{:S(2)}) collective-permute-start(f32[8,13,13]{2,1,0:T(8,128)S(1)} %add.96), channel_id=1, source_target_pairs={{0,4},{1,5},{2,6},{3,7},{4,0},{5,1},{6,2},{7,3},{8,12},{9,13},{10,... | collective-permute-start | bytes 16232 | tf_op jit(solution)/shard_map/ppermute | solution.py:39
  163.9 11.5 %collective-permute-start.11 = (f32[8,13,13]{2,1,0:T(8,128)S(1)}, f32[8,13,13]{2,1,0:T(8,128)S(1)}, u32[]{:S(2)}, u32[]{:S(2)}) collective-permute-start(f32[8,13,13]{2,1,0:T(8,128)S(1)} %add.97), channel_id=1, source_target_pairs={{0,8},{1,9},{2,10},{3,11},{4,12},{5,13},{6,14},{7,15},{8,0},{9,1},... | collective-permute-start | bytes 16232 | tf_op jit(solution)/shard_map/ppermute | solution.py:39
  175.4 6.2 %collective-permute-start.12 = (f32[8,13,13]{2,1,0:T(8,128)S(1)}, f32[8,13,13]{2,1,0:T(8,128)S(1)}, u32[]{:S(2)}, u32[]{:S(2)}) collective-permute-start(f32[8,13,13]{2,1,0:T(8,128)S(1)} %add.98), channel_id=1, source_target_pairs={{0,16},{1,17},{2,18},{3,19},{4,20},{5,21},{6,22},{7,23},{8,24},{9,... | collective-permute-start | bytes 16232 | tf_op jit(solution)/shard_map/ppermute | solution.py:39
  181.6 7.4 %collective-permute-start.13 = (f32[8,13,13]{2,1,0:T(8,128)S(1)}, f32[8,13,13]{2,1,0:T(8,128)S(1)}, u32[]{:S(2)}, u32[]{:S(2)}) collective-permute-start(f32[8,13,13]{2,1,0:T(8,128)S(1)} %add.99), channel_id=1, source_target_pairs={{0,48},{1,49},{2,50},{3,51},{4,52},{5,53},{6,54},{7,55},{8,56},{9,... | collective-permute-start | bytes 16232 | tf_op jit(solution)/shard_map/ppermute | solution.py:39
  189.0 6.2 %collective-permute-start.14 = (f32[8,13,13]{2,1,0:T(8,128)S(1)}, f32[8,13,13]{2,1,0:T(8,128)S(1)}, u32[]{:S(2)}, u32[]{:S(2)}) collective-permute-start(f32[8,13,13]{2,1,0:T(8,128)S(1)} %add.100), channel_id=1, source_target_pairs={{0,64},{64,0},{128,192},{192,128},{256,320},{320,256},{384,448},{4... | collective-permute-start | bytes 16232 | tf_op jit(solution)/shard_map/ppermute | solution.py:39
  195.2 7.4 %collective-permute-start.15 = (f32[8,13,13]{2,1,0:T(8,128)S(1)}, f32[8,13,13]{2,1,0:T(8,128)S(1)}, u32[]{:S(2)}, u32[]{:S(2)}) collective-permute-start(f32[8,13,13]{2,1,0:T(8,128)S(1)} %add.101), channel_id=1, source_target_pairs={{0,192},{64,128},{128,64},{192,0},{256,448},{320,384},{384,320},{4... | collective-permute-start | bytes 16232 | tf_op jit(solution)/shard_map/ppermute | solution.py:39
  202.6 21.1 %collective-permute-start.16 = (f32[8,13,13]{2,1,0:T(8,128)S(1)}, f32[8,13,13]{2,1,0:T(8,128)S(1)}, u32[]{:S(2)}, u32[]{:S(2)}) collective-permute-start(f32[8,13,13]{2,1,0:T(8,128)S(1)} %add.102), channel_id=1, source_target_pairs={{0,256},{64,320},{128,384},{192,448},{256,0},{320,64},{384,128},{4... | collective-permute-start | bytes 16232 | tf_op jit(solution)/shard_map/ppermute | solution.py:39
  219.2 26.0 %copy-start.6 = (bf16[768,8,64]{0,2,1:T(8,128)(2,1)S(1)}, bf16[768,8,64]{0,2,1:T(8,128)(2,1)}, u32[]{:S(2)}) copy-start(bf16[768,8,64]{0,2,1:T(8,128)(2,1)} %copy.43) | copy-start | bytes 2359300
  224.2 28.0 %collective-permute-start.17 = (f32[8,13,13]{2,1,0:T(8,128)}, f32[8,13,13]{2,1,0:T(8,128)}, u32[]{:S(2)}, u32[]{:S(2)}) collective-permute-start(f32[8,13,13]{2,1,0:T(8,128)} %add.103), channel_id=1, source_target_pairs={{0,768},{64,832},{128,896},{192,960},{256,512},{320,576},{384,640}... | collective-permute-start | bytes 16232 | tf_op jit(solution)/shard_map/ppermute | solution.py:39
  230.4 23.4 %collective-permute-start.6 = (bf16[8,8,1024]{2,1,0:T(8,128)(2,1)S(1)}, bf16[8,8,1024]{2,1,0:T(8,128)(2,1)S(1)}, u32[]{:S(2)}, u32[]{:S(2)}) collective-permute-start(bf16[8,8,1024]{2,1,0:T(8,128)(2,1)S(1)} %get-tuple-element.92), channel_id=1, source_target_pairs={{0,64},{64,128},{128,192},{192,256},{256,320},{320,384},{384,448},... | collective-permute-start | bytes 393224 | tf_op jit(solution)/shard_map/ppermute | solution.py:14
  243.3 25.1 %collective-permute-start.7 = (bf16[8,8,1024]{2,1,0:T(8,128)(2,1)S(1)}, bf16[8,8,1024]{2,1,0:T(8,128)(2,1)S(1)}, u32[]{:S(2)}, u32[]{:S(2)}) collective-permute-start(bf16[8,8,1024]{2,1,0:T(8,128)(2,1)S(1)} %get-tuple-element.93), channel_id=1, source_target_pairs={{64,0},{128,64},{192,128},{256,192},{320,256},{384,320},{448,384},... | collective-permute-start | bytes 393224 | tf_op jit(solution)/shard_map/ppermute | solution.py:15
  (1 other events, 2.3 us)

commit v7 on v6

--- a/solution.py
+++ b/solution.py
@@ -107,9 +107,9 @@
     )
     grad_queries = grad_query.astype(jnp.bfloat16).reshape(height, breadth, model_width)
     grad_cells = dscore.reshape(head_count, height, breadth, keys)
-    by_col = jnp.sum(grad_cells[:, :, :, None, :] * col_hot[None, None, :, :, :], axis=2)
+    by_row = jnp.sum(grad_cells[:, :, None, :, :] * row_hot[None, :, :, None, :], axis=1)
     grad_table = jnp.einsum(
-        "hibk,iak->hab", by_col, row_hot, precision=lax.Precision.HIGH
+        "hajk,jbk->hab", by_row, col_hot, precision=lax.Precision.HIGH
     )
     grad_keys = (
         jnp.einsum("hqk,qhd->khd", dscore_round, query_heads, preferred_element_type=jnp.float32)

time: 270 us -> 259 us (0.959)
  other arithmetic: 37.3 us -> 28.3 us
  matrix products: 23.3 us -> 18 us
    reduce_sum x1, other arithmetic: 15.2 us -> 6.76 us  [per_device(): jnp.sum(grad_cells[:, :, None, :, :] * row_hot[None, :, :, None, :], axis=1)]
    dot_general x1, matrix products: 7.39 us -> 2.84 us  [per_device(): jnp.einsum('hajk,jbk->hab', by_row, col_hot, precision=lax.Precision.HIGH)]
  transfers between devices with their start and end apart: 18 -> 18, of which waited for: 13 -> 13; matrix products, arithmetic and copies ran while one was open for 21% -> 17% of each run, Pallas kernels for 0% -> 0%
where the time goes in v7:
time: 259 us; the launch traced here: 258 us
  waiting for transfers between devices  89 us (34%)
  starting transfers between devices  88.7 us (34%)
  local copies, waits for them, and re-layouts  32.5 us (13%)
  other arithmetic  28.3 us (11%)
  matrix products  18 us (7%)
    ppermute x10, waiting for transfers between devices, exchange_sum(): return value + lax.ppermute(value, axis, pairs)  43.7 us
    ppermute x10, starting transfers between devices, exchange_sum(): return value + lax.ppermute(value, axis, pairs)  37.7 us
    ppermute x4, waiting for transfers between devices, padded_2(): after = lax.ppermute(leading, axis, down)  36.7 us
    ppermute x4, starting transfers between devices, padded_2(): before = lax.ppermute(last, axis, up)  32.7 us
    ppermute x4, starting transfers between devices, padded_2(): after = lax.ppermute(leading, axis, down)  18.3 us
    ppermute x4, waiting for transfers between devices, padded_2(): before = lax.ppermute(last, axis, up)  8.64 us
    reduce_sum x1, other arithmetic, per_device(): jnp.sum(grad_cells[:, :, None, :, :] * row_hot[None, :, :, None, :], axis=1)  6.76 us
    reduce_sum x1, other arithmetic, per_device(): jnp.sum(window_bias[:, None, :, :, None] * row_hot[None, :, :, None, :],...  6.49 us
  transfers between devices with their start and end apart: 18, of which 13 were waited for; matrix products, arithmetic and copies ran while one was open for 17% of the time, Pallas kernels for 0%

profile of v7, /device:TPU:6, one launch (start us, length us, event | category | flops | bytes accessed | tf_op | source)
XLA Modules:
  0.0 257.6 jit_solution(7059360151265716858)
XLA Ops:
  2.5 15.6 %collective-permute-start = (bf16[8,8,1024]{2,1,0:T(8,128)(2,1)S(1)}, bf16[8,8,1024]{2,1,0:T(8,128)(2,1)S(1)}, u32[]{:S(2)}, u32[]{:S(2)}) collective-permute-start(bf16[8,8,1024]{2,1,0:T(8,128)(2,1)S(1)} %get-tuple-element.96), channel_id=1, source_target_pairs={{0,64},{64,128},{128,192},{192,256},{256,320},{320,384},{384,448},... | collective-permute-start | bytes 393224 | tf_op jit(solution)/shard_map/ppermute | solution.py:14
  27.4 6.5 %multiply_reduce_fusion = f32[8,16,13,768]{3,1,2,0:T(8,128)S(1)} fusion(f32[16,13,768]{2,0,1:T(8,128)S(1)} %fusion.17, f32[8,13,13]{2,1,0:T(8,128)S(1)} %copy.40), kind=kLoop, calls=%fused_computation.1 | loop fusion | flops 31948800 | bytes 5756192 | tf_op jit(solution)/shard_map/reduce_sum | solution.py:74
  33.9 2.9 %copy.41 = f32[8,16,13,768]{3,2,1,0:T(8,128)S(1)} copy(f32[8,16,13,768]{3,1,2,0:T(8,128)S(1)} %multiply_reduce_fusion) | data formatting | bytes 10223616 | tf_op jit(solution)/shard_map/reduce_sum | solution.py:74
  37.0 18.6 %collective-permute-done.1 = bf16[8,8,1024]{2,1,0:T(8,128)(2,1)S(1)} collective-permute-done((bf16[8,8,1024]{2,1,0:T(8,128)(2,1)S(1)}, bf16[8,8,1024]{2,1,0:T(8,128)(2,1)S(1)}, u32[]{:S(2)}, u32[]{:S(2)}) %collective-permute-start.1) | collective-permute-done | bytes 131104 | tf_op jit(solution)/shard_map/ppermute | solution.py:15
  60.2 5.9 %multiply_reduce_fusion.2 = f32[8,16,8,768]{3,2,1,0:T(8,128)} fusion(f32[8,13,768]{2,0,1:T(8,128)S(1)} %copy.42, f32[8,16,13,768]{3,2,1,0:T(8,128)S(1)} %copy.41), kind=kLoop, calls=%fused_computation.3 | loop fusion | flops 19660800 | bytes 8577024 | tf_op jit(solution)/shard_map/reduce_sum | solution.py:75
  68.1 8.6 %collective-permute-done.2 = bf16[32,8,1024]{2,1,0:T(8,128)(2,1)S(1)} collective-permute-done((bf16[32,8,1024]{2,1,0:T(8,128)(2,1)S(1)}, bf16[32,8,1024]{2,1,0:T(8,128)(2,1)S(1)}, u32[]{:S(2)}, u32[]{:S(2)}) %collective-permute-start.2) | collective-permute-done | bytes 524320 | tf_op jit(solution)/shard_map/ppermute | solution.py:14
  87.5 3.2 %convolution_bitcast_fusion = f32[768,8,64]{0,2,1:T(8,128)} fusion(bf16[128,8,64]{0,2,1:T(8,128)(2,1)S(1)} %copy-done.6, f32[8,128]{1,0:T(8,128)S(1)} %get-tuple-element.98, f32[8,128,768]{2,1,0:T(8,128)S(1)} %fusion.3), kind=kOutput, calls=%fused_computation.16 | convolution fusion | flops 103024384 | bytes 4853760 | tf_op jit(solution)/shard_map/hqk,qhd->khd/dot_general | solution.py:118
  94.8 3.0 %fusion.1 = (f32[8,128]{1,0:T(8,128)S(1)}, f32[8,768,128]{1,2,0:T(8,128)S(1)}) fusion(f32[8,128,768]{2,1,0:T(8,128)} %get-tuple-element.99, f32[8,128]{1,0:T(8,128)S(1)} %get-tuple-element.98, bf16[768,8,64]{0,2,1:T(8,128)(2,1)} %copy.43, bf16[128,8,64]{0,2,1:T(8,128)(2,1)S(1)} %copy-done.6), kind=kOutput, calls=%fused_computation.6 | convolution fusion | flops 103021568 | bytes 7217152 | tf_op jit(solution)/shard_map/qhd,khd->hqk/dot_general | solution.py:100
  102.9 3.9 %reshape.311 = f32[32,24,512]{2,1,0:T(8,128)} reshape(f32[768,8,64]{2,1,0:T(8,128)} %copy.50) | data formatting | bytes 3145728 | tf_op jit(solution)/shard_map/reshape | solution.py:122
  112.0 12.6 %collective-permute-start.5 = (bf16[32,8,1024]{2,1,0:T(8,128)(2,1)S(1)}, bf16[32,8,1024]{2,1,0:T(8,128)(2,1)}, u32[]{:S(2)}, u32[]{:S(2)}) collective-permute-start(bf16[32,8,1024]{2,1,0:T(8,128)(2,1)S(1)} %get-tuple-element.89), channel_id=1, source_target_pairs={{1,0},{2,1},{3,2},{4,3},{5,4},{6,5},{7,6},{8,7},{9,8},{10,9},{11,1... | collective-permute-start | bytes 1572872 | tf_op jit(solution)/shard_map/ppermute | solution.py:15
  124.6 6.8 %multiply_reduce_fusion.1 = f32[8,13,8,768]{3,2,1,0:T(8,128)} fusion(f32[16,13,768]{2,1,0:T(8,128)S(1)} %copy-done.5, f32[8,16,8,768]{3,2,1,0:T(8,128)} %get-tuple-element.86), kind=kLoop, calls=%fused_computation.2 | loop fusion | flops 19808256 | bytes 6340608 | tf_op jit(solution)/shard_map/reduce_sum | solution.py:110
  139.3 4.2 %collective-permute-done.9 = f32[8,13,13]{2,1,0:T(8,128)S(1)} collective-permute-done((f32[8,13,13]{2,1,0:T(8,128)S(1)}, f32[8,13,13]{2,1,0:T(8,128)S(1)}, u32[]{:S(2)}, u32[]{:S(2)}) %collective-permute-start.9) | collective-permute-done | bytes 5440 | tf_op jit(solution)/shard_map/ppermute | solution.py:39
  145.5 5.5 %collective-permute-done.10 = f32[8,13,13]{2,1,0:T(8,128)S(1)} collective-permute-done((f32[8,13,13]{2,1,0:T(8,128)S(1)}, f32[8,13,13]{2,1,0:T(8,128)S(1)}, u32[]{:S(2)}, u32[]{:S(2)}) %collective-permute-start.10) | collective-permute-done | bytes 5440 | tf_op jit(solution)/shard_map/ppermute | solution.py:39
  152.9 9.6 %collective-permute-done.11 = f32[8,13,13]{2,1,0:T(8,128)S(1)} collective-permute-done((f32[8,13,13]{2,1,0:T(8,128)S(1)}, f32[8,13,13]{2,1,0:T(8,128)S(1)}, u32[]{:S(2)}, u32[]{:S(2)}) %collective-permute-start.11) | collective-permute-done | bytes 5440 | tf_op jit(solution)/shard_map/ppermute | solution.py:39
  164.4 4.2 %collective-permute-done.12 = f32[8,13,13]{2,1,0:T(8,128)S(1)} collective-permute-done((f32[8,13,13]{2,1,0:T(8,128)S(1)}, f32[8,13,13]{2,1,0:T(8,128)S(1)}, u32[]{:S(2)}, u32[]{:S(2)}) %collective-permute-start.12) | collective-permute-done | bytes 5440 | tf_op jit(solution)/shard_map/ppermute | solution.py:39
  171.2 4.9 %collective-permute-done.13 = f32[8,13,13]{2,1,0:T(8,128)S(1)} collective-permute-done((f32[8,13,13]{2,1,0:T(8,128)S(1)}, f32[8,13,13]{2,1,0:T(8,128)S(1)}, u32[]{:S(2)}, u32[]{:S(2)}) %collective-permute-start.13) | collective-permute-done | bytes 5440 | tf_op jit(solution)/shard_map/ppermute | solution.py:39
  178.0 4.2 %collective-permute-done.14 = f32[8,13,13]{2,1,0:T(8,128)S(1)} collective-permute-done((f32[8,13,13]{2,1,0:T(8,128)S(1)}, f32[8,13,13]{2,1,0:T(8,128)S(1)}, u32[]{:S(2)}, u32[]{:S(2)}) %collective-permute-start.14) | collective-permute-done | bytes 5440 | tf_op jit(solution)/shard_map/ppermute | solution.py:39
  184.2 5.4 %collective-permute-done.15 = f32[8,13,13]{2,1,0:T(8,128)S(1)} collective-permute-done((f32[8,13,13]{2,1,0:T(8,128)S(1)}, f32[8,13,13]{2,1,0:T(8,128)S(1)}, u32[]{:S(2)}, u32[]{:S(2)}) %collective-permute-start.15) | collective-permute-done | bytes 5440 | tf_op jit(solution)/shard_map/ppermute | solution.py:39
  189.6 15.9 %collective-permute-start.16 = (f32[8,13,13]{2,1,0:T(8,128)S(1)}, f32[8,13,13]{2,1,0:T(8,128)S(1)}, u32[]{:S(2)}, u32[]{:S(2)}) collective-permute-start(f32[8,13,13]{2,1,0:T(8,128)S(1)} %add.102), channel_id=1, source_target_pairs={{0,256},{64,320},{128,384},{192,448},{256,0},{320,64},{384,128},{4... | collective-permute-start | bytes 16232 | tf_op jit(solution)/shard_map/ppermute | solution.py:39
  206.3 4.4 %collective-permute-done.16 = f32[8,13,13]{2,1,0:T(8,128)S(1)} collective-permute-done((f32[8,13,13]{2,1,0:T(8,128)S(1)}, f32[8,13,13]{2,1,0:T(8,128)S(1)}, u32[]{:S(2)}, u32[]{:S(2)}) %collective-permute-start.16) | collective-permute-done | bytes 5440 | tf_op jit(solution)/shard_map/ppermute | solution.py:39
  210.7 5.8 %collective-permute-start.17 = (f32[8,13,13]{2,1,0:T(8,128)S(1)}, f32[8,13,13]{2,1,0:T(8,128)S(1)}, u32[]{:S(2)}, u32[]{:S(2)}) collective-permute-start(f32[8,13,13]{2,1,0:T(8,128)S(1)} %add.103), channel_id=1, source_target_pairs={{0,768},{64,832},{128,896},{192,960},{256,512},{320,576},{384,640}... | collective-permute-start | bytes 16232 | tf_op jit(solution)/shard_map/ppermute | solution.py:39
  218.4 12.6 %collective-permute-start.6 = (bf16[8,8,1024]{2,1,0:T(8,128)(2,1)S(1)}, bf16[8,8,1024]{2,1,0:T(8,128)(2,1)S(1)}, u32[]{:S(2)}, u32[]{:S(2)}) collective-permute-start(bf16[8,8,1024]{2,1,0:T(8,128)(2,1)S(1)} %get-tuple-element.92), channel_id=1, source_target_pairs={{0,64},{64,128},{128,192},{192,256},{256,320},{320,384},{384,448},... | collective-permute-start | bytes 393224 | tf_op jit(solution)/shard_map/ppermute | solution.py:14
  232.9 5.1 %fusion.9 = bf16[128,8,64]{0,2,1:T(8,128)(2,1)S(1)} fusion(bf16[768,8,64]{0,2,1:T(8,128)(2,1)} %copy.43, f32[8,128]{1,0:T(8,128)S(1)} %get-tuple-element.98, f32[8,128,768]{2,1,0:T(8,128)} %copy-done), kind=kOutput, calls=%fused_computation.22 | convolution fusion | flops 103089920 | bytes 4067328 | tf_op jit(solution)/shard_map/hqk,khd->qhd/dot_general | solution.py:96
  240.8 16.0 %collective-permute-done.7 = bf16[8,8,1024]{2,1,0:T(8,128)(2,1)S(1)} collective-permute-done((bf16[8,8,1024]{2,1,0:T(8,128)(2,1)S(1)}, bf16[8,8,1024]{2,1,0:T(8,128)(2,1)S(1)}, u32[]{:S(2)}, u32[]{:S(2)}) %collective-permute-start.7) | collective-permute-done | bytes 131104 | tf_op jit(solution)/shard_map/ppermute | solution.py:15
  (97 shorter events, 71.0 us)
Async XLA Ops:
  2.5 34.5 %collective-permute-start = (bf16[8,8,1024]{2,1,0:T(8,128)(2,1)S(1)}, bf16[8,8,1024]{2,1,0:T(8,128)(2,1)S(1)}, u32[]{:S(2)}, u32[]{:S(2)}) collective-permute-start(bf16[8,8,1024]{2,1,0:T(8,128)(2,1)S(1)} %get-tuple-element.96), channel_id=1, source_target_pairs={{0,64},{64,128},{128,192},{192,256},{256,320},{320,384},{384,448},... | collective-permute-start | bytes 393224 | tf_op jit(solution)/shard_map/ppermute | solution.py:14
  18.1 37.4 %collective-permute-start.1 = (bf16[8,8,1024]{2,1,0:T(8,128)(2,1)S(1)}, bf16[8,8,1024]{2,1,0:T(8,128)(2,1)S(1)}, u32[]{:S(2)}, u32[]{:S(2)}) collective-permute-start(bf16[8,8,1024]{2,1,0:T(8,128)(2,1)S(1)} %get-tuple-element.97), channel_id=1, source_target_pairs={{64,0},{128,64},{192,128},{256,192},{320,256},{384,320},{448,384},... | collective-permute-start | bytes 393224 | tf_op jit(solution)/shard_map/ppermute | solution.py:15
  55.6 12.5 %collective-permute-start.3 = (bf16[32,8,1024]{2,1,0:T(8,128)(2,1)S(1)}, bf16[32,8,1024]{2,1,0:T(8,128)(2,1)S(1)}, u32[]{:S(2)}, u32[]{:S(2)}) collective-permute-start(bf16[32,8,1024]{2,1,0:T(8,128)(2,1)S(1)} %pad_maximum_fusion.4), channel_id=1, source_target_pairs={{1,0},{2,1},{3,2},{4,3},{5,4},{6,5},{7,6},{8,7},{9,8},{10,9},{11,1... | collective-permute-start | bytes 1572872 | tf_op jit(solution)/shard_map/ppermute | solution.py:15
  57.6 19.2 %collective-permute-start.2 = (bf16[32,8,1024]{2,1,0:T(8,128)(2,1)S(1)}, bf16[32,8,1024]{2,1,0:T(8,128)(2,1)S(1)}, u32[]{:S(2)}, u32[]{:S(2)}) collective-permute-start(bf16[32,8,1024]{2,1,0:T(8,128)(2,1)S(1)} %pad_maximum_fusion.4), channel_id=1, source_target_pairs={{0,1},{1,2},{2,3},{3,4},{4,5},{5,6},{6,7},{7,8},{8,9},{9,10},{10,1... | collective-permute-start | bytes 1572872 | tf_op jit(solution)/shard_map/ppermute | solution.py:14
  84.9 2.6 %copy-start = (f32[8,128,768]{2,1,0:T(8,128)}, f32[8,128,768]{2,1,0:T(8,128)S(1)}, u32[]{:S(2)}) copy-start(f32[8,128,768]{2,1,0:T(8,128)S(1)} %fusion.3) | copy-start | bytes 9437188
  84.9 2.6 %copy-start.6 = (bf16[128,8,64]{0,2,1:T(8,128)(2,1)S(1)}, bf16[128,8,64]{0,2,1:T(8,128)(2,1)}, u32[]{:S(2)}) copy-start(bf16[128,8,64]{0,2,1:T(8,128)(2,1)} %copy.46) | copy-start | bytes 393220
  94.8 3.1 %copy-start.1 = (f32[8,128,768]{2,1,0:T(8,128)S(1)}, f32[8,128,768]{2,1,0:T(8,128)}, u32[]{:S(2)}) copy-start(f32[8,128,768]{2,1,0:T(8,128)} %get-tuple-element.99) | copy-start | bytes 9437188
  102.9 5.4 %copy-start.4 = (f32[32,24,512]{2,1,0:T(8,128)S(1)}, f32[32,24,512]{2,1,0:T(8,128)}, u32[]{:S(2)}) copy-start(f32[32,24,512]{2,1,0:T(8,128)} %reshape.312) | copy-start | bytes 4718596
  108.4 16.2 %copy-start.5 = (f32[16,13,768]{2,1,0:T(8,128)S(1)}, f32[16,13,768]{2,1,0:T(8,128)}, u32[]{:S(2)}) copy-start(f32[16,13,768]{2,1,0:T(8,128)} %copy.53) | copy-start | bytes 1916932
  110.1 106.4 %collective-permute-start.4 = (bf16[32,8,1024]{2,1,0:T(8,128)(2,1)S(1)}, bf16[32,8,1024]{2,1,0:T(8,128)(2,1)}, u32[]{:S(2)}, u32[]{:S(2)}) collective-permute-start(bf16[32,8,1024]{2,1,0:T(8,128)(2,1)S(1)} %get-tuple-element.88), channel_id=1, source_target_pairs={{0,1},{1,2},{2,3},{3,4},{4,5},{5,6},{6,7},{7,8},{8,9},{9,10},{10,1... | collective-permute-start | bytes 1572872 | tf_op jit(solution)/shard_map/ppermute | solution.py:14
  112.0 104.5 %collective-permute-start.5 = (bf16[32,8,1024]{2,1,0:T(8,128)(2,1)S(1)}, bf16[32,8,1024]{2,1,0:T(8,128)(2,1)}, u32[]{:S(2)}, u32[]{:S(2)}) collective-permute-start(bf16[32,8,1024]{2,1,0:T(8,128)(2,1)S(1)} %get-tuple-element.89), channel_id=1, source_target_pairs={{1,0},{2,1},{3,2},{4,3},{5,4},{6,5},{7,6},{8,7},{9,8},{10,9},{11,1... | collective-permute-start | bytes 1572872 | tf_op jit(solution)/shard_map/ppermute | solution.py:15
  131.4 74.2 %copy-start.3 = (bf16[768,8,64]{0,2,1:T(8,128)(2,1)S(1)}, bf16[768,8,64]{0,2,1:T(8,128)(2,1)}, u32[]{:S(2)}) copy-start(bf16[768,8,64]{0,2,1:T(8,128)(2,1)} %copy.38) | copy-start | bytes 2359300
  134.2 3.1 %collective-permute-start.8 = (f32[8,13,13]{2,1,0:T(8,128)S(1)}, f32[8,13,13]{2,1,0:T(8,128)S(1)}, u32[]{:S(2)}, u32[]{:S(2)}) collective-permute-start(f32[8,13,13]{2,1,0:T(8,128)S(1)} %fusion.11), channel_id=1, source_target_pairs={{0,1},{1,0},{2,3},{3,2},{4,5},{5,4},{6,7},{7,6},{8,9},{9,8},{10,11... | collective-permute-start | bytes 16232 | tf_op jit(solution)/shard_map/ppermute | solution.py:39
  137.4 6.2 %collective-permute-start.9 = (f32[8,13,13]{2,1,0:T(8,128)S(1)}, f32[8,13,13]{2,1,0:T(8,128)S(1)}, u32[]{:S(2)}, u32[]{:S(2)}) collective-permute-start(f32[8,13,13]{2,1,0:T(8,128)S(1)} %add.95), channel_id=1, source_target_pairs={{0,2},{1,3},{2,0},{3,1},{4,6},{5,7},{6,4},{7,5},{8,10},{9,11},{10,... | collective-permute-start | bytes 16232 | tf_op jit(solution)/shard_map/ppermute | solution.py:39
  143.6 7.4 %collective-permute-start.10 = (f32[8,13,13]{2,1,0:T(8,128)S(1)}, f32[8,13,13]{2,1,0:T(8,128)S(1)}, u32[]{:S(2)}, u32[]{:S(2)}) collective-permute-start(f32[8,13,13]{2,1,0:T(8,128)S(1)} %add.96), channel_id=1, source_target_pairs={{0,4},{1,5},{2,6},{3,7},{4,0},{5,1},{6,2},{7,3},{8,12},{9,13},{10,... | collective-permute-start | bytes 16232 | tf_op jit(solution)/shard_map/ppermute | solution.py:39
  151.0 11.5 %collective-permute-start.11 = (f32[8,13,13]{2,1,0:T(8,128)S(1)}, f32[8,13,13]{2,1,0:T(8,128)S(1)}, u32[]{:S(2)}, u32[]{:S(2)}) collective-permute-start(f32[8,13,13]{2,1,0:T(8,128)S(1)} %add.97), channel_id=1, source_target_pairs={{0,8},{1,9},{2,10},{3,11},{4,12},{5,13},{6,14},{7,15},{8,0},{9,1},... | collective-permute-start | bytes 16232 | tf_op jit(solution)/shard_map/ppermute | solution.py:39
  162.5 6.2 %collective-permute-start.12 = (f32[8,13,13]{2,1,0:T(8,128)S(1)}, f32[8,13,13]{2,1,0:T(8,128)S(1)}, u32[]{:S(2)}, u32[]{:S(2)}) collective-permute-start(f32[8,13,13]{2,1,0:T(8,128)S(1)} %add.98), channel_id=1, source_target_pairs={{0,16},{1,17},{2,18},{3,19},{4,20},{5,21},{6,22},{7,23},{8,24},{9,... | collective-permute-start | bytes 16232 | tf_op jit(solution)/shard_map/ppermute | solution.py:39
  168.7 7.4 %collective-permute-start.13 = (f32[8,13,13]{2,1,0:T(8,128)S(1)}, f32[8,13,13]{2,1,0:T(8,128)S(1)}, u32[]{:S(2)}, u32[]{:S(2)}) collective-permute-start(f32[8,13,13]{2,1,0:T(8,128)S(1)} %add.99), channel_id=1, source_target_pairs={{0,48},{1,49},{2,50},{3,51},{4,52},{5,53},{6,54},{7,55},{8,56},{9,... | collective-permute-start | bytes 16232 | tf_op jit(solution)/shard_map/ppermute | solution.py:39
  176.1 6.2 %collective-permute-start.14 = (f32[8,13,13]{2,1,0:T(8,128)S(1)}, f32[8,13,13]{2,1,0:T(8,128)S(1)}, u32[]{:S(2)}, u32[]{:S(2)}) collective-permute-start(f32[8,13,13]{2,1,0:T(8,128)S(1)} %add.100), channel_id=1, source_target_pairs={{0,64},{64,0},{128,192},{192,128},{256,320},{320,256},{384,448},{4... | collective-permute-start | bytes 16232 | tf_op jit(solution)/shard_map/ppermute | solution.py:39
  182.2 7.4 %collective-permute-start.15 = (f32[8,13,13]{2,1,0:T(8,128)S(1)}, f32[8,13,13]{2,1,0:T(8,128)S(1)}, u32[]{:S(2)}, u32[]{:S(2)}) collective-permute-start(f32[8,13,13]{2,1,0:T(8,128)S(1)} %add.101), channel_id=1, source_target_pairs={{0,192},{64,128},{128,64},{192,0},{256,448},{320,384},{384,320},{4... | collective-permute-start | bytes 16232 | tf_op jit(solution)/shard_map/ppermute | solution.py:39
  189.6 21.1 %collective-permute-start.16 = (f32[8,13,13]{2,1,0:T(8,128)S(1)}, f32[8,13,13]{2,1,0:T(8,128)S(1)}, u32[]{:S(2)}, u32[]{:S(2)}) collective-permute-start(f32[8,13,13]{2,1,0:T(8,128)S(1)} %add.102), channel_id=1, source_target_pairs={{0,256},{64,320},{128,384},{192,448},{256,0},{320,64},{384,128},{4... | collective-permute-start | bytes 16232 | tf_op jit(solution)/shard_map/ppermute | solution.py:39
  210.7 29.4 %collective-permute-start.17 = (f32[8,13,13]{2,1,0:T(8,128)S(1)}, f32[8,13,13]{2,1,0:T(8,128)S(1)}, u32[]{:S(2)}, u32[]{:S(2)}) collective-permute-start(f32[8,13,13]{2,1,0:T(8,128)S(1)} %add.103), channel_id=1, source_target_pairs={{0,768},{64,832},{128,896},{192,960},{256,512},{320,576},{384,640}... | collective-permute-start | bytes 16232 | tf_op jit(solution)/shard_map/ppermute | solution.py:39
  218.4 22.4 %collective-permute-start.6 = (bf16[8,8,1024]{2,1,0:T(8,128)(2,1)S(1)}, bf16[8,8,1024]{2,1,0:T(8,128)(2,1)S(1)}, u32[]{:S(2)}, u32[]{:S(2)}) collective-permute-start(bf16[8,8,1024]{2,1,0:T(8,128)(2,1)S(1)} %get-tuple-element.92), channel_id=1, source_target_pairs={{0,64},{64,128},{128,192},{192,256},{256,320},{320,384},{384,448},... | collective-permute-start | bytes 393224 | tf_op jit(solution)/shard_map/ppermute | solution.py:14
  231.0 25.8 %collective-permute-start.7 = (bf16[8,8,1024]{2,1,0:T(8,128)(2,1)S(1)}, bf16[8,8,1024]{2,1,0:T(8,128)(2,1)S(1)}, u32[]{:S(2)}, u32[]{:S(2)}) collective-permute-start(bf16[8,8,1024]{2,1,0:T(8,128)(2,1)S(1)} %get-tuple-element.93), channel_id=1, source_target_pairs={{64,0},{128,64},{192,128},{256,192},{320,256},{384,320},{448,384},... | collective-permute-start | bytes 393224 | tf_op jit(solution)/shard_map/ppermute | solution.py:15
  (1 other events, 1.7 us)

commit v8 on v7

--- a/solution.py
+++ b/solution.py
@@ -111,12 +111,25 @@
     grad_table = jnp.einsum(
         "hajk,jbk->hab", by_row, col_hot, precision=lax.Precision.HIGH
     )
+    own_head = jnp.arange(head_count, dtype=jnp.int32)[:, None, None] == (
+        jnp.arange(model_width, dtype=jnp.int32) // head_dim
+    )[None, None, :]
+    query_blocks = jnp.where(own_head, queries.reshape(1, cells, model_width), 0)
+    grad_blocks = jnp.where(own_head, out_cotangent.reshape(1, cells, model_width), 0)
     grad_keys = (
-        jnp.einsum("hqk,qhd->khd", dscore_round, query_heads, preferred_element_type=jnp.float32)
+        jnp.einsum(
+            "pk,pf->kf",
+            dscore_round.reshape(head_count * cells, keys),
+            query_blocks.reshape(head_count * cells, model_width),
+            preferred_element_type=jnp.float32,
+        )
         * score_scale
     )
     grad_vals = jnp.einsum(
-        "hqk,qhd->khd", rounded_probs, grad_heads, preferred_element_type=jnp.float32
+        "pk,pf->kf",
+        rounded_probs.reshape(head_count * cells, keys),
+        grad_blocks.reshape(head_count * cells, model_width),
+        preferred_element_type=jnp.float32,
     )
     accum = jnp.concatenate(
         (grad_keys.reshape(rows, cols, model_width), grad_vals.reshape(rows, cols, model_width)),

time: 259 us -> 256 us (0.988)
  waiting for transfers between devices: 89 us -> 79.3 us
  starting transfers between devices: 88.7 us -> 98.3 us
  matrix products: 18 us -> 15 us
    ppermute x4, starting transfers between devices: 18.3 us -> 29 us  [padded_2(): after = lax.ppermute(leading, axis, down)]
    ppermute x4, waiting for transfers between devices: 8.64 us -> 0.01 us  [padded_2(): before = lax.ppermute(last, axis, up)]
    reshape x2 -> x0, local copies, waits for them, and re-layouts: 5.55 us -> none  [the longest x1 3.86 us: per_device(): grad_keys.reshape(rows, cols, model_width)]
    dot_general x1, matrix products: 5.09 us -> 0.66 us  [per_device(): jnp.einsum('hqk,khd->qhd', rounded_probs, value_heads, preferred_element_...]
    sub x0 -> x1, matrix products: none -> 3.99 us  [per_device(): weights_raw = jnp.exp(scores - row_peak)]
    reshape x2, local copies, waits for them, and re-layouts: 2.54 us -> 5.96 us  [per_device(): key_heads = padded[..., :model_width].reshape(keys, head_count, head_dim)]
    reshape x2, local copies, waits for them, and re-layouts: 2.52 us -> 5.91 us  [per_device(): value_heads = padded[..., model_width:].reshape(keys, head_count, head_dim)]
    reduce_sum x1, local copies, waits for them, and re-layouts: 2.95 us -> 5.59 us  [per_device(): jnp.sum(window_bias[:, None, :, :, None] * row_hot[None, :, :, None, :],...]
  transfers between devices with their start and end apart: 18 -> 18, of which waited for: 13 -> 11; matrix products, arithmetic and copies ran while one was open for 17% -> 17% of each run, Pallas kernels for 0% -> 0%
where the time goes in v8:
time: 256 us; the launch traced here: 254 us
  starting transfers between devices  98.3 us (38%)
  waiting for transfers between devices  79.3 us (31%)
  local copies, waits for them, and re-layouts  32.2 us (13%)
  other arithmetic  28.5 us (11%)
  matrix products  15 us (6%)
    ppermute x10, waiting for transfers between devices, exchange_sum(): return value + lax.ppermute(value, axis, pairs)  43.8 us
    ppermute x10, starting transfers between devices, exchange_sum(): return value + lax.ppermute(value, axis, pairs)  37.1 us
    ppermute x4, waiting for transfers between devices, padded_2(): after = lax.ppermute(leading, axis, down)  35.5 us
    ppermute x4, starting transfers between devices, padded_2(): before = lax.ppermute(last, axis, up)  32.3 us
    ppermute x4, starting transfers between devices, padded_2(): after = lax.ppermute(leading, axis, down)  29 us
    reduce_sum x1, other arithmetic, per_device(): jnp.sum(half_bias[:, :, None, :, :] * col_hot[None, None, :, :, :], axis=3)  7.09 us
    reduce_sum x1, other arithmetic, per_device(): jnp.sum(grad_cells[:, :, None, :, :] * row_hot[None, :, :, None, :], axis=1)  7.05 us
    reduce_sum x1, other arithmetic, per_device(): jnp.sum(window_bias[:, None, :, :, None] * row_hot[None, :, :, None, :],...  6.46 us
  transfers between devices with their start and end apart: 18, of which 11 were waited for; matrix products, arithmetic and copies ran while one was open for 17% of the time, Pallas kernels for 0%

profile of v8, /device:TPU:6, one launch (start us, length us, event | category | flops | bytes accessed | tf_op | source)
XLA Modules:
  0.0 254.4 jit_solution(2506282359952060433)
XLA Ops:
  2.5 15.6 %collective-permute-start = (bf16[8,8,1024]{2,1,0:T(8,128)(2,1)S(1)}, bf16[8,8,1024]{2,1,0:T(8,128)(2,1)S(1)}, u32[]{:S(2)}, u32[]{:S(2)}) collective-permute-start(bf16[8,8,1024]{2,1,0:T(8,128)(2,1)S(1)} %get-tuple-element.97), channel_id=1, source_target_pairs={{0,64},{64,128},{128,192},{192,256},{256,320},{320,384},{384,448},... | collective-permute-start | bytes 393224 | tf_op jit(solution)/shard_map/ppermute | solution.py:14
  23.9 6.5 %multiply_reduce_fusion = f32[8,16,13,768]{3,1,2,0:T(8,128)S(1)} fusion(f32[16,13,768]{2,0,1:T(8,128)S(1)} %fusion.20, f32[8,13,13]{2,1,0:T(8,128)S(1)} %copy.36), kind=kLoop, calls=%fused_computation.1 | loop fusion | flops 31948800 | bytes 5756192 | tf_op jit(solution)/shard_map/reduce_sum | solution.py:74
  30.4 5.6 %copy.37 = f32[8,16,13,768]{3,2,1,0:T(8,128)} copy(f32[8,16,13,768]{3,1,2,0:T(8,128)S(1)} %multiply_reduce_fusion) | data formatting | bytes 10223616 | tf_op jit(solution)/shard_map/reduce_sum | solution.py:74
  40.5 15.2 %collective-permute-done.1 = bf16[8,8,1024]{2,1,0:T(8,128)(2,1)S(1)} collective-permute-done((bf16[8,8,1024]{2,1,0:T(8,128)(2,1)S(1)}, bf16[8,8,1024]{2,1,0:T(8,128)(2,1)S(1)}, u32[]{:S(2)}, u32[]{:S(2)}) %collective-permute-start.1) | collective-permute-done | bytes 131104 | tf_op jit(solution)/shard_map/ppermute | solution.py:15
  57.7 12.5 %collective-permute-start.3 = (bf16[32,8,1024]{2,1,0:T(8,128)(2,1)S(1)}, bf16[32,8,1024]{2,1,0:T(8,128)(2,1)S(1)}, u32[]{:S(2)}, u32[]{:S(2)}) collective-permute-start(bf16[32,8,1024]{2,1,0:T(8,128)(2,1)S(1)} %pad_maximum_fusion.5), channel_id=1, source_target_pairs={{1,0},{2,1},{3,2},{4,3},{5,4},{6,5},{7,6},{8,7},{9,8},{10,9},{11,1... | collective-permute-start | bytes 1572872 | tf_op jit(solution)/shard_map/ppermute | solution.py:15
  70.3 7.1 %multiply_reduce_fusion.2 = f32[8,16,8,768]{3,2,1,0:T(8,128)S(1)} fusion(f32[8,13,768]{2,0,1:T(8,128)} %copy.38, f32[8,16,13,768]{3,2,1,0:T(8,128)} %copy.37), kind=kLoop, calls=%fused_computation.3 | loop fusion | flops 19660800 | bytes 8577024 | tf_op jit(solution)/shard_map/reduce_sum | solution.py:75
  78.9 3.2 %reshape.361 = bf16[768,8,64]{2,1,0:T(8,128)(2,1)} reshape(bf16[32,24,512]{2,1,0:T(8,128)(2,1)} %get-tuple-element.91) | data formatting | bytes 1572864 | tf_op jit(solution)/shard_map/reshape | solution.py:82
  84.8 3.2 %reshape.360 = bf16[768,8,64]{2,1,0:T(8,128)(2,1)} reshape(bf16[32,24,512]{2,1,0:T(8,128)(2,1)} %get-tuple-element.92) | data formatting | bytes 1572864 | tf_op jit(solution)/shard_map/reshape | solution.py:83
  90.7 4.0 %fusion.52 = (f32[8,128]{1,0:T(8,128)S(1)}, f32[8,128,768]{2,1,0:T(8,128)}) fusion(f32[8,16,8,768]{3,2,1,0:T(8,128)S(1)} %multiply_reduce_fusion.2, bf16[768,8,64]{0,2,1:T(8,128)(2,1)} %copy.34, pred[128,768]{1,0:T(8,128)(4,1)S(1)} %copy-done.11, bf16[128,8,64]{2,1,0:T(8,128)(2,1)S(1)} %copy-done.7), kind=kOutput, calls=%fused_computation.95 | convolution fusion | flops 104596224 | bytes 7311360 | tf_op jit(solution)/shard_map/sub | solution.py:92
  94.7 3.0 %fusion.2 = (f32[8,128]{1,0:T(8,128)S(1)}, f32[8,768,128]{1,2,0:T(8,128)S(1)}) fusion(f32[8,128,768]{2,1,0:T(8,128)} %get-tuple-element.100, f32[8,128]{1,0:T(8,128)S(1)} %get-tuple-element.99, bf16[768,8,64]{0,2,1:T(8,128)(2,1)} %copy.39, bf16[128,8,64]{2,1,0:T(8,128)(2,1)} %reshape.365), kind=kOutput, calls=%fused_computation.10 | convolution fusion | flops 103021568 | bytes 7217152 | tf_op jit(solution)/shard_map/qhd,khd->hqk/dot_general | solution.py:100
  109.1 12.6 %collective-permute-start.5 = (bf16[32,8,1024]{2,1,0:T(8,128)(2,1)}, bf16[32,8,1024]{2,1,0:T(8,128)(2,1)}, u32[]{:S(2)}, u32[]{:S(2)}) collective-permute-start(bf16[32,8,1024]{2,1,0:T(8,128)(2,1)} %get-tuple-element.90), channel_id=1, source_target_pairs={{1,0},{2,1},{3,2},{4,3},{5,4},{6,5},{7,6},{8,7},{9,8},{10,9},{11,1... | collective-permute-start | bytes 1572872 | tf_op jit(solution)/shard_map/ppermute | solution.py:15
  121.7 7.0 %multiply_reduce_fusion.1 = f32[8,13,8,768]{3,2,1,0:T(8,128)} fusion(f32[16,13,768]{2,1,0:T(8,128)} %copy.47, f32[8,16,8,768]{3,2,1,0:T(8,128)} %get-tuple-element.86), kind=kLoop, calls=%fused_computation.2 | loop fusion | flops 19808256 | bytes 6340608 | tf_op jit(solution)/shard_map/reduce_sum | solution.py:110
  136.8 4.2 %collective-permute-done.9 = f32[8,13,13]{2,1,0:T(8,128)S(1)} collective-permute-done((f32[8,13,13]{2,1,0:T(8,128)S(1)}, f32[8,13,13]{2,1,0:T(8,128)S(1)}, u32[]{:S(2)}, u32[]{:S(2)}) %collective-permute-start.9) | collective-permute-done | bytes 5440 | tf_op jit(solution)/shard_map/ppermute | solution.py:39
  142.9 5.5 %collective-permute-done.10 = f32[8,13,13]{2,1,0:T(8,128)S(1)} collective-permute-done((f32[8,13,13]{2,1,0:T(8,128)S(1)}, f32[8,13,13]{2,1,0:T(8,128)S(1)}, u32[]{:S(2)}, u32[]{:S(2)}) %collective-permute-start.10) | collective-permute-done | bytes 5440 | tf_op jit(solution)/shard_map/ppermute | solution.py:39
  150.3 9.6 %collective-permute-done.11 = f32[8,13,13]{2,1,0:T(8,128)S(1)} collective-permute-done((f32[8,13,13]{2,1,0:T(8,128)S(1)}, f32[8,13,13]{2,1,0:T(8,128)S(1)}, u32[]{:S(2)}, u32[]{:S(2)}) %collective-permute-start.11) | collective-permute-done | bytes 5440 | tf_op jit(solution)/shard_map/ppermute | solution.py:39
  161.9 4.2 %collective-permute-done.12 = f32[8,13,13]{2,1,0:T(8,128)S(1)} collective-permute-done((f32[8,13,13]{2,1,0:T(8,128)S(1)}, f32[8,13,13]{2,1,0:T(8,128)S(1)}, u32[]{:S(2)}, u32[]{:S(2)}) %collective-permute-start.12) | collective-permute-done | bytes 5440 | tf_op jit(solution)/shard_map/ppermute | solution.py:39
  168.5 5.0 %collective-permute-done.13 = f32[8,13,13]{2,1,0:T(8,128)S(1)} collective-permute-done((f32[8,13,13]{2,1,0:T(8,128)S(1)}, f32[8,13,13]{2,1,0:T(8,128)S(1)}, u32[]{:S(2)}, u32[]{:S(2)}) %collective-permute-start.13) | collective-permute-done | bytes 5440 | tf_op jit(solution)/shard_map/ppermute | solution.py:39
  175.4 4.2 %collective-permute-done.14 = f32[8,13,13]{2,1,0:T(8,128)S(1)} collective-permute-done((f32[8,13,13]{2,1,0:T(8,128)S(1)}, f32[8,13,13]{2,1,0:T(8,128)S(1)}, u32[]{:S(2)}, u32[]{:S(2)}) %collective-permute-start.14) | collective-permute-done | bytes 5440 | tf_op jit(solution)/shard_map/ppermute | solution.py:39
  181.6 5.4 %collective-permute-done.15 = f32[8,13,13]{2,1,0:T(8,128)S(1)} collective-permute-done((f32[8,13,13]{2,1,0:T(8,128)S(1)}, f32[8,13,13]{2,1,0:T(8,128)S(1)}, u32[]{:S(2)}, u32[]{:S(2)}) %collective-permute-start.15) | collective-permute-done | bytes 5440 | tf_op jit(solution)/shard_map/ppermute | solution.py:39
  187.0 15.8 %collective-permute-start.16 = (f32[8,13,13]{2,1,0:T(8,128)S(1)}, f32[8,13,13]{2,1,0:T(8,128)S(1)}, u32[]{:S(2)}, u32[]{:S(2)}) collective-permute-start(f32[8,13,13]{2,1,0:T(8,128)S(1)} %add.107), channel_id=1, source_target_pairs={{0,256},{64,320},{128,384},{192,448},{256,0},{320,64},{384,128},{4... | collective-permute-start | bytes 16232 | tf_op jit(solution)/shard_map/ppermute | solution.py:39
  203.6 4.4 %collective-permute-done.16 = f32[8,13,13]{2,1,0:T(8,128)S(1)} collective-permute-done((f32[8,13,13]{2,1,0:T(8,128)S(1)}, f32[8,13,13]{2,1,0:T(8,128)S(1)}, u32[]{:S(2)}, u32[]{:S(2)}) %collective-permute-start.16) | collective-permute-done | bytes 5440 | tf_op jit(solution)/shard_map/ppermute | solution.py:39
  208.0 5.4 %collective-permute-start.17 = (f32[8,13,13]{2,1,0:T(8,128)S(1)}, f32[8,13,13]{2,1,0:T(8,128)S(1)}, u32[]{:S(2)}, u32[]{:S(2)}) collective-permute-start(f32[8,13,13]{2,1,0:T(8,128)S(1)} %add.108), channel_id=1, source_target_pairs={{0,768},{64,832},{128,896},{192,960},{256,512},{320,576},{384,640}... | collective-permute-start | bytes 16232 | tf_op jit(solution)/shard_map/ppermute | solution.py:39
  215.0 12.8 %collective-permute-start.6 = (bf16[8,8,1024]{2,1,0:T(8,128)(2,1)S(1)}, bf16[8,8,1024]{2,1,0:T(8,128)(2,1)S(1)}, u32[]{:S(2)}, u32[]{:S(2)}) collective-permute-start(bf16[8,8,1024]{2,1,0:T(8,128)(2,1)S(1)} %get-tuple-element.93), channel_id=1, source_target_pairs={{0,64},{64,128},{128,192},{192,256},{256,320},{320,384},{384,448},... | collective-permute-start | bytes 393224 | tf_op jit(solution)/shard_map/ppermute | solution.py:14
  233.3 20.3 %collective-permute-done.7 = bf16[8,8,1024]{2,1,0:T(8,128)(2,1)S(1)} collective-permute-done((bf16[8,8,1024]{2,1,0:T(8,128)(2,1)S(1)}, bf16[8,8,1024]{2,1,0:T(8,128)(2,1)S(1)}, u32[]{:S(2)}, u32[]{:S(2)}) %collective-permute-start.7) | collective-permute-done | bytes 131104 | tf_op jit(solution)/shard_map/ppermute | solution.py:15
  (110 shorter events, 60.8 us)
Async XLA Ops:
  2.5 38.0 %collective-permute-start = (bf16[8,8,1024]{2,1,0:T(8,128)(2,1)S(1)}, bf16[8,8,1024]{2,1,0:T(8,128)(2,1)S(1)}, u32[]{:S(2)}, u32[]{:S(2)}) collective-permute-start(bf16[8,8,1024]{2,1,0:T(8,128)(2,1)S(1)} %get-tuple-element.97), channel_id=1, source_target_pairs={{0,64},{64,128},{128,192},{192,256},{256,320},{320,384},{384,448},... | collective-permute-start | bytes 393224 | tf_op jit(solution)/shard_map/ppermute | solution.py:14
  18.1 37.6 %collective-permute-start.1 = (bf16[8,8,1024]{2,1,0:T(8,128)(2,1)S(1)}, bf16[8,8,1024]{2,1,0:T(8,128)(2,1)S(1)}, u32[]{:S(2)}, u32[]{:S(2)}) collective-permute-start(bf16[8,8,1024]{2,1,0:T(8,128)(2,1)S(1)} %get-tuple-element.98), channel_id=1, source_target_pairs={{64,0},{128,64},{192,128},{256,192},{320,256},{384,320},{448,384},... | collective-permute-start | bytes 393224 | tf_op jit(solution)/shard_map/ppermute | solution.py:15
  21.7 14.3 %copy-start.12 = (s32[8,768]{1,0:T(8,128)}, s32[8,768]{1,0:T(8,128)S(1)}, u32[]{:S(2)}) copy-start(s32[8,768]{1,0:T(8,128)S(1)} %broadcast_subtract_fusion.1) | copy-start | bytes 73732
  55.8 21.6 %collective-permute-start.2 = (bf16[32,8,1024]{2,1,0:T(8,128)(2,1)S(1)}, bf16[32,8,1024]{2,1,0:T(8,128)(2,1)S(1)}, u32[]{:S(2)}, u32[]{:S(2)}) collective-permute-start(bf16[32,8,1024]{2,1,0:T(8,128)(2,1)S(1)} %pad_maximum_fusion.5), channel_id=1, source_target_pairs={{0,1},{1,2},{2,3},{3,4},{4,5},{5,6},{6,7},{7,8},{8,9},{9,10},{10,1... | collective-permute-start | bytes 1572872 | tf_op jit(solution)/shard_map/ppermute | solution.py:14
  57.7 19.7 %collective-permute-start.3 = (bf16[32,8,1024]{2,1,0:T(8,128)(2,1)S(1)}, bf16[32,8,1024]{2,1,0:T(8,128)(2,1)S(1)}, u32[]{:S(2)}, u32[]{:S(2)}) collective-permute-start(bf16[32,8,1024]{2,1,0:T(8,128)(2,1)S(1)} %pad_maximum_fusion.5), channel_id=1, source_target_pairs={{1,0},{2,1},{3,2},{4,3},{5,4},{6,5},{7,6},{8,7},{9,8},{10,9},{11,1... | collective-permute-start | bytes 1572872 | tf_op jit(solution)/shard_map/ppermute | solution.py:15
  82.1 8.7 %copy-start.11 = (pred[128,768]{1,0:T(8,128)(4,1)S(1)}, pred[128,768]{1,0:T(8,128)(4,1)}, u32[]{:S(2)}) copy-start(pred[128,768]{1,0:T(8,128)(4,1)} %and_bitcast_fusion) | copy-start | bytes 294916
  107.2 106.3 %collective-permute-start.4 = (bf16[32,8,1024]{2,1,0:T(8,128)(2,1)}, bf16[32,8,1024]{2,1,0:T(8,128)(2,1)}, u32[]{:S(2)}, u32[]{:S(2)}) collective-permute-start(bf16[32,8,1024]{2,1,0:T(8,128)(2,1)} %get-tuple-element.89), channel_id=1, source_target_pairs={{0,1},{1,2},{2,3},{3,4},{4,5},{5,6},{6,7},{7,8},{8,9},{9,10},{10,1... | collective-permute-start | bytes 1572872 | tf_op jit(solution)/shard_map/ppermute | solution.py:14
  109.1 104.4 %collective-permute-start.5 = (bf16[32,8,1024]{2,1,0:T(8,128)(2,1)}, bf16[32,8,1024]{2,1,0:T(8,128)(2,1)}, u32[]{:S(2)}, u32[]{:S(2)}) collective-permute-start(bf16[32,8,1024]{2,1,0:T(8,128)(2,1)} %get-tuple-element.90), channel_id=1, source_target_pairs={{1,0},{2,1},{3,2},{4,3},{5,4},{6,5},{7,6},{8,7},{9,8},{10,9},{11,1... | collective-permute-start | bytes 1572872 | tf_op jit(solution)/shard_map/ppermute | solution.py:15
  128.7 74.2 %copy-start.1 = (bf16[768,8,64]{0,2,1:T(8,128)(2,1)S(1)}, bf16[768,8,64]{0,2,1:T(8,128)(2,1)}, u32[]{:S(2)}) copy-start(bf16[768,8,64]{0,2,1:T(8,128)(2,1)} %copy.34) | copy-start | bytes 2359300
  128.7 84.7 %copy-start.3 = (f32[32,24,512]{2,1,0:T(8,128)S(1)}, f32[32,24,512]{2,1,0:T(8,128)}, u32[]{:S(2)}) copy-start(f32[32,24,512]{2,1,0:T(8,128)} %copy-done.2) | copy-start | bytes 4718596
  128.7 84.8 %copy-start.5 = (f32[768,512]{1,0:T(8,128)S(1)}, f32[768,512]{1,0:T(8,128)}, u32[]{:S(2)}) copy-start(f32[768,512]{1,0:T(8,128)} %copy-done.4) | copy-start | bytes 4718596
  131.7 3.1 %collective-permute-start.8 = (f32[8,13,13]{2,1,0:T(8,128)S(1)}, f32[8,13,13]{2,1,0:T(8,128)S(1)}, u32[]{:S(2)}, u32[]{:S(2)}) collective-permute-start(f32[8,13,13]{2,1,0:T(8,128)S(1)} %fusion.12), channel_id=1, source_target_pairs={{0,1},{1,0},{2,3},{3,2},{4,5},{5,4},{6,7},{7,6},{8,9},{9,8},{10,11... | collective-permute-start | bytes 16232 | tf_op jit(solution)/shard_map/ppermute | solution.py:39
  134.8 6.2 %collective-permute-start.9 = (f32[8,13,13]{2,1,0:T(8,128)S(1)}, f32[8,13,13]{2,1,0:T(8,128)S(1)}, u32[]{:S(2)}, u32[]{:S(2)}) collective-permute-start(f32[8,13,13]{2,1,0:T(8,128)S(1)} %add.100), channel_id=1, source_target_pairs={{0,2},{1,3},{2,0},{3,1},{4,6},{5,7},{6,4},{7,5},{8,10},{9,11},{10,... | collective-permute-start | bytes 16232 | tf_op jit(solution)/shard_map/ppermute | solution.py:39
  141.0 7.4 %collective-permute-start.10 = (f32[8,13,13]{2,1,0:T(8,128)S(1)}, f32[8,13,13]{2,1,0:T(8,128)S(1)}, u32[]{:S(2)}, u32[]{:S(2)}) collective-permute-start(f32[8,13,13]{2,1,0:T(8,128)S(1)} %add.101), channel_id=1, source_target_pairs={{0,4},{1,5},{2,6},{3,7},{4,0},{5,1},{6,2},{7,3},{8,12},{9,13},{10,... | collective-permute-start | bytes 16232 | tf_op jit(solution)/shard_map/ppermute | solution.py:39
  148.4 11.5 %collective-permute-start.11 = (f32[8,13,13]{2,1,0:T(8,128)S(1)}, f32[8,13,13]{2,1,0:T(8,128)S(1)}, u32[]{:S(2)}, u32[]{:S(2)}) collective-permute-start(f32[8,13,13]{2,1,0:T(8,128)S(1)} %add.102), channel_id=1, source_target_pairs={{0,8},{1,9},{2,10},{3,11},{4,12},{5,13},{6,14},{7,15},{8,0},{9,1},... | collective-permute-start | bytes 16232 | tf_op jit(solution)/shard_map/ppermute | solution.py:39
  159.9 6.2 %collective-permute-start.12 = (f32[8,13,13]{2,1,0:T(8,128)S(1)}, f32[8,13,13]{2,1,0:T(8,128)S(1)}, u32[]{:S(2)}, u32[]{:S(2)}) collective-permute-start(f32[8,13,13]{2,1,0:T(8,128)S(1)} %add.103), channel_id=1, source_target_pairs={{0,16},{1,17},{2,18},{3,19},{4,20},{5,21},{6,22},{7,23},{8,24},{9,... | collective-permute-start | bytes 16232 | tf_op jit(solution)/shard_map/ppermute | solution.py:39
  166.1 7.4 %collective-permute-start.13 = (f32[8,13,13]{2,1,0:T(8,128)S(1)}, f32[8,13,13]{2,1,0:T(8,128)S(1)}, u32[]{:S(2)}, u32[]{:S(2)}) collective-permute-start(f32[8,13,13]{2,1,0:T(8,128)S(1)} %add.104), channel_id=1, source_target_pairs={{0,48},{1,49},{2,50},{3,51},{4,52},{5,53},{6,54},{7,55},{8,56},{9,... | collective-permute-start | bytes 16232 | tf_op jit(solution)/shard_map/ppermute | solution.py:39
  173.5 6.2 %collective-permute-start.14 = (f32[8,13,13]{2,1,0:T(8,128)S(1)}, f32[8,13,13]{2,1,0:T(8,128)S(1)}, u32[]{:S(2)}, u32[]{:S(2)}) collective-permute-start(f32[8,13,13]{2,1,0:T(8,128)S(1)} %add.105), channel_id=1, source_target_pairs={{0,64},{64,0},{128,192},{192,128},{256,320},{320,256},{384,448},{4... | collective-permute-start | bytes 16232 | tf_op jit(solution)/shard_map/ppermute | solution.py:39
  179.7 7.4 %collective-permute-start.15 = (f32[8,13,13]{2,1,0:T(8,128)S(1)}, f32[8,13,13]{2,1,0:T(8,128)S(1)}, u32[]{:S(2)}, u32[]{:S(2)}) collective-permute-start(f32[8,13,13]{2,1,0:T(8,128)S(1)} %add.106), channel_id=1, source_target_pairs={{0,192},{64,128},{128,64},{192,0},{256,448},{320,384},{384,320},{4... | collective-permute-start | bytes 16232 | tf_op jit(solution)/shard_map/ppermute | solution.py:39
  187.0 21.0 %collective-permute-start.16 = (f32[8,13,13]{2,1,0:T(8,128)S(1)}, f32[8,13,13]{2,1,0:T(8,128)S(1)}, u32[]{:S(2)}, u32[]{:S(2)}) collective-permute-start(f32[8,13,13]{2,1,0:T(8,128)S(1)} %add.107), channel_id=1, source_target_pairs={{0,256},{64,320},{128,384},{192,448},{256,0},{320,64},{384,128},{4... | collective-permute-start | bytes 16232 | tf_op jit(solution)/shard_map/ppermute | solution.py:39
  208.0 21.7 %copy-start.6 = (bf16[768,8,64]{0,2,1:T(8,128)(2,1)S(1)}, bf16[768,8,64]{0,2,1:T(8,128)(2,1)}, u32[]{:S(2)}) copy-start(bf16[768,8,64]{0,2,1:T(8,128)(2,1)} %copy.39) | copy-start | bytes 2359300
  208.0 24.5 %collective-permute-start.17 = (f32[8,13,13]{2,1,0:T(8,128)S(1)}, f32[8,13,13]{2,1,0:T(8,128)S(1)}, u32[]{:S(2)}, u32[]{:S(2)}) collective-permute-start(f32[8,13,13]{2,1,0:T(8,128)S(1)} %add.108), channel_id=1, source_target_pairs={{0,768},{64,832},{128,896},{192,960},{256,512},{320,576},{384,640}... | collective-permute-start | bytes 16232 | tf_op jit(solution)/shard_map/ppermute | solution.py:39
  215.0 18.3 %collective-permute-start.6 = (bf16[8,8,1024]{2,1,0:T(8,128)(2,1)S(1)}, bf16[8,8,1024]{2,1,0:T(8,128)(2,1)S(1)}, u32[]{:S(2)}, u32[]{:S(2)}) collective-permute-start(bf16[8,8,1024]{2,1,0:T(8,128)(2,1)S(1)} %get-tuple-element.93), channel_id=1, source_target_pairs={{0,64},{64,128},{128,192},{192,256},{256,320},{320,384},{384,448},... | collective-permute-start | bytes 393224 | tf_op jit(solution)/shard_map/ppermute | solution.py:14
  227.8 25.7 %collective-permute-start.7 = (bf16[8,8,1024]{2,1,0:T(8,128)(2,1)S(1)}, bf16[8,8,1024]{2,1,0:T(8,128)(2,1)S(1)}, u32[]{:S(2)}, u32[]{:S(2)}) collective-permute-start(bf16[8,8,1024]{2,1,0:T(8,128)(2,1)S(1)} %get-tuple-element.94), channel_id=1, source_target_pairs={{64,0},{128,64},{192,128},{256,192},{320,256},{384,320},{448,384},... | collective-permute-start | bytes 393224 | tf_op jit(solution)/shard_map/ppermute | solution.py:15
  (10 other events, 47.6 us)
